TPU v7x, 256 devices: a whole 4x4x8 slice. The times are simulated.
256 devices in a mesh: seq: 16 (over z, y_lo), chan: 16 (over y_hi, x, core).
Axes of the slice: x: 4, y: 4 (y_hi: 2, y_lo: 2; y = y_hi * 2 + y_lo), z: 8, core: 2. Of those that a mesh axis runs over, the one named last changes fastest.
Arguments:
- tokens: bfloat16 [4096, 4096], P('seq', 'chan'), may hold values from -6 to 6
- in_weight: bfloat16 [4096, 3, 4096], P(None, None, 'chan'), may hold values from -0.09375 to 0.09375
- short_weight: float32 [3, 3, 4096], P(None, None, 'chan'), may hold values from -3 to 3
- filter_taps: bfloat16 [4096, 4096], P(None, 'chan'), may hold values from -0.09375 to 0.09375
- cotangent: bfloat16 [4096, 4096], P('seq', 'chan'), may hold values from -1.5 to 1.5
Outputs:
- operator_out: bfloat16 [4096, 4096], P('seq', 'chan')
- stream_grads: bfloat16 [4096, 3, 4096], P('seq', None, 'chan')
- tap_grads: float32 [4096, 4096], P('seq', 'chan')
All inputs are finite; a program needn't handle non-finite values.
Results may differ from a plain program's by a relative error of at most 0.015.
Values may be sent and summed in bfloat16 or wider, within the bound.
No kernel may reach another device: no remote copies, remote signals or barrier semaphores. Data moves between devices by JAX's collectives and lax.ppermute only.
A program may use at most 128 MiB of HBM per device.

v0:
```python
import math

import jax
import jax.numpy as jnp
from jax import lax
from jax.sharding import PartitionSpec as P


def passed_along(block, axis, distance):
    devices = range(lax.axis_size(axis))
    route = [(i - distance, i) for i in devices if i - distance in devices]
    return lax.ppermute(block, axis, route)


def dft_tables(row_count):
    length = 2 * row_count
    sample = jnp.arange(length, dtype=jnp.int32)
    frequency = jnp.arange(row_count, dtype=jnp.int32)
    angles = (frequency[:, None] * sample[None, :] % length).astype(jnp.float32) * (
        2.0 * math.pi / length
    )
    parity = 1.0 - 2.0 * (sample % 2).astype(jnp.float32)
    lower_rows = jnp.where(frequency[:, None] == 0, parity[None, :], -jnp.sin(angles))
    forward = jnp.concatenate([jnp.cos(angles), lower_rows], axis=0)
    out_index = row_count + frequency
    back_angles = (out_index[:, None] * frequency[None, :] % length).astype(jnp.float32) * (
        2.0 * math.pi / length
    )
    factor = jnp.where(frequency == 0, 1.0, 2.0) / length
    out_parity = 1.0 - 2.0 * (out_index % 2).astype(jnp.float32)
    real_part = jnp.cos(back_angles) * factor[None, :]
    imag_part = jnp.where(
        frequency[None, :] == 0, out_parity[:, None] / length, -2.0 * jnp.sin(back_angles) / length
    )
    inverse = jnp.concatenate([real_part, imag_part], axis=1)
    return (forward, inverse)


def spectral_product(left_spec, right_spec):
    half_len = left_spec.shape[0] // 2
    left_spec = left_spec.astype(jnp.float32)
    right_spec = right_spec.astype(jnp.float32)
    left_re, left_im = (left_spec[:half_len], left_spec[half_len:])
    right_re, right_im = (right_spec[:half_len], right_spec[half_len:])
    first_row = (jnp.arange(half_len) == 0).reshape((half_len,) + (1,) * (left_spec.ndim - 1))
    cross_term = left_im * right_im
    real_out = left_re * right_re - jnp.where(first_row, 0.0, cross_term)
    imag_out = jnp.where(first_row, cross_term, left_re * right_im + left_im * right_re)
    return jnp.concatenate([real_out, imag_out], axis=0)


def spectral_adjoint(left_spec, grad_spec):
    half_len = left_spec.shape[0] // 2
    left_spec = left_spec.astype(jnp.float32)
    grad_spec = grad_spec.astype(jnp.float32)
    left_re, left_im = (left_spec[:half_len], left_spec[half_len:])
    grad_re, grad_im = (grad_spec[:half_len], grad_spec[half_len:])
    first_row = (jnp.arange(half_len) == 0).reshape((half_len,) + (1,) * (left_spec.ndim - 1))
    cross_term = left_im * grad_im
    real_out = left_re * grad_re + jnp.where(first_row, 0.0, cross_term)
    imag_out = jnp.where(first_row, cross_term, left_re * grad_im - left_im * grad_re)
    return jnp.concatenate([real_out, imag_out], axis=0)


def neighbour_rows(edge_rows, offset):
    return passed_along(edge_rows, "seq", offset)


def on_device(tokens, in_weight, short_weight, filter_taps, cotangent):
    row_count, local_width = tokens.shape
    spec_rows = 2 * row_count
    seq_count = lax.axis_size("seq")
    own_block = lax.axis_index("seq")
    forward, inverse = dft_tables(row_count)
    full_table = forward.astype(jnp.bfloat16)
    half_table = full_table[:, :row_count]
    back_table = inverse.astype(jnp.bfloat16)
    weight_cols = in_weight.reshape(in_weight.shape[0], 3 * local_width)
    streams = jnp.dot(
        lax.all_gather(tokens, "chan", axis=1, tiled=True),
        weight_cols,
        preferred_element_type=jnp.float32,
    )
    streams = streams.astype(jnp.bfloat16)
    before = neighbour_rows(streams[row_count - 2 :], 1)
    extended = (
        jnp.concatenate([before, streams], axis=0)
        .astype(jnp.float32)
        .reshape(row_count + 2, 3, local_width)
    )
    conv_out = (
        short_weight[:, 0] * extended[2:]
        + short_weight[:, 1] * extended[1:-1]
        + short_weight[:, 2] * extended[:-2]
    )
    query_conv, key_conv, value_conv = (conv_out[:, 0], conv_out[:, 1], conv_out[:, 2])
    gated = (key_conv * value_conv).astype(jnp.bfloat16)
    own_spec = jnp.dot(half_table, gated, preferred_element_type=jnp.float32).astype(jnp.bfloat16)
    tap_blocks = filter_taps.reshape(seq_count, row_count, local_width)
    earlier = jnp.concatenate(
        [jnp.zeros((1, row_count, local_width), jnp.bfloat16), tap_blocks[:-1]], axis=0
    )
    segments = jnp.concatenate([earlier, tap_blocks], axis=1)
    filters = jnp.einsum(
        "fn,bnc->bfc", full_table, segments, preferred_element_type=jnp.float32
    ).astype(jnp.bfloat16)
    pieces = lax.all_gather(own_spec, "seq", axis=0, tiled=True)

    def forward_add_block(position, carried):
        lag_index = own_block - position
        incoming = lax.dynamic_slice_in_dim(pieces, position * spec_rows, spec_rows, 0)
        filter_spec = lax.dynamic_index_in_dim(
            filters, jnp.clip(lag_index, 0, seq_count - 1), 0, keepdims=False
        )
        return carried + jnp.where(lag_index >= 0, spectral_product(filter_spec, incoming), 0.0)

    mixed_spec = lax.fori_loop(
        0,
        pieces.shape[0] // spec_rows,
        forward_add_block,
        jnp.zeros((spec_rows, local_width), jnp.float32),
    )
    long_out = jnp.dot(
        back_table, mixed_spec.astype(jnp.bfloat16), preferred_element_type=jnp.float32
    ).astype(jnp.bfloat16)
    operator_out = (query_conv * long_out.astype(jnp.float32)).astype(jnp.bfloat16)
    cot_wide = cotangent.astype(jnp.float32)
    grad_long = (cot_wide * query_conv).astype(jnp.bfloat16)
    grad_query = cot_wide * long_out.astype(jnp.float32)
    grad_spec = jnp.dot(back_table.T, grad_long, preferred_element_type=jnp.float32).astype(
        jnp.bfloat16
    )
    start_state = (
        jnp.zeros((spec_rows, local_width), jnp.float32),
        jnp.zeros((seq_count, spec_rows, local_width), jnp.float32),
    )
    backward_pieces = lax.all_gather(grad_spec, "seq", axis=0, tiled=True)

    def backward_add_block(position, state):
        spectral_grad, filter_grad = state
        lag_index = position - own_block
        usable = lag_index >= 0
        clipped = jnp.clip(lag_index, 0, seq_count - 1)
        incoming = lax.dynamic_slice_in_dim(backward_pieces, position * spec_rows, spec_rows, 0)
        filter_spec = lax.dynamic_index_in_dim(filters, clipped, 0, keepdims=False)
        spectral_grad = spectral_grad + jnp.where(
            usable, spectral_adjoint(filter_spec, incoming), 0.0
        )
        current = lax.dynamic_index_in_dim(filter_grad, clipped, 0, keepdims=False)
        current = current + jnp.where(usable, spectral_adjoint(own_spec, incoming), 0.0)
        filter_grad = lax.dynamic_update_index_in_dim(filter_grad, current, clipped, 0)
        return (spectral_grad, filter_grad)

    spectral_grad, filter_grad = lax.fori_loop(
        0, backward_pieces.shape[0] // spec_rows, backward_add_block, start_state
    )
    grad_gated = jnp.dot(
        half_table.T, spectral_grad.astype(jnp.bfloat16), preferred_element_type=jnp.float32
    ).astype(jnp.bfloat16)
    tap_spec = jnp.einsum("fn,bfc->bnc", forward, filter_grad, precision=lax.Precision.HIGHEST)
    tap_terms = tap_spec[:, row_count:] + jnp.concatenate(
        [tap_spec[1:, :row_count], jnp.zeros((1, row_count, local_width), jnp.float32)], axis=0
    )
    tap_grads = lax.psum_scatter(
        tap_terms.reshape(seq_count * row_count, local_width).astype(jnp.bfloat16),
        "seq",
        scatter_dimension=0,
        tiled=True,
    ).astype(jnp.float32)
    gated_wide = grad_gated.astype(jnp.float32)
    grad_streams = jnp.stack(
        [grad_query, gated_wide * value_conv, gated_wide * key_conv], axis=1
    ).astype(jnp.bfloat16)
    grad_streams = grad_streams.reshape(row_count, 3 * local_width)
    after = neighbour_rows(grad_streams[:2], -1)
    padded = (
        jnp.concatenate([grad_streams, after], axis=0)
        .astype(jnp.float32)
        .reshape(row_count + 2, 3, local_width)
    )
    stream_grads = (
        short_weight[:, 0] * padded[:row_count]
        + short_weight[:, 1] * padded[1 : row_count + 1]
        + short_weight[:, 2] * padded[2:]
    ).astype(jnp.bfloat16)
    return (operator_out, stream_grads, tap_grads)


def solution(mesh):
    return jax.shard_map(
        on_device,
        mesh=mesh,
        in_specs=(
            P("seq", "chan"),
            P(None, None, "chan"),
            P(None, None, "chan"),
            P(None, "chan"),
            P("seq", "chan"),
        ),
        out_specs=(P("seq", "chan"), P("seq", None, "chan"), P("seq", "chan")),
        check_vma=False,
    )
```

profile of v0, /device:TPU:2, one launch (start us, length us, event | category | flops | bytes accessed | tf_op | source)
XLA Modules:
  0.0 376.9 jit_solution(4375459504469983553)
XLA Ops:
  8.0 8.7 %copy.31 = bf16[4096,3,256]{0,2,1:T(8,128)(2,1)} copy(bf16[4096,3,256]{2,0,1:T(8,128)(2,1)} %param.10) | data formatting | bytes 12582912 | tf_op args[1]
  18.9 48.9 %all-gather.4.cloned.1.call-done = bf16[256,4096]{1,0:T(8,128)(2,1)} async-done(((bf16[256,256]{1,0:T(8,128)(2,1)}), bf16[256,4096]{1,0:T(8,128)(2,1)}) %all-gather.4.cloned.1.call-update) | async-done | bytes 2097168 | tf_op jit(solution)/shard_map/all_gather | solution.py:80
  67.7 5.3 %convolution_convert_fusion = bf16[256,768]{1,0:T(8,128)(2,1)S(1)} fusion(bf16[256,4096]{1,0:T(8,128)(2,1)} %all-gather.4.cloned.1.call-done, bf16[4096,768]{0,1:T(8,128)(2,1)} %bitcast.104), kind=kOutput, calls=%fused_computation.38 | convolution fusion | flops 1610809344 | bytes 8781824 | tf_op jit(solution)/shard_map/dot_general | solution.py:79
  73.0 2.5 collective-permute-start
  84.5 2.3 copy.38
  86.7 3.9 %copy.39 = bf16[16,256,256]{1,2,0:T(8,128)(2,1)} copy(bf16[16,256,256]{2,1,0:T(8,128)(2,1)} %bitcast.102) | data formatting | bytes 4194304 | tf_op jit(solution)/shard_map/reshape | solution.py:99
  90.6 2.1 negate_select_fusion.2
  92.9 6.7 %convert_bitcast_fusion = bf16[16,512,256]{1,2,0:T(8,128)(2,1)} fusion(bf16[15,256,256]{1,2,0:T(8,128)(2,1)} %copy.38, bf16[16,256,256]{1,2,0:T(8,128)(2,1)} %copy.39, bf16[512,512]{1,0:T(8,128)(2,1)S(1)} %fusion.20), kind=kOutput, calls=%fused_computation.35 | convolution fusion | flops 2162163712 | bytes 8781824 | tf_op jit(solution)/shard_map/fn,bnc->bfc/dot_general | solution.py:104
  99.6 6.4 %copy.40 = bf16[16,512,256]{2,1,0:T(8,128)(2,1)} copy(bf16[16,512,256]{1,2,0:T(8,128)(2,1)} %convert_bitcast_fusion) | data formatting | bytes 8388608
  105.9 2.0 convolution_convert_fusion.2
  108.2 77.8 %all-gather.8.cloned.1.call-done = bf16[8192,256]{1,0:T(8,128)(2,1)} async-done(((bf16[512,256]{1,0:T(8,128)(2,1)}), bf16[8192,256]{1,0:T(8,128)(2,1)}) %all-gather.8.cloned.1.call-update) | async-done | bytes 4194320 | tf_op jit(solution)/shard_map/all_gather | solution.py:137
  185.9 4.2 %broadcast_in_dim.154 = f32[16,512,256]{2,1,0:T(8,128)} broadcast(f32[]{:T(128)} %constant.182.clone.1), dimensions={} | broadcast | bytes 8388612 | tf_op jit(solution)/shard_map/broadcast_in_dim | solution.py:135
  190.1 69.8 %while.31 = (s32[]{:T(128)}, f32[512,256]{1,0:T(8,128)S(1)}, f32[16,512,256]{2,1,0:T(8,128)}, s32[]{:T(128)}, bf16[16,512,256]{2,1,0:T(8,128)(2,1)}, /*index=5*/...) while((s32[]{:T(128)}, f32[512,256]{1,0:T(8,128)S(1)}, ...), condition=%wide.region_3.4_spmd.clone, body=%wide.region_2.3_spmd.clone.sunk | while | flops 2359563 | bytes 8127216 | solution.py:154
  196.9 1.9 fusion.74
  201.2 1.9 fusion.74
  205.6 1.9 fusion.74
  209.9 1.9 fusion.74
  214.3 1.9 fusion.74
  218.6 1.9 fusion.74
  227.3 1.9 fusion.74
  231.7 1.9 fusion.74
  236.1 1.9 fusion.74
  240.4 1.9 fusion.74
  244.8 1.9 fusion.74
  253.5 1.9 fusion.74
  257.9 2.0 fusion.74
  259.8 16.5 %convolution_bitcast_fusion = f32[16,512,256]{1,2,0:T(8,128)S(1)} fusion(f32[16,512,256]{2,1,0:T(8,128)} %get-tuple-element.224, f32[256,512]{1,0:T(8,128)S(1)} %get-tuple-element.350, f32[256,512]{1,0:T(8,128)S(1)} %get-tuple-element.351), kind=kOutput, calls=%fused_computation.36 | convolution fusion | flops 12885164032 | bytes 17825792 | tf_op jit(solution)/shard_map/fn,bfc->bnc/dot_general | solution.py:160
  277.9 2.4 copy.48
  280.3 7.1 %all-gather.6.cloned.1.call-done = bf16[8192,256]{1,0:T(8,128)(2,1)} async-done(((bf16[512,256]{1,0:T(8,128)(2,1)}), bf16[8192,256]{1,0:T(8,128)(2,1)}) %all-gather.6.cloned.1.call-update) | async-done | bytes 4194320 | tf_op jit(solution)/shard_map/all_gather | solution.py:107
  287.4 37.5 %while.30 = (s32[]{:T(128)}, f32[512,256]{1,0:T(8,128)S(1)}, s32[]{:T(128)}, bf16[16,512,256]{2,1,0:T(8,128)(2,1)}, bf16[8192,256]{1,0:T(8,128)(2,1)}, /*index=5...) while((s32[]{:T(128)}, f32[512,256]{1,0:T(8,128)S(1)}, s32[]{:T(128)}, ...), condition=%wide.region_1.2_spmd.clone, body=%wide.region_0.1_spmd.clone.sunk | while | flops 1310987 | bytes 4719323 | solution.py:117
  327.8 10.0 %collective-permute-done.1 = bf16[2,768]{0,1:T(8,128)(2,1)S(1)} collective-permute-done((bf16[2,768]{0,1:T(8,128)(2,1)S(1)}, bf16[2,768]{0,1:T(8,128)(2,1)S(1)}, u32[]{:S(2)}, u32[]{:S(2)}) %collective-permute-start.1) | collective-permute-done | bytes 3104 | tf_op jit(solution)/shard_map/ppermute | solution.py:12
  340.1 28.7 %reduce-scatter.2.cloned.1.call-done = bf16[256,256]{1,0:T(8,128)(2,1)} async-done(((bf16[4096,256]{1,0:T(8,128)(2,1)}), bf16[256,256]{1,0:T(8,128)(2,1)}) %reduce-scatter.2.cloned.1.call-update) | async-done | bytes 131088 | tf_op jit(solution)/shard_map/reduce_scatter | solution.py:164
  (249 shorter events, 101.2 us)
Async XLA Ops:
  7.2 60.6 %all-gather.4.cloned.1.call-start = ((), (), s32[]{:S(2)}) async-start(), calls=%async_computation.1 | async-start | bytes 2228224 | tf_op jit(solution)/shard_map/all_gather | solution.py:80
  7.9 8.8 %copy-start.8 = (f32[3,3,256]{2,1,0:T(4,128)S(1)}, f32[3,3,256]{2,1,0:T(4,128)}, u32[]{:S(2)}) copy-start(f32[3,3,256]{2,1,0:T(4,128)} %param.11) | copy-start | bytes 27652
  7.9 178.0 %all-gather.8.cloned.1.call-start = ((), (), s32[]{:S(2)}) async-start(), calls=%async_computation.3 | async-start | bytes 4456448 | tf_op jit(solution)/shard_map/all_gather | solution.py:137
  18.9 64.5 %copy-start.5 = (bf16[256,256]{1,0:T(8,128)(2,1)}, bf16[256,256]{1,0:T(8,128)(2,1)S(1)}, u32[]{:S(2)}) copy-start(bf16[256,256]{1,0:T(8,128)(2,1)S(1)} %select_convert_fusion) | copy-start | bytes 393220
  73.0 3.8 %collective-permute-start = (bf16[2,768]{1,0:T(2,128)(2,1)S(1)}, bf16[2,768]{1,0:T(2,128)(2,1)S(1)}, u32[]{:S(2)}, u32[]{:S(2)}) collective-permute-start(bf16[2,768]{1,0:T(2,128)(2,1)S(1)} %slice.215), channel_id=1, source_target_pairs={{0,16},{16,32},{32,48},{48,64},{64,80},{80,96},{96,112},{112,128},... | collective-permute-start | bytes 9224 | tf_op jit(solution)/shard_map/ppermute | solution.py:12
  78.8 4.6 %copy-start.7 = (bf16[256,256]{1,0:T(8,128)(2,1)S(1)}, bf16[256,256]{1,0:T(8,128)(2,1)}, u32[]{:S(2)}) copy-start(bf16[256,256]{1,0:T(8,128)(2,1)} %param.13) | copy-start | bytes 393220
  81.4 3.0 slice-start
  83.4 1.1 copy-start.1
  84.4 203.0 %all-gather.6.cloned.1.call-start = ((), (), s32[]{:S(2)}) async-start(), calls=%async_computation.2 | async-start | bytes 4456448 | tf_op jit(solution)/shard_map/all_gather | solution.py:107
  92.9 13.1 %copy-start.3 = (bf16[512,512]{1,0:T(8,128)(2,1)}, bf16[512,512]{1,0:T(8,128)(2,1)S(1)}, u32[]{:S(2)}) copy-start(bf16[512,512]{1,0:T(8,128)(2,1)S(1)} %fusion.20) | copy-start | bytes 1572868
  107.9 82.2 %copy-start = (bf16[512,256]{1,0:T(8,128)(2,1)S(1)}, bf16[512,256]{1,0:T(8,128)(2,1)}, u32[]{:S(2)}) copy-start(bf16[512,256]{1,0:T(8,128)(2,1)} %convolution_convert_fusion.2) | copy-start | bytes 786436
  107.9 260.8 %reduce-scatter.2.cloned.1.call-start = ((), (), s32[]{:S(2)}) async-start(), calls=%async_computation.4 | async-start | bytes 2228224 | tf_op jit(solution)/shard_map/reduce_scatter | solution.py:164
  287.4 37.5 %copy-start.2 = (f32[256,3,256]{2,0,1:T(8,128)S(1)}, f32[256,3,256]{2,0,1:T(8,128)}, u32[]{:S(2)}) copy-start(f32[256,3,256]{2,0,1:T(8,128)} %copy-done.1) | copy-start | bytes 2359300
  287.4 37.5 %copy-start.4 = (bf16[512,512]{1,0:T(8,128)(2,1)S(1)}, bf16[512,512]{1,0:T(8,128)(2,1)}, u32[]{:S(2)}) copy-start(bf16[512,512]{1,0:T(8,128)(2,1)} %copy-done.3) | copy-start | bytes 1572868
  287.4 37.8 %copy-start.6 = (bf16[256,256]{1,0:T(8,128)(2,1)S(1)}, bf16[256,256]{1,0:T(8,128)(2,1)}, u32[]{:S(2)}) copy-start(bf16[256,256]{1,0:T(8,128)(2,1)} %copy-done.5) | copy-start | bytes 393220
  326.3 11.4 %collective-permute-start.1 = (bf16[2,768]{0,1:T(8,128)(2,1)S(1)}, bf16[2,768]{0,1:T(8,128)(2,1)S(1)}, u32[]{:S(2)}, u32[]{:S(2)}) collective-permute-start(bf16[2,768]{0,1:T(8,128)(2,1)S(1)} %copy.43), channel_id=1, source_target_pairs={{16,0},{32,16},{48,32},{64,48},{80,64},{96,80},{112,96},{128,112},... | collective-permute-start | bytes 9224 | tf_op jit(solution)/shard_map/ppermute | solution.py:12
Sparse Core Ops, SparseCore 0:
  10.5 57.1 all-gather.3
  84.5 101.3 all-gather.7
  188.3 99.0 all-gather.5
  289.8 78.9 reduce-scatter.1
where the time goes:
time: 380 us; the launch traced here: 377 us
  waiting for transfers between devices  174 us (46%)
  other arithmetic  116 us (31%)
  local copies, waits for them, and re-layouts  34.5 us (9%)
  matrix products  32.6 us (9%)
  between operations  14.1 us (4%)
  starting transfers between devices  4.12 us (1%)
    all_gather x1, waiting for transfers between devices, on_device(): backward_pieces = lax.all_gather(grad_spec, 'seq', axis=0, tiled=True)  77.8 us
    all_gather x1, waiting for transfers between devices, on_device(): lax.all_gather(tokens, 'chan', axis=1, tiled=True)  48.9 us
    dynamic_update_slice x16, other arithmetic, backward_add_block(): lax.dynamic_update_index_in_dim(filter_grad, current, clipped, 0)  30.8 us
    reduce_scatter x1, waiting for transfers between devices, on_device(): lax.psum_scatter(tap_terms.reshape(seq_count * row_count, local_width).as...  28.7 us
    dot_general x1, matrix products, on_device(): jnp.einsum('fn,bfc->bnc', forward, filter_grad, precision=lax.Precision.H...  16.5 us
    convert_element_type x32, other arithmetic, spectral_adjoint(): left_spec = left_spec.astype(jnp.float32)  16.5 us
    convert_element_type x16, other arithmetic, spectral_product(): right_spec = right_spec.astype(jnp.float32)  16 us
    convert_element_type x16, other arithmetic, spectral_product(): left_spec = left_spec.astype(jnp.float32)  15.9 us
  transfers between devices with their start and end apart: 6, of which 6 were waited for; matrix products, arithmetic and copies ran while one was open for 45% of the time, Pallas kernels for 0%

commit v1 on v0

v1 whole, which is shorter than its diff:
```python
import math

import jax
import jax.numpy as jnp
from jax import lax
from jax.sharding import PartitionSpec as P


def passed_along(block, axis, distance):
    devices = range(lax.axis_size(axis))
    route = [(i - distance, i) for i in devices if i - distance in devices]
    return lax.ppermute(block, axis, route)


def dft_tables(row_count):
    length = 2 * row_count
    sample = jnp.arange(length, dtype=jnp.int32)
    frequency = jnp.arange(row_count, dtype=jnp.int32)
    angles = (frequency[:, None] * sample[None, :] % length).astype(jnp.float32) * (
        2.0 * math.pi / length
    )
    parity = 1.0 - 2.0 * (sample % 2).astype(jnp.float32)
    lower_rows = jnp.where(frequency[:, None] == 0, parity[None, :], -jnp.sin(angles))
    forward = jnp.concatenate([jnp.cos(angles), lower_rows], axis=0)
    out_index = row_count + frequency
    back_angles = (out_index[:, None] * frequency[None, :] % length).astype(jnp.float32) * (
        2.0 * math.pi / length
    )
    factor = jnp.where(frequency == 0, 1.0, 2.0) / length
    out_parity = 1.0 - 2.0 * (out_index % 2).astype(jnp.float32)
    real_part = jnp.cos(back_angles) * factor[None, :]
    imag_part = jnp.where(
        frequency[None, :] == 0, out_parity[:, None] / length, -2.0 * jnp.sin(back_angles) / length
    )
    inverse = jnp.concatenate([real_part, imag_part], axis=1)
    return (forward, inverse)


def spectral_product(left_spec, right_spec):
    half_len = left_spec.shape[-1] // 2
    left_spec = left_spec.astype(jnp.float32)
    right_spec = right_spec.astype(jnp.float32)
    left_re, left_im = (left_spec[..., :half_len], left_spec[..., half_len:])
    right_re, right_im = (right_spec[..., :half_len], right_spec[..., half_len:])
    first_row = lax.broadcasted_iota(jnp.int32, (1,) * (left_spec.ndim - 1) + (half_len,), left_spec.ndim - 1) == 0
    cross_term = left_im * right_im
    real_out = left_re * right_re - jnp.where(first_row, 0.0, cross_term)
    imag_out = jnp.where(first_row, cross_term, left_re * right_im + left_im * right_re)
    return jnp.concatenate([real_out, imag_out], axis=-1)


def spectral_adjoint(left_spec, grad_spec):
    half_len = left_spec.shape[-1] // 2
    left_spec = left_spec.astype(jnp.float32)
    grad_spec = grad_spec.astype(jnp.float32)
    left_re, left_im = (left_spec[..., :half_len], left_spec[..., half_len:])
    grad_re, grad_im = (grad_spec[..., :half_len], grad_spec[..., half_len:])
    first_row = lax.broadcasted_iota(jnp.int32, (1,) * (left_spec.ndim - 1) + (half_len,), left_spec.ndim - 1) == 0
    cross_term = left_im * grad_im
    real_out = left_re * grad_re + jnp.where(first_row, 0.0, cross_term)
    imag_out = jnp.where(first_row, cross_term, left_re * grad_im - left_im * grad_re)
    return jnp.concatenate([real_out, imag_out], axis=-1)


def neighbour_rows(edge_rows, offset):
    return passed_along(edge_rows, "seq", offset)


def swap_layout(values):
    return lax.all_to_all(values, "seq", 1, 1, tiled=True)


def on_device(tokens, in_weight, short_weight, filter_taps, cotangent):
    row_count, local_width = tokens.shape
    seq_count = lax.axis_size("seq")
    group = local_width // seq_count
    own_block = lax.axis_index("seq")
    forward, inverse = dft_tables(row_count)
    full_table = forward.astype(jnp.bfloat16)
    half_table = full_table[:, :row_count]
    back_table = inverse.astype(jnp.bfloat16)
    weight_cols = in_weight.reshape(in_weight.shape[0], 3 * local_width)
    streams = jnp.dot(
        lax.all_gather(tokens, "chan", axis=1, tiled=True),
        weight_cols,
        preferred_element_type=jnp.float32,
    )
    streams = streams.astype(jnp.bfloat16)
    before = neighbour_rows(streams[row_count - 2 :], 1)
    extended = (
        jnp.concatenate([before, streams], axis=0)
        .astype(jnp.float32)
        .reshape(row_count + 2, 3, local_width)
    )
    conv_out = (
        short_weight[:, 0] * extended[2:]
        + short_weight[:, 1] * extended[1:-1]
        + short_weight[:, 2] * extended[:-2]
    )
    query_conv, key_conv, value_conv = (conv_out[:, 0], conv_out[:, 1], conv_out[:, 2])
    gated = (key_conv * value_conv).astype(jnp.bfloat16)

    gated_cols = swap_layout(gated.reshape(row_count, seq_count, group))
    own_spec = jnp.einsum(
        "tbc,kt->bck", gated_cols, half_table, preferred_element_type=jnp.float32
    ).astype(jnp.bfloat16)
    own_taps = lax.dynamic_slice_in_dim(filter_taps, own_block * group, group, axis=1)
    tap_blocks = own_taps.reshape(seq_count, row_count, group)
    earlier = jnp.concatenate(
        [jnp.zeros((1, row_count, group), jnp.bfloat16), tap_blocks[:-1]], axis=0
    )
    segments = jnp.concatenate([earlier, tap_blocks], axis=1)
    filters = jnp.einsum(
        "fn,bnc->bcf", full_table, segments, preferred_element_type=jnp.float32
    ).astype(jnp.bfloat16)

    mixed_spec = jnp.zeros(own_spec.shape, jnp.float32)
    for lag_step in range(seq_count):
        term = spectral_product(filters[lag_step][None], own_spec[: seq_count - lag_step])
        mixed_spec = mixed_spec + jnp.pad(term, ((lag_step, 0), (0, 0), (0, 0)))
    long_cols = jnp.einsum(
        "bck,ak->abc", mixed_spec.astype(jnp.bfloat16), back_table,
        preferred_element_type=jnp.float32,
    ).astype(jnp.bfloat16)
    long_out = swap_layout(long_cols).reshape(row_count, local_width)

    operator_out = (query_conv * long_out.astype(jnp.float32)).astype(jnp.bfloat16)
    cot_wide = cotangent.astype(jnp.float32)
    grad_long = (cot_wide * query_conv).astype(jnp.bfloat16)
    grad_query = cot_wide * long_out.astype(jnp.float32)

    grad_long_cols = swap_layout(grad_long.reshape(row_count, seq_count, group))
    grad_spec = jnp.einsum(
        "abc,ak->bck", grad_long_cols, back_table, preferred_element_type=jnp.float32
    ).astype(jnp.bfloat16)
    spectral_grad = jnp.zeros(grad_spec.shape, jnp.float32)
    filter_parts = []
    for lag_step in range(seq_count):
        ahead = grad_spec[lag_step:]
        term = spectral_adjoint(filters[lag_step][None], ahead)
        spectral_grad = spectral_grad + jnp.pad(term, ((0, lag_step), (0, 0), (0, 0)))
        filter_parts.append(
            jnp.sum(spectral_adjoint(own_spec[: seq_count - lag_step], ahead), axis=0)
        )
    filter_grad = jnp.stack(filter_parts, axis=0)
    gated_grad_cols = jnp.einsum(
        "bck,kt->tbc", spectral_grad.astype(jnp.bfloat16), half_table,
        preferred_element_type=jnp.float32,
    ).astype(jnp.bfloat16)
    grad_gated = swap_layout(gated_grad_cols).reshape(row_count, local_width)

    tap_spec = jnp.einsum("dck,kn->dcn", filter_grad, forward, precision=lax.Precision.HIGHEST)
    tap_cols = tap_spec[:, :, row_count:] + jnp.concatenate(
        [tap_spec[1:, :, :row_count], jnp.zeros((1, group, row_count), jnp.float32)], axis=0
    )
    tap_grads = swap_layout(tap_cols.transpose(2, 0, 1)).reshape(row_count, local_width)

    gated_wide = grad_gated.astype(jnp.float32)
    grad_streams = jnp.stack(
        [grad_query, gated_wide * value_conv, gated_wide * key_conv], axis=1
    ).astype(jnp.bfloat16)
    grad_streams = grad_streams.reshape(row_count, 3 * local_width)
    after = neighbour_rows(grad_streams[:2], -1)
    padded = (
        jnp.concatenate([grad_streams, after], axis=0)
        .astype(jnp.float32)
        .reshape(row_count + 2, 3, local_width)
    )
    stream_grads = (
        short_weight[:, 0] * padded[:row_count]
        + short_weight[:, 1] * padded[1 : row_count + 1]
        + short_weight[:, 2] * padded[2:]
    ).astype(jnp.bfloat16)
    return (operator_out, stream_grads, tap_grads)


def solution(mesh):
    return jax.shard_map(
        on_device,
        mesh=mesh,
        in_specs=(
            P("seq", "chan"),
            P(None, None, "chan"),
            P(None, None, "chan"),
            P(None, "chan"),
            P("seq", "chan"),
        ),
        out_specs=(P("seq", "chan"), P("seq", None, "chan"), P("seq", "chan")),
        check_vma=False,
    )
```

time: 380 us -> 208 us (0.55)
  waiting for transfers between devices: 174 us -> 62.8 us
  other arithmetic: 116 us -> 37.3 us
  starting transfers between devices: 4.12 us -> 36.4 us
  matrix products: 32.6 us -> 11.5 us
  local copies, waits for them, and re-layouts: 34.5 us -> 41.8 us
    all_gather x2 -> x0, waiting for transfers between devices: 84.8 us -> none  [the longest x1 77.8 us: on_device(): backward_pieces = lax.all_gather(grad_spec, 'seq', axis=0, tiled=True)]
    all_to_all x0 -> x5, starting transfers between devices: none -> 32.6 us  [swap_layout(): return lax.all_to_all(values, 'seq', 1, 1, tiled=True)]
    dynamic_update_slice x16 -> x0, other arithmetic: 30.8 us -> none  [backward_add_block(): lax.dynamic_update_index_in_dim(filter_grad, current, clipped, 0)]
    all_to_all x0 -> x5, waiting for transfers between devices: none -> 29.4 us  [swap_layout(): return lax.all_to_all(values, 'seq', 1, 1, tiled=True)]
    reduce_scatter x1 -> x0, waiting for transfers between devices: 28.7 us -> none  [on_device(): lax.psum_scatter(tap_terms.reshape(seq_count * row_count, local_width).as...]
    dot_general x6, matrix products: 27.4 us -> 6.27 us  [the longest x1 1.39 us: on_device(): jnp.einsum('bck,kt->tbc', spectral_grad.astype(jnp.bfloat16), half_table,...]
    all_gather x1, waiting for transfers between devices: 48.9 us -> 31.4 us  [on_device(): lax.all_gather(tokens, 'chan', axis=1, tiled=True)]
    convert_element_type x34 -> x2, other arithmetic: 19 us -> 2.38 us  [the longest x1 1.7 us: on_device(): grad_long = (cot_wide * query_conv).astype(jnp.bfloat16)]
  transfers between devices with their start and end apart: 6 -> 8, of which waited for: 6 -> 6; matrix products, arithmetic and copies ran while one was open for 45% -> 23% of each run, Pallas kernels for 0% -> 0%
where the time goes in v1:
time: 208 us; the launch traced here: 206 us
  waiting for transfers between devices  62.8 us (30%)
  local copies, waits for them, and re-layouts  41.8 us (20%)
  other arithmetic  37.3 us (18%)
  starting transfers between devices  36.4 us (18%)
  between operations  16.3 us (8%)
  matrix products  11.5 us (6%)
    all_to_all x5, starting transfers between devices, swap_layout(): return lax.all_to_all(values, 'seq', 1, 1, tiled=True)  32.6 us
    all_gather x1, waiting for transfers between devices, on_device(): lax.all_gather(tokens, 'chan', axis=1, tiled=True)  31.4 us
    all_to_all x5, waiting for transfers between devices, swap_layout(): return lax.all_to_all(values, 'seq', 1, 1, tiled=True)  29.4 us
    unnamed x290, local copies, waits for them, and re-layouts  20 us
    add x16, other arithmetic, spectral_adjoint(): real_out = left_re * grad_re + jnp.where(first_row, 0.0, cross_term)  11.8 us
    mul x15, local copies, waits for them, and re-layouts, spectral_product(): real_out = left_re * right_re - jnp.where(first_row, 0.0, cross_term)  9.12 us
    reduce_sum x15, other arithmetic, on_device(): jnp.sum(spectral_adjoint(own_spec[:seq_count - lag_step], ahead), axis=0)  7.78 us
    dot_general x1, matrix products, on_device(): jnp.dot(lax.all_gather(tokens, 'chan', axis=1, tiled=True), weight_cols,...  5.25 us
  transfers between devices with their start and end apart: 8, of which 6 were waited for; matrix products, arithmetic and copies ran while one was open for 23% of the time, Pallas kernels for 0%

profile of v1, /device:TPU:2, one launch (start us, length us, event | category | flops | bytes accessed | tf_op | source)
XLA Modules:
  0.0 206.2 jit_solution(6617892866155665454)
XLA Ops:
  9.1 1.3 constant_dynamic-slice_fusion
  11.0 8.7 %copy.18 = bf16[4096,3,256]{0,2,1:T(8,128)(2,1)} copy(bf16[4096,3,256]{2,0,1:T(8,128)(2,1)} %param.6) | data formatting | bytes 12582912 | tf_op args[1]
  20.0 2.2 %copy.23 = bf16[15,256,16]{1,2,0:T(8,128)(2,1)} copy(bf16[15,256,16]{2,1,0:T(8,128)(2,1)} %bitcast.155) | data formatting | bytes 245760 | tf_op jit(solution)/shard_map/slice | solution.py:110
  22.2 2.1 %negate_select_fusion.2 = (f32[256,512]{1,0:T(8,128)S(1)}, f32[256,512]{1,0:T(8,128)S(1)}) fusion(f32[512]{0:T(512)S(1)} %fusion.64, pred[256]{0:T(512)(128)(4,1)S(1)} %iota_compare_fusion.31), kind=kLoop, calls=%fused_computation.115 | loop fusion | flops 2097152 | bytes 1050880 | tf_op jit(solution)/shard_map/jit(_where)/select_n | solution.py:23
  34.6 1.7 select_convert_fusion
  36.3 31.4 %all-gather.2.cloned.1.call-done = bf16[256,4096]{1,0:T(8,128)(2,1)} async-done(((bf16[256,256]{1,0:T(8,128)(2,1)}), bf16[256,4096]{1,0:T(8,128)(2,1)}) %all-gather.2.cloned.1.call-update) | async-done | bytes 2097168 | tf_op jit(solution)/shard_map/all_gather | solution.py:84
  67.8 5.3 %convolution_convert_fusion = bf16[256,768]{1,0:T(8,128)(2,1)S(1)} fusion(bf16[256,4096]{1,0:T(8,128)(2,1)} %all-gather.2.cloned.1.call-done, bf16[4096,768]{0,1:T(8,128)(2,1)} %bitcast.153), kind=kOutput, calls=%fused_computation | convolution fusion | flops 1610809344 | bytes 8781824 | tf_op jit(solution)/shard_map/dot_general | solution.py:83
  73.0 2.5 %collective-permute-start = (bf16[2,768]{1,0:T(2,128)(2,1)S(1)}, bf16[2,768]{1,0:T(2,128)(2,1)S(1)}, u32[]{:S(2)}, u32[]{:S(2)}) collective-permute-start(bf16[2,768]{1,0:T(2,128)(2,1)S(1)} %slice.802), channel_id=1, source_target_pairs={{0,16},{16,32},{32,48},{48,64},{64,80},{80,96},{96,112},{112,128},... | collective-permute-start | bytes 9224 | tf_op jit(solution)/shard_map/ppermute | solution.py:12
  75.6 1.2 collective-permute-done
  76.9 1.5 fusion.114
  78.5 2.4 %copy.19 = f32[256,768]{0,1:T(8,128)} copy(f32[256,768]{1,0:T(8,128)} %get-tuple-element.22) | data formatting | bytes 1572864 | tf_op jit(solution)/shard_map/slice | solution.py:96
  80.8 2.3 %copy.20 = f32[256,768]{0,1:T(8,128)} copy(f32[256,768]{1,0:T(8,128)} %get-tuple-element.24) | data formatting | bytes 1572864 | tf_op jit(solution)/shard_map/slice | solution.py:97
  84.3 2.0 multiply_add_fusion
  87.0 10.9 %all-to-all-start = ((bf16[256,16,16]{0,2,1:T(8,128)(2,1)}), bf16[256,16,16]{0,2,1:T(8,128)(2,1)S(1)}, u32[]{:S(2)}, u32[]{:S(2)}) async-start(bf16[256,16,16]{0,2,1:T(8,128)(2,1)} %bitcast.10), calls=%async_computation | async-start | bytes 262144 | tf_op jit(solution)/shard_map/all_to_all | solution.py:70
  97.9 1.7 multiply_convert_fusion.1
  99.7 8.0 %all-to-all-done = bf16[256,16,16]{0,2,1:T(8,128)(2,1)S(1)} async-done(((bf16[256,16,16]{0,2,1:T(8,128)(2,1)}), bf16[256,16,16]{0,2,1:T(8,128)(2,1)S(1)}, u32[]{:S(2)}, u32[]{:S(2)}) %all-to-all-start) | async-done | bytes 131104 | tf_op jit(solution)/shard_map/all_to_all | solution.py:70
  107.6 1.2 fusion.116
  113.1 4.2 %all-to-all-start.1 = ((bf16[256,16,16]{0,2,1:T(8,128)(2,1)}), bf16[256,16,16]{0,2,1:T(8,128)(2,1)}, u32[]{:S(2)}, u32[]{:S(2)}) async-start(bf16[256,16,16]{0,2,1:T(8,128)(2,1)} %convolution_convert_fusion.5), calls=%async_computation.1 | async-start | bytes 262144 | tf_op jit(solution)/shard_map/all_to_all | solution.py:70
  117.3 1.7 copy.26
  118.9 8.1 %all-to-all-done.1 = bf16[256,16,16]{0,2,1:T(8,128)(2,1)} async-done(((bf16[256,16,16]{0,2,1:T(8,128)(2,1)}), bf16[256,16,16]{0,2,1:T(8,128)(2,1)}, u32[]{:S(2)}, u32[]{:S(2)}) %all-to-all-start.1) | async-done | bytes 131104 | tf_op jit(solution)/shard_map/all_to_all | solution.py:70
  127.0 1.7 fusion.43
  128.7 4.2 %all-to-all-start.2 = ((bf16[256,16,16]{0,2,1:T(8,128)(2,1)}), bf16[256,16,16]{0,2,1:T(8,128)(2,1)}, u32[]{:S(2)}, u32[]{:S(2)}) async-start(bf16[256,16,16]{0,2,1:T(8,128)(2,1)} %bitcast.163), calls=%async_computation.2 | async-start | bytes 262144 | tf_op jit(solution)/shard_map/all_to_all | solution.py:70
  132.9 1.7 copy.27
  134.6 1.7 fusion.45
  136.2 6.5 %all-to-all-done.2 = bf16[256,16,16]{0,2,1:T(8,128)(2,1)} async-done(((bf16[256,16,16]{0,2,1:T(8,128)(2,1)}), bf16[256,16,16]{0,2,1:T(8,128)(2,1)}, u32[]{:S(2)}, u32[]{:S(2)}) %all-to-all-start.2) | async-done | bytes 131104 | tf_op jit(solution)/shard_map/all_to_all | solution.py:70
  142.7 1.3 fusion.117
  157.8 1.4 convolution_convert_fusion.4
  159.2 4.2 %all-to-all-start.3 = ((bf16[256,16,16]{0,2,1:T(8,128)(2,1)}), bf16[256,16,16]{0,2,1:T(8,128)(2,1)}, u32[]{:S(2)}, u32[]{:S(2)}) async-start(bf16[256,16,16]{0,2,1:T(8,128)(2,1)} %convolution_convert_fusion.4), calls=%async_computation.3 | async-start | bytes 262144 | tf_op jit(solution)/shard_map/all_to_all | solution.py:70
  175.4 1.3 collective-permute-start.1
  177.5 9.2 %all-to-all-start.4 = ((f32[256,16,16]{0,2,1:T(8,128)}), f32[256,16,16]{0,2,1:T(8,128)}, u32[]{:S(2)}, u32[]{:S(2)}) async-start(f32[256,16,16]{0,2,1:T(8,128)} %fusion.51), calls=%async_computation.4 | async-start | bytes 524288 | tf_op jit(solution)/shard_map/all_to_all | solution.py:70
  190.6 6.9 %all-to-all-done.4 = f32[256,16,16]{0,2,1:T(8,128)} async-done(((f32[256,16,16]{0,2,1:T(8,128)}), f32[256,16,16]{0,2,1:T(8,128)}, u32[]{:S(2)}, u32[]{:S(2)}) %all-to-all-start.4) | async-done | bytes 262176 | tf_op jit(solution)/shard_map/all_to_all | solution.py:70
  197.5 1.8 copy.29
  (408 shorter events, 47.8 us)
Async XLA Ops:
  7.2 60.6 %all-gather.2.cloned.1.call-start = ((), (), s32[]{:S(2)}) async-start(), calls=%async_computation.5 | async-start | bytes 2228224 | tf_op jit(solution)/shard_map/all_gather | solution.py:84
  24.4 10.3 %copy-start.132 = (s32[256]{0:T(256)S(1)}, s32[256]{0:T(256)}, u32[]{:S(2)}) copy-start(s32[256]{0:T(256)} %iota_add_fusion) | copy-start | bytes 3076
  73.0 3.8 %collective-permute-start = (bf16[2,768]{1,0:T(2,128)(2,1)S(1)}, bf16[2,768]{1,0:T(2,128)(2,1)S(1)}, u32[]{:S(2)}, u32[]{:S(2)}) collective-permute-start(bf16[2,768]{1,0:T(2,128)(2,1)S(1)} %slice.802), channel_id=1, source_target_pairs={{0,16},{16,32},{32,48},{48,64},{64,80},{80,96},{96,112},{112,128},... | collective-permute-start | bytes 9224 | tf_op jit(solution)/shard_map/ppermute | solution.py:12
  75.5 8.8 %copy-start.125 = (f32[3,256]{1,0:T(4,128)}, f32[3,256]{1,0:T(4,128)S(1)}, u32[]{:S(2)}) copy-start(f32[3,256]{1,0:T(4,128)S(1)} %get-tuple-element.200) | copy-start | bytes 9220
  75.6 8.7 %copy-start.127 = (f32[3,256]{1,0:T(4,128)}, f32[3,256]{1,0:T(4,128)S(1)}, u32[]{:S(2)}) copy-start(f32[3,256]{1,0:T(4,128)S(1)} %get-tuple-element.201) | copy-start | bytes 9220
  75.6 8.7 %copy-start.129 = (f32[3,1,256]{2,0,1:T(4,128)}, f32[3,1,256]{2,0,1:T(4,128)S(1)}, u32[]{:S(2)}) copy-start(f32[3,1,256]{2,0,1:T(4,128)S(1)} %copy.40) | copy-start | bytes 9220
  84.3 13.6 %copy-start.133 = (s32[256]{0:T(256)S(1)}, s32[256]{0:T(256)}, u32[]{:S(2)}) copy-start(s32[256]{0:T(256)} %iota_add_fusion) | copy-start | bytes 3076
  87.0 20.6 %all-to-all-start = ((bf16[256,16,16]{0,2,1:T(8,128)(2,1)}), bf16[256,16,16]{0,2,1:T(8,128)(2,1)S(1)}, u32[]{:S(2)}, u32[]{:S(2)}) async-start(bf16[256,16,16]{0,2,1:T(8,128)(2,1)} %bitcast.10), calls=%async_computation | async-start | bytes 262144 | tf_op jit(solution)/shard_map/all_to_all | solution.py:70
  113.1 13.9 %all-to-all-start.1 = ((bf16[256,16,16]{0,2,1:T(8,128)(2,1)}), bf16[256,16,16]{0,2,1:T(8,128)(2,1)}, u32[]{:S(2)}, u32[]{:S(2)}) async-start(bf16[256,16,16]{0,2,1:T(8,128)(2,1)} %convolution_convert_fusion.5), calls=%async_computation.1 | async-start | bytes 262144 | tf_op jit(solution)/shard_map/all_to_all | solution.py:70
  128.7 13.9 %all-to-all-start.2 = ((bf16[256,16,16]{0,2,1:T(8,128)(2,1)}), bf16[256,16,16]{0,2,1:T(8,128)(2,1)}, u32[]{:S(2)}, u32[]{:S(2)}) async-start(bf16[256,16,16]{0,2,1:T(8,128)(2,1)} %bitcast.163), calls=%async_computation.2 | async-start | bytes 262144 | tf_op jit(solution)/shard_map/all_to_all | solution.py:70
  144.5 4.8 %copy-start.22 = (f32[8,16,512]{2,1,0:T(8,128)S(1)}, f32[8,16,512]{2,1,0:T(8,128)}, u32[]{:S(2)}) copy-start(f32[8,16,512]{2,1,0:T(8,128)} %copy-done.21) | copy-start | bytes 786436
  144.5 4.8 %copy-start.95 = (f32[16,256]{1,0:T(8,128)S(1)}, f32[16,256]{1,0:T(8,128)}, u32[]{:S(2)}) copy-start(f32[16,256]{1,0:T(8,128)} %get-tuple-element.179) | copy-start | bytes 49156
  157.7 8.4 %copy-start.56 = (f32[5,16,256]{2,1,0:T(8,128)S(1)}, f32[5,16,256]{2,1,0:T(8,128)}, u32[]{:S(2)}) copy-start(f32[5,16,256]{2,1,0:T(8,128)} %get-tuple-element.81) | copy-start | bytes 245764
  157.7 9.3 %copy-start.54 = (f32[6,16,256]{2,1,0:T(8,128)S(1)}, f32[6,16,256]{2,1,0:T(8,128)}, u32[]{:S(2)}) copy-start(f32[6,16,256]{2,1,0:T(8,128)} %get-tuple-element.67) | copy-start | bytes 294916
  157.7 9.3 %copy-start.55 = (f32[6,16,256]{2,1,0:T(8,128)S(1)}, f32[6,16,256]{2,1,0:T(8,128)}, u32[]{:S(2)}) copy-start(f32[6,16,256]{2,1,0:T(8,128)} %get-tuple-element.68) | copy-start | bytes 294916
  157.8 9.4 %copy-start.52 = (f32[7,16,256]{2,1,0:T(8,128)S(1)}, f32[7,16,256]{2,1,0:T(8,128)}, u32[]{:S(2)}) copy-start(f32[7,16,256]{2,1,0:T(8,128)} %get-tuple-element.53) | copy-start | bytes 344068
  157.8 9.4 %copy-start.53 = (f32[7,16,256]{2,1,0:T(8,128)S(1)}, f32[7,16,256]{2,1,0:T(8,128)}, u32[]{:S(2)}) copy-start(f32[7,16,256]{2,1,0:T(8,128)} %get-tuple-element.54) | copy-start | bytes 344068
  157.8 10.5 %copy-start.46 = (f32[9,16,256]{2,1,0:T(8,128)S(1)}, f32[9,16,256]{2,1,0:T(8,128)}, u32[]{:S(2)}) copy-start(f32[9,16,256]{2,1,0:T(8,128)} %get-tuple-element.33) | copy-start | bytes 442372
  159.2 15.1 %all-to-all-start.3 = ((bf16[256,16,16]{0,2,1:T(8,128)(2,1)}), bf16[256,16,16]{0,2,1:T(8,128)(2,1)}, u32[]{:S(2)}, u32[]{:S(2)}) async-start(bf16[256,16,16]{0,2,1:T(8,128)(2,1)} %convolution_convert_fusion.4), calls=%async_computation.3 | async-start | bytes 262144 | tf_op jit(solution)/shard_map/all_to_all | solution.py:70
  163.3 6.9 %copy-start.44 = (f32[11,16,256]{2,1,0:T(8,128)S(1)}, f32[11,16,256]{2,1,0:T(8,128)}, u32[]{:S(2)}) copy-start(f32[11,16,256]{2,1,0:T(8,128)} %get-tuple-element.29) | copy-start | bytes 540676
  163.4 7.9 %copy-start.42 = (f32[12,16,256]{2,1,0:T(8,128)S(1)}, f32[12,16,256]{2,1,0:T(8,128)}, u32[]{:S(2)}) copy-start(f32[12,16,256]{2,1,0:T(8,128)} %get-tuple-element.25) | copy-start | bytes 589828
  163.4 7.9 %copy-start.43 = (f32[12,16,256]{2,1,0:T(8,128)S(1)}, f32[12,16,256]{2,1,0:T(8,128)}, u32[]{:S(2)}) copy-start(f32[12,16,256]{2,1,0:T(8,128)} %get-tuple-element.26) | copy-start | bytes 589828
  163.4 7.9 %copy-start.40 = (f32[13,16,256]{2,1,0:T(8,128)S(1)}, f32[13,16,256]{2,1,0:T(8,128)}, u32[]{:S(2)}) copy-start(f32[13,16,256]{2,1,0:T(8,128)} %get-tuple-element.20) | copy-start | bytes 638980
  163.4 7.9 %copy-start.41 = (f32[13,16,256]{2,1,0:T(8,128)S(1)}, f32[13,16,256]{2,1,0:T(8,128)}, u32[]{:S(2)}) copy-start(f32[13,16,256]{2,1,0:T(8,128)} %get-tuple-element.21) | copy-start | bytes 638980
  163.4 7.9 %copy-start.36 = (f32[14,16,256]{2,1,0:T(8,128)S(1)}, f32[14,16,256]{2,1,0:T(8,128)}, u32[]{:S(2)}) copy-start(f32[14,16,256]{2,1,0:T(8,128)} %get-tuple-element.16) | copy-start | bytes 688132
  163.4 7.9 %copy-start.37 = (f32[14,16,256]{2,1,0:T(8,128)S(1)}, f32[14,16,256]{2,1,0:T(8,128)}, u32[]{:S(2)}) copy-start(f32[14,16,256]{2,1,0:T(8,128)} %get-tuple-element.17) | copy-start | bytes 688132
  163.4 8.0 %copy-start.33 = (f32[15,16,256]{2,1,0:T(8,128)S(1)}, f32[15,16,256]{2,1,0:T(8,128)}, u32[]{:S(2)}) copy-start(f32[15,16,256]{2,1,0:T(8,128)} %get-tuple-element.14) | copy-start | bytes 737284
  163.4 8.0 %copy-start.34 = (f32[15,16,256]{2,1,0:T(8,128)S(1)}, f32[15,16,256]{2,1,0:T(8,128)}, u32[]{:S(2)}) copy-start(f32[15,16,256]{2,1,0:T(8,128)} %get-tuple-element.15) | copy-start | bytes 737284
  165.2 6.2 %copy-start.45 = (f32[16,16,512]{2,1,0:T(8,128)S(1)}, f32[16,16,512]{2,1,0:T(8,128)}, u32[]{:S(2)}) copy-start(f32[16,16,512]{2,1,0:T(8,128)} %constant_dynamic-update-slice_fusion.15) | copy-start | bytes 1572868
  175.4 11.4 %copy-start.20 = (bf16[256,3,256]{0,2,1:T(8,128)(2,1)}, bf16[256,3,256]{0,2,1:T(8,128)(2,1)S(1)}, u32[]{:S(2)}) copy-start(bf16[256,3,256]{0,2,1:T(8,128)(2,1)S(1)} %maximum_convert_fusion) | copy-start | bytes 1179652
  175.4 11.3 %collective-permute-start.1 = (bf16[2,768]{0,1:T(8,128)(2,1)S(1)}, bf16[2,768]{0,1:T(8,128)(2,1)S(1)}, u32[]{:S(2)}, u32[]{:S(2)}) collective-permute-start(bf16[2,768]{0,1:T(8,128)(2,1)S(1)} %bitcast.164), channel_id=1, source_target_pairs={{16,0},{32,16},{48,32},{64,48},{80,64},{96,80},{112,96},{128,112},... | collective-permute-start | bytes 9224 | tf_op jit(solution)/shard_map/ppermute | solution.py:12
  177.5 20.0 %all-to-all-start.4 = ((f32[256,16,16]{0,2,1:T(8,128)}), f32[256,16,16]{0,2,1:T(8,128)}, u32[]{:S(2)}, u32[]{:S(2)}) async-start(f32[256,16,16]{0,2,1:T(8,128)} %fusion.51), calls=%async_computation.4 | async-start | bytes 524288 | tf_op jit(solution)/shard_map/all_to_all | solution.py:70
  (110 other events, 224.6 us)
Sparse Core Ops, SparseCore 0:
  10.6 57.1 all-gather.1

commit v2 on v1

--- a/solution.py
+++ b/solution.py
@@ -79,13 +79,14 @@
     full_table = forward.astype(jnp.bfloat16)
     half_table = full_table[:, :row_count]
     back_table = inverse.astype(jnp.bfloat16)
-    weight_cols = in_weight.reshape(in_weight.shape[0], 3 * local_width)
-    streams = jnp.dot(
-        lax.all_gather(tokens, "chan", axis=1, tiled=True),
-        weight_cols,
-        preferred_element_type=jnp.float32,
-    )
-    streams = streams.astype(jnp.bfloat16)
+    chan_count = lax.axis_size("chan")
+    copies = jnp.broadcast_to(tokens[None], (chan_count,) + tokens.shape)
+    gathered = lax.all_to_all(copies, "chan", 0, 0, tiled=True)
+    weight_parts = in_weight.reshape(chan_count, local_width, 3, local_width)
+    streams = jnp.einsum(
+        "stf,sfqc->tqc", gathered, weight_parts, preferred_element_type=jnp.float32
+    ).astype(jnp.bfloat16)
+    streams = streams.reshape(row_count, 3 * local_width)
     before = neighbour_rows(streams[row_count - 2 :], 1)
     extended = (
         jnp.concatenate([before, streams], axis=0)
@@ -99,8 +100,16 @@
     )
     query_conv, key_conv, value_conv = (conv_out[:, 0], conv_out[:, 1], conv_out[:, 2])
     gated = (key_conv * value_conv).astype(jnp.bfloat16)
-
-    gated_cols = swap_layout(gated.reshape(row_count, seq_count, group))
+    cot_wide = cotangent.astype(jnp.float32)
+    grad_long = (cot_wide * query_conv).astype(jnp.bfloat16)
+
+    both_cols = swap_layout(
+        jnp.concatenate(
+            [gated.reshape(row_count, seq_count, group), grad_long.reshape(row_count, seq_count, group)],
+            axis=2,
+        )
+    )
+    gated_cols, grad_long_cols = (both_cols[..., :group], both_cols[..., group:])
     own_spec = jnp.einsum(
         "tbc,kt->bck", gated_cols, half_table, preferred_element_type=jnp.float32
     ).astype(jnp.bfloat16)
@@ -122,14 +131,7 @@
         "bck,ak->abc", mixed_spec.astype(jnp.bfloat16), back_table,
         preferred_element_type=jnp.float32,
     ).astype(jnp.bfloat16)
-    long_out = swap_layout(long_cols).reshape(row_count, local_width)
-
-    operator_out = (query_conv * long_out.astype(jnp.float32)).astype(jnp.bfloat16)
-    cot_wide = cotangent.astype(jnp.float32)
-    grad_long = (cot_wide * query_conv).astype(jnp.bfloat16)
-    grad_query = cot_wide * long_out.astype(jnp.float32)
-
-    grad_long_cols = swap_layout(grad_long.reshape(row_count, seq_count, group))
+
     grad_spec = jnp.einsum(
         "abc,ak->bck", grad_long_cols, back_table, preferred_element_type=jnp.float32
     ).astype(jnp.bfloat16)
@@ -147,15 +149,28 @@
         "bck,kt->tbc", spectral_grad.astype(jnp.bfloat16), half_table,
         preferred_element_type=jnp.float32,
     ).astype(jnp.bfloat16)
-    grad_gated = swap_layout(gated_grad_cols).reshape(row_count, local_width)
 
     tap_spec = jnp.einsum("dck,kn->dcn", filter_grad, forward, precision=lax.Precision.HIGHEST)
     tap_cols = tap_spec[:, :, row_count:] + jnp.concatenate(
         [tap_spec[1:, :, :row_count], jnp.zeros((1, group, row_count), jnp.float32)], axis=0
     )
-    tap_grads = swap_layout(tap_cols.transpose(2, 0, 1)).reshape(row_count, local_width)
-
-    gated_wide = grad_gated.astype(jnp.float32)
+    returned = swap_layout(
+        jnp.concatenate(
+            [
+                long_cols.astype(jnp.float32),
+                gated_grad_cols.astype(jnp.float32),
+                tap_cols.transpose(2, 0, 1),
+            ],
+            axis=2,
+        )
+    )
+    long_out = returned[..., :group].reshape(row_count, local_width)
+    gated_wide = returned[..., group : 2 * group].reshape(row_count, local_width)
+    tap_grads = returned[..., 2 * group :].reshape(row_count, local_width)
+
+    operator_out = (query_conv * long_out).astype(jnp.bfloat16)
+    grad_query = cot_wide * long_out
+
     grad_streams = jnp.stack(
         [grad_query, gated_wide * value_conv, gated_wide * key_conv], axis=1
     ).astype(jnp.bfloat16)

time: 208 us -> 124 us (0.60)
  waiting for transfers between devices: 62.8 us -> 21.1 us
  blocking collectives: 0 us -> 24 us
  other arithmetic: 37.3 us -> 15 us
  local copies, waits for them, and re-layouts: 41.8 us -> 26.6 us
  between operations: 16.3 us -> 1.88 us
  starting transfers between devices: 36.4 us -> 24.4 us
    all_gather x1 -> x0, waiting for transfers between devices: 31.4 us -> none  [on_device(): lax.all_gather(tokens, 'chan', axis=1, tiled=True)]
    all_to_all x0 -> x1, blocking collectives: none -> 24 us  [swap_layout(): return lax.all_to_all(values, 'seq', 1, 1, tiled=True)]
    all_to_all x5 -> x1, waiting for transfers between devices: 29.4 us -> 6.34 us  [swap_layout(): return lax.all_to_all(values, 'seq', 1, 1, tiled=True)]
    all_to_all x5 -> x1, starting transfers between devices: 32.6 us -> 12.4 us  [swap_layout(): return lax.all_to_all(values, 'seq', 1, 1, tiled=True)]
    unnamed x290 -> x107, local copies, waits for them, and re-layouts: 20 us -> 5.97 us
    add x16 -> x1, other arithmetic: 11.8 us -> 0.01 us  [spectral_adjoint(): real_out = left_re * grad_re + jnp.where(first_row, 0.0, cross_term)]
    all_to_all x0 -> x1, waiting for transfers between devices: none -> 10.7 us  [on_device(): gathered = lax.all_to_all(copies, 'chan', 0, 0, tiled=True)]
    all_to_all x0 -> x1, starting transfers between devices: none -> 7.48 us  [on_device(): gathered = lax.all_to_all(copies, 'chan', 0, 0, tiled=True)]
  transfers between devices with their start and end apart: 8 -> 4, of which waited for: 6 -> 3; matrix products, arithmetic and copies ran while one was open for 23% -> 21% of each run, Pallas kernels for 0% -> 0%
where the time goes in v2:
time: 124 us; the launch traced here: 123 us
  local copies, waits for them, and re-layouts  26.6 us (21%)
  starting transfers between devices  24.4 us (20%)
  blocking collectives  24 us (19%)
  waiting for transfers between devices  21.1 us (17%)
  other arithmetic  15 us (12%)
  matrix products  9.97 us (8%)
  between operations  1.88 us (2%)
    all_to_all x1, blocking collectives, swap_layout(): return lax.all_to_all(values, 'seq', 1, 1, tiled=True)  24 us
    all_to_all x1, starting transfers between devices, swap_layout(): return lax.all_to_all(values, 'seq', 1, 1, tiled=True)  12.4 us
    all_to_all x1, waiting for transfers between devices, on_device(): gathered = lax.all_to_all(copies, 'chan', 0, 0, tiled=True)  10.7 us
    mul x15, local copies, waits for them, and re-layouts, spectral_product(): real_out = left_re * right_re - jnp.where(first_row, 0.0, cross_term)  9.24 us
    all_to_all x1, starting transfers between devices, on_device(): gathered = lax.all_to_all(copies, 'chan', 0, 0, tiled=True)  7.48 us
    all_to_all x1, waiting for transfers between devices, swap_layout(): return lax.all_to_all(values, 'seq', 1, 1, tiled=True)  6.34 us
    unnamed x107, local copies, waits for them, and re-layouts  5.97 us
    dot_general x1, matrix products, on_device(): jnp.einsum('stf,sfqc->tqc', gathered, weight_parts, preferred_element_typ...  5.23 us
  transfers between devices with their start and end apart: 4, of which 3 were waited for; matrix products, arithmetic and copies ran while one was open for 21% of the time, Pallas kernels for 0%

profile of v2, /device:TPU:2, one launch (start us, length us, event | category | flops | bytes accessed | tf_op | source)
XLA Modules:
  0.0 122.9 jit_solution(16363661491549152992)
XLA Ops:
  0.6 2.6 %broadcast_in_dim.729 = bf16[16,256,256]{2,1,0:T(8,128)(2,1)} broadcast(bf16[256,256]{1,0:T(8,128)(2,1)} %param.5), dimensions={1,2} | broadcast | bytes 2228224 | tf_op jit(solution)/shard_map/broadcast_in_dim | solution.py:83
  3.2 7.5 %all-to-all-start = ((bf16[16,256,256]{2,1,0:T(8,128)(2,1)}), bf16[16,256,256]{2,1,0:T(8,128)(2,1)}, u32[]{:S(2)}, u32[]{:S(2)}) async-start(bf16[16,256,256]{2,1,0:T(8,128)(2,1)} %broadcast_in_dim.729), calls=%async_computation | async-start | bytes 4194304 | tf_op jit(solution)/shard_map/all_to_all | solution.py:84
  10.8 1.3 %constant_dynamic-slice_fusion = bf16[3840,16]{1,0:T(8,128)(2,1)} fusion(bf16[4096,256]{1,0:T(8,128)(2,1)S(1)} %copy-done, s32[]{:T(128)S(6)} %select_n.380), kind=kLoop, calls=%fused_computation.433 | loop fusion | bytes 245764 | tf_op jit(solution)/shard_map/slice | solution.py:119
  13.0 2.2 %copy.27 = bf16[15,256,16]{1,2,0:T(8,128)(2,1)} copy(bf16[15,256,16]{2,1,0:T(8,128)(2,1)} %bitcast.165) | data formatting | bytes 245760 | tf_op jit(solution)/shard_map/slice | solution.py:119
  15.5 2.1 %negate_select_fusion.2 = (f32[256,512]{1,0:T(8,128)S(1)}, f32[256,512]{1,0:T(8,128)S(1)}) fusion(f32[512]{0:T(512)S(1)} %fusion.76, pred[256]{0:T(512)(128)(4,1)S(1)} %iota_compare_fusion.31), kind=kLoop, calls=%fused_computation.122 | loop fusion | flops 2097152 | bytes 1050880 | tf_op jit(solution)/shard_map/jit(_where)/select_n | solution.py:23
  18.1 0.7 slice_convert_fusion.45
  19.4 0.6 slice_bitcast_fusion.31
  20.6 0.6 slice_bitcast_fusion.27
  21.9 0.6 slice_bitcast_fusion.23
  24.3 0.6 slice_bitcast_fusion.17
  26.2 0.6 slice_bitcast_fusion.11
  28.6 10.7 %all-to-all-done = bf16[16,256,256]{2,1,0:T(8,128)(2,1)} async-done(((bf16[16,256,256]{2,1,0:T(8,128)(2,1)}), bf16[16,256,256]{2,1,0:T(8,128)(2,1)}, u32[]{:S(2)}, u32[]{:S(2)}) %all-to-all-start) | async-done | bytes 2097184 | tf_op jit(solution)/shard_map/all_to_all | solution.py:84
  39.4 5.2 %fusion.5 = bf16[256,3,256]{2,0,1:T(8,128)(2,1)S(1)} fusion(bf16[16,256,3,256]{3,1,0,2:T(8,128)(2,1)} %bitcast.180, bf16[16,256,256]{2,1,0:T(8,128)(2,1)} %all-to-all-done), kind=kOutput, calls=%fused_computation.3 | convolution fusion | flops 1610809344 | bytes 8781824 | tf_op jit(solution)/shard_map/stf,sfqc->tqc/dot_general | solution.py:86
  45.2 3.2 %collective-permute-start = (bf16[2,768]{1,0:T(2,128)(2,1)}, bf16[2,768]{1,0:T(2,128)(2,1)}, u32[]{:S(2)}, u32[]{:S(2)}) collective-permute-start(bf16[2,768]{1,0:T(2,128)(2,1)} %bitcast.4), channel_id=1, source_target_pairs={{0,16},{16,32},{32,48},{48,64},{64,80},{80,96},{96,112},{112,128},... | collective-permute-start | bytes 9224 | tf_op jit(solution)/shard_map/ppermute | solution.py:12
  49.3 0.9 copy.25
  51.3 0.7 pad_maximum_fusion.3
  52.1 12.4 %all-to-all-start.1 = ((bf16[256,16,32]{0,2,1:T(8,128)(2,1)}), bf16[256,16,32]{0,2,1:T(8,128)(2,1)}, u32[]{:S(2)}, u32[]{:S(2)}) async-start(bf16[256,16,32]{0,2,1:T(8,128)(2,1)} %pad_maximum_fusion.3), calls=%async_computation.1 | async-start | bytes 524288 | tf_op jit(solution)/shard_map/all_to_all | solution.py:70
  64.5 2.4 %select_convert_fusion = bf16[256,256]{1,0:T(8,128)(2,1)} fusion(bf16[256]{0:T(256)(128)(2,1)S(1)} %fusion.113, s32[256]{0:T(256)} %iota_add_fusion, pred[256]{0:T(512)(128)(4,1)S(1)} %iota_compare_fusion.31), kind=kLoop, calls=%fused_computation.167 | loop fusion | flops 1048576 | bytes 132864 | tf_op jit(solution)/shard_map/convert.1
  66.9 2.4 %multiply_convert_fusion.1 = bf16[256,256]{1,0:T(8,128)(2,1)} fusion(f32[256]{0:T(256)} %select_multiply_fusion, s32[256]{0:T(256)} %iota_add_fusion), kind=kLoop, calls=%fused_computation.168 | loop fusion | flops 1048576 | bytes 133120 | tf_op jit(solution)/shard_map/convert
  69.3 6.3 %all-to-all-done.1 = bf16[256,16,32]{0,2,1:T(8,128)(2,1)} async-done(((bf16[256,16,32]{0,2,1:T(8,128)(2,1)}), bf16[256,16,32]{0,2,1:T(8,128)(2,1)}, u32[]{:S(2)}, u32[]{:S(2)}) %all-to-all-start.1) | async-done | bytes 262176 | tf_op jit(solution)/shard_map/all_to_all | solution.py:70
  75.7 1.3 %fusion.129 = (f32[16,16,512]{2,1,0:T(8,128)S(1)}, bf16[16,16,512]{2,1,0:T(8,128)(2,1)S(1)}) fusion(bf16[512,512]{1,0:T(8,128)(2,1)} %copy-done.3, bf16[256,16,32]{0,2,1:T(8,128)(2,1)} %all-to-all-done.1), kind=kOutput, calls=%fused_computation.449 | convolution fusion | flops 67371008 | bytes 1179648 | tf_op jit(solution)/shard_map/tbc,kt->bck/dot_general | solution.py:113
  77.1 1.1 fusion.130
  84.4 1.0 fusion.10
  86.6 24.0 %all_to_all.15 = f32[256,16,48]{0,2,1:T(8,128)S(1)} all-to-all(f32[256,16,48]{0,2,1:T(8,128)S(1)} %pad_maximum_fusion.2), channel_id=1, replica_groups=mesh['seq'=16,'chan'=16] {'seq'}, dimensions={1} | all-to-all | bytes 1572864 | tf_op jit(solution)/shard_map/all_to_all | solution.py:70
  110.6 0.8 fusion.127
  111.5 0.7 slice.982
  112.2 1.3 %collective-permute-start.1 = (bf16[2,768]{0,1:T(8,128)(2,1)}, bf16[2,768]{0,1:T(8,128)(2,1)}, u32[]{:S(2)}, u32[]{:S(2)}) collective-permute-start(bf16[2,768]{0,1:T(8,128)(2,1)} %bitcast.68), channel_id=1, source_target_pairs={{16,0},{32,16},{48,32},{64,48},{80,64},{96,80},{112,96},{128,112},... | collective-permute-start | bytes 9224 | tf_op jit(solution)/shard_map/ppermute | solution.py:12
  113.6 0.8 copy.31
  114.3 1.8 %copy.33 = f32[256,256]{1,0:T(8,128)} copy(f32[256,256]{0,1:T(8,128)} %bitcast.174) | data formatting | bytes 524288
  116.1 4.0 %collective-permute-done.1 = bf16[2,768]{0,1:T(8,128)(2,1)} collective-permute-done((bf16[2,768]{0,1:T(8,128)(2,1)}, bf16[2,768]{0,1:T(8,128)(2,1)}, u32[]{:S(2)}, u32[]{:S(2)}) %collective-permute-start.1) | collective-permute-done | bytes 3104 | tf_op jit(solution)/shard_map/ppermute | solution.py:12
  120.1 1.0 maximum_convert_fusion.2
  122.0 0.9 copy.32
  (206 shorter events, 18.6 us)
Async XLA Ops:
  0.6 10.1 %copy-start = (bf16[4096,256]{1,0:T(8,128)(2,1)S(1)}, bf16[4096,256]{1,0:T(8,128)(2,1)}, u32[]{:S(2)}) copy-start(bf16[4096,256]{1,0:T(8,128)(2,1)} %param.8) | copy-start | bytes 6291460
  3.2 36.1 %all-to-all-start = ((bf16[16,256,256]{2,1,0:T(8,128)(2,1)}), bf16[16,256,256]{2,1,0:T(8,128)(2,1)}, u32[]{:S(2)}, u32[]{:S(2)}) async-start(bf16[16,256,256]{2,1,0:T(8,128)(2,1)} %broadcast_in_dim.729), calls=%async_computation | async-start | bytes 4194304 | tf_op jit(solution)/shard_map/all_to_all | solution.py:84
  10.7 1.7 %copy-start.42 = (f32[3,3,256]{2,1,0:T(4,128)S(1)}, f32[3,3,256]{2,1,0:T(4,128)}, u32[]{:S(2)}) copy-start(f32[3,3,256]{2,1,0:T(4,128)} %param.7) | copy-start | bytes 27652
  15.5 2.2 %copy-start.9 = (bf16[15,256,16]{1,2,0:T(8,128)(2,1)S(1)}, bf16[15,256,16]{1,2,0:T(8,128)(2,1)}, u32[]{:S(2)}) copy-start(bf16[15,256,16]{1,2,0:T(8,128)(2,1)} %copy.27) | copy-start | bytes 368644
  17.7 4.8 %copy-start.1 = (f32[256,512]{1,0:T(8,128)}, f32[256,512]{1,0:T(8,128)S(1)}, u32[]{:S(2)}) copy-start(f32[256,512]{1,0:T(8,128)S(1)} %get-tuple-element.235) | copy-start | bytes 1572868
  17.7 5.5 %copy-start.41 = (f32[3,1,256]{2,1,0:T(1,128)S(1)}, f32[3,1,256]{2,1,0:T(1,128)}, u32[]{:S(2)}) copy-start(f32[3,1,256]{2,1,0:T(1,128)} %get-tuple-element.229) | copy-start | bytes 9220
  17.8 4.7 %copy-start.3 = (bf16[512,512]{1,0:T(8,128)(2,1)}, bf16[512,512]{1,0:T(8,128)(2,1)S(1)}, u32[]{:S(2)}) copy-start(bf16[512,512]{1,0:T(8,128)(2,1)S(1)} %fusion.12) | copy-start | bytes 1572868
  39.4 9.6 %copy-start.8 = (bf16[256,256]{1,0:T(8,128)(2,1)S(1)}, bf16[256,256]{1,0:T(8,128)(2,1)}, u32[]{:S(2)}) copy-start(bf16[256,256]{1,0:T(8,128)(2,1)} %param.9) | copy-start | bytes 393220
  39.4 9.7 %copy-start.40 = (f32[3,1,256]{2,1,0:T(1,128)S(1)}, f32[3,1,256]{2,1,0:T(1,128)}, u32[]{:S(2)}) copy-start(f32[3,1,256]{2,1,0:T(1,128)} %get-tuple-element.227) | copy-start | bytes 9220
  45.2 4.1 %collective-permute-start = (bf16[2,768]{1,0:T(2,128)(2,1)}, bf16[2,768]{1,0:T(2,128)(2,1)}, u32[]{:S(2)}, u32[]{:S(2)}) collective-permute-start(bf16[2,768]{1,0:T(2,128)(2,1)} %bitcast.4), channel_id=1, source_target_pairs={{0,16},{16,32},{32,48},{48,64},{64,80},{80,96},{96,112},{112,128},... | collective-permute-start | bytes 9224 | tf_op jit(solution)/shard_map/ppermute | solution.py:12
  52.1 23.6 %all-to-all-start.1 = ((bf16[256,16,32]{0,2,1:T(8,128)(2,1)}), bf16[256,16,32]{0,2,1:T(8,128)(2,1)}, u32[]{:S(2)}, u32[]{:S(2)}) async-start(bf16[256,16,32]{0,2,1:T(8,128)(2,1)} %pad_maximum_fusion.3), calls=%async_computation.1 | async-start | bytes 524288 | tf_op jit(solution)/shard_map/all_to_all | solution.py:70
  75.7 1.4 %copy-start.5 = (bf16[256,256]{1,0:T(8,128)(2,1)S(1)}, bf16[256,256]{1,0:T(8,128)(2,1)}, u32[]{:S(2)}) copy-start(bf16[256,256]{1,0:T(8,128)(2,1)} %select_convert_fusion) | copy-start | bytes 393220
  75.7 1.4 %copy-start.6 = (bf16[256,256]{1,0:T(8,128)(2,1)S(1)}, bf16[256,256]{1,0:T(8,128)(2,1)}, u32[]{:S(2)}) copy-start(bf16[256,256]{1,0:T(8,128)(2,1)} %multiply_convert_fusion.1) | copy-start | bytes 393220
  79.0 0.8 copy-start.28
  79.0 0.8 copy-start.29
  80.8 0.9 copy-start.20
  80.8 0.9 copy-start.21
  81.4 0.7 copy-start.19
  81.9 0.7 copy-start.15
  82.3 0.7 copy-start.13
  82.6 0.7 copy-start.11
  82.6 0.8 copy-start.38
  82.6 0.8 copy-start.39
  82.8 0.8 copy-start.36
  82.8 0.8 copy-start.37
  83.1 0.7 copy-start.35
  83.2 0.8 copy-start.32
  83.2 0.8 copy-start.33
  83.4 1.0 copy-start.2
  83.9 1.6 %copy-start.7 = (f32[1,16,512]{2,1,0:T(8,128)S(1)}, f32[1,16,512]{2,1,0:T(8,128)}, u32[]{:S(2)}) copy-start(f32[1,16,512]{2,1,0:T(8,128)} %get-tuple-element.126) | copy-start | bytes 98308
  84.0 1.6 %copy-start.4 = (bf16[512,512]{1,0:T(8,128)(2,1)S(1)}, bf16[512,512]{1,0:T(8,128)(2,1)}, u32[]{:S(2)}) copy-start(bf16[512,512]{1,0:T(8,128)(2,1)} %copy-done.3) | copy-start | bytes 1572868
  112.2 7.9 %collective-permute-start.1 = (bf16[2,768]{0,1:T(8,128)(2,1)}, bf16[2,768]{0,1:T(8,128)(2,1)}, u32[]{:S(2)}, u32[]{:S(2)}) collective-permute-start(bf16[2,768]{0,1:T(8,128)(2,1)} %bitcast.68), channel_id=1, source_target_pairs={{16,0},{32,16},{48,32},{64,48},{80,64},{96,80},{112,96},{128,112},... | collective-permute-start | bytes 9224 | tf_op jit(solution)/shard_map/ppermute | solution.py:12
  (15 other events, 10.8 us)

commit v3 on v2

--- a/solution.py
+++ b/solution.py
@@ -73,25 +73,31 @@
 def on_device(tokens, in_weight, short_weight, filter_taps, cotangent):
     row_count, local_width = tokens.shape
     seq_count = lax.axis_size("seq")
+    chan_count = lax.axis_size("chan")
     group = local_width // seq_count
     own_block = lax.axis_index("seq")
     forward, inverse = dft_tables(row_count)
     full_table = forward.astype(jnp.bfloat16)
     half_table = full_table[:, :row_count]
     back_table = inverse.astype(jnp.bfloat16)
-    chan_count = lax.axis_size("chan")
+
+    prev_tokens = neighbour_rows(tokens[row_count - 2 :], 1)
+    next_rows = neighbour_rows(jnp.concatenate([tokens[:2], cotangent[:2]], axis=1), -1)
+    next_tokens, next_cot = (next_rows[:, :local_width], next_rows[:, local_width:])
+    edge_tokens = lax.all_gather(
+        jnp.concatenate([prev_tokens, next_tokens], axis=0), "chan", axis=0, tiled=False
+    )
     copies = jnp.broadcast_to(tokens[None], (chan_count,) + tokens.shape)
     gathered = lax.all_to_all(copies, "chan", 0, 0, tiled=True)
     weight_parts = in_weight.reshape(chan_count, local_width, 3, local_width)
     streams = jnp.einsum(
         "stf,sfqc->tqc", gathered, weight_parts, preferred_element_type=jnp.float32
     ).astype(jnp.bfloat16)
-    streams = streams.reshape(row_count, 3 * local_width)
-    before = neighbour_rows(streams[row_count - 2 :], 1)
-    extended = (
-        jnp.concatenate([before, streams], axis=0)
-        .astype(jnp.float32)
-        .reshape(row_count + 2, 3, local_width)
+    edge_streams = jnp.einsum(
+        "stf,sfqc->tqc", edge_tokens, weight_parts, preferred_element_type=jnp.float32
+    ).astype(jnp.bfloat16)
+    extended = jnp.concatenate([edge_streams[:2], streams, edge_streams[2:]], axis=0).astype(
+        jnp.float32
     )
     conv_out = (
         short_weight[:, 0] * extended[2:]
@@ -99,9 +105,9 @@
         + short_weight[:, 2] * extended[:-2]
     )
     query_conv, key_conv, value_conv = (conv_out[:, 0], conv_out[:, 1], conv_out[:, 2])
-    gated = (key_conv * value_conv).astype(jnp.bfloat16)
-    cot_wide = cotangent.astype(jnp.float32)
-    grad_long = (cot_wide * query_conv).astype(jnp.bfloat16)
+    gated = (key_conv[:row_count] * value_conv[:row_count]).astype(jnp.bfloat16)
+    cot_wide = jnp.concatenate([cotangent, next_cot], axis=0).astype(jnp.float32)
+    grad_long = (cot_wide[:row_count] * query_conv[:row_count]).astype(jnp.bfloat16)
 
     both_cols = swap_layout(
         jnp.concatenate(
@@ -154,37 +160,45 @@
     tap_cols = tap_spec[:, :, row_count:] + jnp.concatenate(
         [tap_spec[1:, :, :row_count], jnp.zeros((1, group, row_count), jnp.float32)], axis=0
     )
+    tap_cols = tap_cols.transpose(2, 0, 1)
+    tap_high = tap_cols.astype(jnp.bfloat16)
+    tap_low = (tap_cols - tap_high.astype(jnp.float32)).astype(jnp.bfloat16)
+
+    def with_next_rows(cols):
+        following = jnp.concatenate(
+            [cols[:2, 1:], jnp.zeros((2, 1, group), cols.dtype)], axis=1
+        )
+        return jnp.concatenate([cols, following], axis=0)
+
+    edge_pad = jnp.zeros((2, seq_count, group), jnp.bfloat16)
     returned = swap_layout(
         jnp.concatenate(
             [
-                long_cols.astype(jnp.float32),
-                gated_grad_cols.astype(jnp.float32),
-                tap_cols.transpose(2, 0, 1),
+                with_next_rows(long_cols),
+                with_next_rows(gated_grad_cols),
+                jnp.concatenate([tap_high, edge_pad], axis=0),
+                jnp.concatenate([tap_low, edge_pad], axis=0),
             ],
             axis=2,
         )
     )
-    long_out = returned[..., :group].reshape(row_count, local_width)
-    gated_wide = returned[..., group : 2 * group].reshape(row_count, local_width)
-    tap_grads = returned[..., 2 * group :].reshape(row_count, local_width)
-
-    operator_out = (query_conv * long_out).astype(jnp.bfloat16)
+    wide_rows = row_count + 2
+    long_out = returned[..., :group].reshape(wide_rows, local_width).astype(jnp.float32)
+    gated_wide = returned[..., group : 2 * group].reshape(wide_rows, local_width).astype(jnp.float32)
+    tap_grads = (
+        returned[:row_count, :, 2 * group : 3 * group].astype(jnp.float32)
+        + returned[:row_count, :, 3 * group :].astype(jnp.float32)
+    ).reshape(row_count, local_width)
+
+    operator_out = (query_conv[:row_count] * long_out[:row_count]).astype(jnp.bfloat16)
     grad_query = cot_wide * long_out
-
     grad_streams = jnp.stack(
         [grad_query, gated_wide * value_conv, gated_wide * key_conv], axis=1
-    ).astype(jnp.bfloat16)
-    grad_streams = grad_streams.reshape(row_count, 3 * local_width)
-    after = neighbour_rows(grad_streams[:2], -1)
-    padded = (
-        jnp.concatenate([grad_streams, after], axis=0)
-        .astype(jnp.float32)
-        .reshape(row_count + 2, 3, local_width)
-    )
+    ).astype(jnp.bfloat16).astype(jnp.float32)
     stream_grads = (
-        short_weight[:, 0] * padded[:row_count]
-        + short_weight[:, 1] * padded[1 : row_count + 1]
-        + short_weight[:, 2] * padded[2:]
+        short_weight[:, 0] * grad_streams[:row_count]
+        + short_weight[:, 1] * grad_streams[1 : row_count + 1]
+        + short_weight[:, 2] * grad_streams[2:]
     ).astype(jnp.bfloat16)
     return (operator_out, stream_grads, tap_grads)
 

time: 124 us -> 149 us (1.20)
  the two profiles are of different devices: /device:TPU:2 before, /device:TPU:1 now
where the time goes in v3:
time: 149 us; the launch traced here: 148 us
  blocking collectives  49.5 us (33%)
  local copies, waits for them, and re-layouts  32 us (21%)
  starting transfers between devices  23.6 us (16%)
  other arithmetic  20.8 us (14%)
  matrix products  13.6 us (9%)
  waiting for transfers between devices  6.58 us (4%)
  between operations  1.93 us (1%)
    all_to_all x1, blocking collectives, swap_layout(): return lax.all_to_all(values, 'seq', 1, 1, tiled=True)  25.1 us
    all_gather x1, blocking collectives, on_device(): lax.all_gather(jnp.concatenate([prev_tokens, next_tokens], axis=0), 'chan...  24.5 us
    all_to_all x1, starting transfers between devices, swap_layout(): return lax.all_to_all(values, 'seq', 1, 1, tiled=True)  8.81 us
    all_to_all x1, starting transfers between devices, on_device(): gathered = lax.all_to_all(copies, 'chan', 0, 0, tiled=True)  8.33 us
    mul x15, local copies, waits for them, and re-layouts, spectral_product(): real_out = left_re * right_re - jnp.where(first_row, 0.0, cross_term)  7.97 us
    unnamed x108, local copies, waits for them, and re-layouts  7.19 us
    another operation x4, other arithmetic  6.7 us
    all_to_all x1, waiting for transfers between devices, swap_layout(): return lax.all_to_all(values, 'seq', 1, 1, tiled=True)  6.57 us
  transfers between devices with their start and end apart: 4, of which 1 were waited for; matrix products, arithmetic and copies ran while one was open for 21% of the time, Pallas kernels for 0%

profile of v3, /device:TPU:1, one launch (start us, length us, event | category | flops | bytes accessed | tf_op | source)
XLA Modules:
  0.0 148.0 jit_solution(15012363455423692422)
XLA Ops:
  0.6 0.8 slice.685
  1.5 1.3 fusion.148
  3.4 1.3 collective-permute-start.1
  4.6 5.2 %collective-permute-start = (bf16[2,256]{1,0:T(2,128)(2,1)}, bf16[2,256]{1,0:T(2,128)(2,1)}, u32[]{:S(2)}, u32[]{:S(2)}) collective-permute-start(bf16[2,256]{1,0:T(2,128)(2,1)} %get-tuple-element.172), channel_id=1, source_target_pairs={{0,16},{16,32},{32,48},{48,64},{64,80},{80,96},{96,112},{112,128},... | collective-permute-start | bytes 3080 | tf_op jit(solution)/shard_map/ppermute | solution.py:12
  9.9 2.4 %broadcast_in_dim.730 = bf16[16,256,256]{2,1,0:T(8,128)(2,1)} broadcast(bf16[256,256]{1,0:T(8,128)(2,1)} %param.5), dimensions={1,2} | broadcast | bytes 2228224 | tf_op jit(solution)/shard_map/broadcast_in_dim | solution.py:90
  12.3 8.3 %all-to-all-start = ((bf16[16,256,256]{2,1,0:T(8,128)(2,1)}), bf16[16,256,256]{2,1,0:T(8,128)(2,1)}, u32[]{:S(2)}, u32[]{:S(2)}) async-start(bf16[16,256,256]{2,1,0:T(8,128)(2,1)} %broadcast_in_dim.730), calls=%async_computation | async-start | bytes 4194304 | tf_op jit(solution)/shard_map/all_to_all | solution.py:91
  20.7 1.3 constant_dynamic-slice_fusion
  23.5 2.2 %copy.26 = bf16[15,256,16]{1,2,0:T(8,128)(2,1)} copy(bf16[15,256,16]{2,1,0:T(8,128)(2,1)} %bitcast.176) | data formatting | bytes 245760 | tf_op jit(solution)/shard_map/slice | solution.py:125
  25.7 1.0 copy.28
  26.7 2.1 %negate_select_fusion.2 = (f32[256,512]{1,0:T(8,128)S(1)}, f32[256,512]{1,0:T(8,128)S(1)}) fusion(f32[512]{0:T(512)S(1)} %fusion.97, pred[256]{0:T(512)(128)(4,1)S(1)} %iota_compare_fusion.38), kind=kLoop, calls=%fused_computation.149 | loop fusion | flops 2097152 | bytes 1050880 | tf_op jit(solution)/shard_map/jit(_where)/select_n | solution.py:23
  39.4 1.3 slice_bitcast_fusion.34
  41.3 24.5 %all-gather.1 = bf16[16,4,256]{2,1,0:T(4,128)(2,1)S(1)} all-gather(bf16[1,4,256]{2,1,0:T(4,128)(2,1)S(1)} %maximum_bitcast_fusion.3), channel_id=2, replica_groups=mesh['seq'=16,'chan'=16] {'chan'}, dimensions={0}, use_global_device_ids=true | all-gather | bytes 34816 | tf_op jit(solution)/shard_map/all_gather | solution.py:87
  65.8 3.7 %fusion.18 = bf16[4,3,256]{2,0,1:T(4,128)(2,1)S(1)} fusion(bf16[16,256,3,256]{3,1,0,2:T(8,128)(2,1)} %bitcast.173, bf16[16,4,256]{2,1,0:T(4,128)(2,1)S(1)} %all-gather.1), kind=kOutput, calls=%fused_computation.27 | convolution fusion | flops 25168896 | bytes 6330368 | tf_op jit(solution)/shard_map/stf,sfqc->tqc/dot_general | solution.py:96
  69.5 5.2 %fusion.15 = bf16[256,3,256]{2,0,1:T(8,128)(2,1)S(1)} fusion(bf16[16,256,3,256]{3,1,0,2:T(8,128)(2,1)} %bitcast.174, bf16[16,256,256]{2,1,0:T(8,128)(2,1)} %all-to-all-done), kind=kOutput, calls=%fused_computation.20 | convolution fusion | flops 1610809344 | bytes 8781824 | tf_op jit(solution)/shard_map/stf,sfqc->tqc/dot_general | solution.py:93
  77.1 1.7 %copy.30 = bf16[256,256]{0,1:T(8,128)(2,1)} copy(bf16[256,256]{1,0:T(8,128)(2,1)} %multiply_convert_fusion.2) | data formatting | bytes 262144 | tf_op jit(solution)/shard_map/convert_element_type | solution.py:110
  78.8 1.7 %copy.29 = bf16[256,1,256]{0,2,1:T(8,128)(2,1)} copy(bf16[256,1,256]{2,0,1:T(8,128)(2,1)} %fusion.80) | data formatting | bytes 262144 | tf_op jit(solution)/shard_map/convert_element_type | solution.py:108
  80.5 1.7 %pad_maximum_fusion.2 = bf16[256,16,32]{0,2,1:T(8,128)(2,1)} fusion(bf16[256,16,16]{0,2,1:T(8,128)(2,1)} %bitcast.181, bf16[256,16,16]{0,2,1:T(8,128)(2,1)} %bitcast.182), kind=kLoop, calls=%fused_computation.185 | loop fusion | flops 524288 | bytes 524288 | tf_op jit(solution)/shard_map/concatenate | solution.py:113
  82.1 8.8 %all-to-all-start.1 = ((bf16[256,16,32]{0,2,1:T(8,128)(2,1)}), bf16[256,16,32]{0,2,1:T(8,128)(2,1)}, u32[]{:S(2)}, u32[]{:S(2)}) async-start(bf16[256,16,32]{0,2,1:T(8,128)(2,1)} %pad_maximum_fusion.2), calls=%async_computation.1 | async-start | bytes 524288 | tf_op jit(solution)/shard_map/all_to_all | solution.py:70
  91.0 2.4 %select_convert_fusion = bf16[256,256]{1,0:T(8,128)(2,1)} fusion(bf16[256]{0:T(256)(128)(2,1)S(1)} %fusion.134, s32[256]{0:T(256)} %iota_add_fusion, pred[256]{0:T(512)(128)(4,1)S(1)} %iota_compare_fusion.38), kind=kLoop, calls=%fused_computation.198 | loop fusion | flops 1048576 | bytes 132864 | tf_op jit(solution)/shard_map/convert.9
  93.4 2.4 %multiply_convert_fusion.3 = bf16[256,256]{1,0:T(8,128)(2,1)} fusion(f32[256]{0:T(256)} %select_multiply_fusion, s32[256]{0:T(256)} %iota_add_fusion), kind=kLoop, calls=%fused_computation.199 | loop fusion | flops 1048576 | bytes 133120 | tf_op jit(solution)/shard_map/convert.8
  95.7 6.6 %all-to-all-done.1 = bf16[256,16,32]{0,2,1:T(8,128)(2,1)} async-done(((bf16[256,16,32]{0,2,1:T(8,128)(2,1)}), bf16[256,16,32]{0,2,1:T(8,128)(2,1)}, u32[]{:S(2)}, u32[]{:S(2)}) %all-to-all-start.1) | async-done | bytes 262176 | tf_op jit(solution)/shard_map/all_to_all | solution.py:70
  102.3 1.3 fusion.151
  103.8 1.1 fusion.152
  111.9 1.0 fusion.19
  114.1 25.1 %all_to_all.15 = bf16[258,16,64]{0,2,1:T(8,128)(2,1)S(1)} all-to-all(bf16[258,16,64]{0,2,1:T(8,128)(2,1)S(1)} %fusion.25), channel_id=1, replica_groups=mesh['seq'=16,'chan'=16] {'seq'}, dimensions={1} | all-to-all | bytes 1056768 | tf_op jit(solution)/shard_map/all_to_all | solution.py:70
  139.2 0.9 copy-done.3
  141.0 1.1 fusion.147
  142.1 0.8 copy.33
  142.9 1.0 fusion.73
  144.2 0.9 multiply_convert_fusion
  145.2 1.0 fusion.30
  146.2 1.0 convert_add_fusion
  (220 shorter events, 25.0 us)
Async XLA Ops:
  0.6 20.0 %copy-start = (bf16[4096,256]{1,0:T(8,128)(2,1)S(1)}, bf16[4096,256]{1,0:T(8,128)(2,1)}, u32[]{:S(2)}) copy-start(bf16[4096,256]{1,0:T(8,128)(2,1)} %param.8) | copy-start | bytes 6291460
  3.4 36.0 %collective-permute-start.1 = (bf16[2,512]{1,0:T(2,128)(2,1)}, bf16[2,512]{1,0:T(2,128)(2,1)}, u32[]{:S(2)}, u32[]{:S(2)}) collective-permute-start(bf16[2,512]{1,0:T(2,128)(2,1)} %pad_maximum_fusion.3), channel_id=1, source_target_pairs={{16,0},{32,16},{48,32},{64,48},{80,64},{96,80},{112,96},{128,112},... | collective-permute-start | bytes 6152 | tf_op jit(solution)/shard_map/ppermute | solution.py:12
  4.6 36.0 %collective-permute-start = (bf16[2,256]{1,0:T(2,128)(2,1)}, bf16[2,256]{1,0:T(2,128)(2,1)}, u32[]{:S(2)}, u32[]{:S(2)}) collective-permute-start(bf16[2,256]{1,0:T(2,128)(2,1)} %get-tuple-element.172), channel_id=1, source_target_pairs={{0,16},{16,32},{32,48},{48,64},{64,80},{80,96},{96,112},{112,128},... | collective-permute-start | bytes 3080 | tf_op jit(solution)/shard_map/ppermute | solution.py:12
  12.3 57.2 %all-to-all-start = ((bf16[16,256,256]{2,1,0:T(8,128)(2,1)}), bf16[16,256,256]{2,1,0:T(8,128)(2,1)}, u32[]{:S(2)}, u32[]{:S(2)}) async-start(bf16[16,256,256]{2,1,0:T(8,128)(2,1)} %broadcast_in_dim.730), calls=%async_computation | async-start | bytes 4194304 | tf_op jit(solution)/shard_map/all_to_all | solution.py:91
  20.7 2.3 %copy-start.43 = (f32[3,3,256]{2,1,0:T(4,128)S(1)}, f32[3,3,256]{2,1,0:T(4,128)}, u32[]{:S(2)}) copy-start(f32[3,3,256]{2,1,0:T(4,128)} %param.7) | copy-start | bytes 27652
  26.7 2.2 %copy-start.9 = (bf16[16,256,16]{1,2,0:T(8,128)(2,1)S(1)}, bf16[16,256,16]{1,2,0:T(8,128)(2,1)}, u32[]{:S(2)}) copy-start(bf16[16,256,16]{1,2,0:T(8,128)(2,1)} %copy.28) | copy-start | bytes 393220
  26.7 2.2 %copy-start.10 = (bf16[15,256,16]{1,2,0:T(8,128)(2,1)S(1)}, bf16[15,256,16]{1,2,0:T(8,128)(2,1)}, u32[]{:S(2)}) copy-start(bf16[15,256,16]{1,2,0:T(8,128)(2,1)} %copy.26) | copy-start | bytes 368644
  28.8 0.8 copy-start.1
  28.9 8.1 %copy-start.4 = (bf16[512,512]{1,0:T(8,128)(2,1)}, bf16[512,512]{1,0:T(8,128)(2,1)S(1)}, u32[]{:S(2)}) copy-start(bf16[512,512]{1,0:T(8,128)(2,1)S(1)} %fusion.21) | copy-start | bytes 1572868
  28.9 6.9 %copy-start.41 = (f32[3,1,256]{2,1,0:T(1,128)S(1)}, f32[3,1,256]{2,1,0:T(1,128)}, u32[]{:S(2)}) copy-start(f32[3,1,256]{2,1,0:T(1,128)} %get-tuple-element.225) | copy-start | bytes 9220
  28.9 6.8 %copy-start.42 = (f32[3,1,256]{2,1,0:T(1,128)S(1)}, f32[3,1,256]{2,1,0:T(1,128)}, u32[]{:S(2)}) copy-start(f32[3,1,256]{2,1,0:T(1,128)} %get-tuple-element.226) | copy-start | bytes 9220
  29.0 9.8 %copy-start.40 = (f32[3,1,256]{2,1,0:T(1,128)S(1)}, f32[3,1,256]{2,1,0:T(1,128)}, u32[]{:S(2)}) copy-start(f32[3,1,256]{2,1,0:T(1,128)} %get-tuple-element.224) | copy-start | bytes 9220
  69.5 5.3 %copy-start.36 = (f32[3,256]{1,0:T(4,128)S(1)}, f32[3,256]{1,0:T(4,128)}, u32[]{:S(2)}) copy-start(f32[3,256]{1,0:T(4,128)} %get-tuple-element.238) | copy-start | bytes 9220
  69.5 5.3 %copy-start.38 = (f32[3,1,256]{2,0,1:T(4,128)S(1)}, f32[3,1,256]{2,0,1:T(4,128)}, u32[]{:S(2)}) copy-start(f32[3,1,256]{2,0,1:T(4,128)} %copy.48) | copy-start | bytes 9220
  74.8 0.9 copy-start.6
  82.1 20.2 %all-to-all-start.1 = ((bf16[256,16,32]{0,2,1:T(8,128)(2,1)}), bf16[256,16,32]{0,2,1:T(8,128)(2,1)}, u32[]{:S(2)}, u32[]{:S(2)}) async-start(bf16[256,16,32]{0,2,1:T(8,128)(2,1)} %pad_maximum_fusion.2), calls=%async_computation.1 | async-start | bytes 524288 | tf_op jit(solution)/shard_map/all_to_all | solution.py:70
  102.3 1.4 copy-start.7
  102.3 1.4 copy-start.8
  106.5 0.7 copy-start.22
  106.5 0.7 copy-start.23
  107.5 0.7 copy-start.18
  107.5 0.7 copy-start.19
  110.4 0.8 copy-start.30
  110.4 0.8 copy-start.31
  110.5 0.8 copy-start.28
  110.5 0.8 copy-start.29
  110.9 1.0 copy-start.2
  111.9 1.2 copy-start.5
  139.2 0.9 copy-start.3
  142.1 2.1 %copy-start.44 = (bf16[2,1,256]{2,0,1:T(2,128)(2,1)S(1)}, bf16[2,1,256]{2,0,1:T(2,128)(2,1)}, u32[]{:S(2)}) copy-start(bf16[2,1,256]{2,0,1:T(2,128)(2,1)} %get-tuple-element.229) | copy-start | bytes 3076
  143.9 1.2 copy-start.37
  144.0 1.2 copy-start.39
  (17 other events, 12.3 us)

commit v4 on v2

--- a/solution.py
+++ b/solution.py
@@ -80,11 +80,24 @@
     half_table = full_table[:, :row_count]
     back_table = inverse.astype(jnp.bfloat16)
     chan_count = lax.axis_size("chan")
-    copies = jnp.broadcast_to(tokens[None], (chan_count,) + tokens.shape)
+    split_rows = row_count // 2
+    offloaded = lax.all_gather(tokens[:split_rows], "chan", axis=1, tiled=True)
+    copies = jnp.broadcast_to(tokens[None, split_rows:], (chan_count, row_count - split_rows, local_width))
     gathered = lax.all_to_all(copies, "chan", 0, 0, tiled=True)
     weight_parts = in_weight.reshape(chan_count, local_width, 3, local_width)
-    streams = jnp.einsum(
-        "stf,sfqc->tqc", gathered, weight_parts, preferred_element_type=jnp.float32
+    streams = jnp.concatenate(
+        [
+            jnp.einsum(
+                "tsf,sfqc->tqc",
+                offloaded.reshape(split_rows, chan_count, local_width),
+                weight_parts,
+                preferred_element_type=jnp.float32,
+            ),
+            jnp.einsum(
+                "stf,sfqc->tqc", gathered, weight_parts, preferred_element_type=jnp.float32
+            ),
+        ],
+        axis=0,
     ).astype(jnp.bfloat16)
     streams = streams.reshape(row_count, 3 * local_width)
     before = neighbour_rows(streams[row_count - 2 :], 1)

time: 124 us -> 160 us (1.29)
  waiting for transfers between devices: 21.1 us -> 40.4 us
  between operations: 1.88 us -> 15.2 us
  starting transfers between devices: 24.4 us -> 18.6 us
  local copies, waits for them, and re-layouts: 26.6 us -> 30.5 us
  matrix products: 9.97 us -> 12.9 us
  blocking collectives: 24 us -> 25.6 us
    all_gather x0 -> x1, waiting for transfers between devices: none -> 28.4 us  [on_device(): offloaded = lax.all_gather(tokens[:split_rows], 'chan', axis=1, tiled=True)]
    all_to_all x1, waiting for transfers between devices: 10.7 us -> 0.01 us  [on_device(): gathered = lax.all_to_all(copies, 'chan', 0, 0, tiled=True)]
    all_to_all x1, starting transfers between devices: 12.4 us -> 7.2 us  [swap_layout(): return lax.all_to_all(values, 'seq', 1, 1, tiled=True)]
    unnamed x107 -> x110, local copies, waits for them, and re-layouts: 5.97 us -> 11 us
    dot_general x0 -> x1, matrix products: none -> 4.17 us  [on_device(): jnp.einsum('tsf,sfqc->tqc', offloaded.reshape(split_rows, chan_count, loc...]
    all_to_all x1, blocking collectives: 24 us -> 25.6 us  [swap_layout(): return lax.all_to_all(values, 'seq', 1, 1, tiled=True)]
  transfers between devices with their start and end apart: 4 -> 5, of which waited for: 3 -> 4; matrix products, arithmetic and copies ran while one was open for 21% -> 20% of each run, Pallas kernels for 0% -> 0%
where the time goes in v4:
time: 160 us; the launch traced here: 158 us
  waiting for transfers between devices  40.4 us (25%)
  local copies, waits for them, and re-layouts  30.5 us (19%)
  blocking collectives  25.6 us (16%)
  starting transfers between devices  18.6 us (12%)
  between operations  15.2 us (10%)
  other arithmetic  15.1 us (9%)
  matrix products  12.9 us (8%)
    all_gather x1, waiting for transfers between devices, on_device(): offloaded = lax.all_gather(tokens[:split_rows], 'chan', axis=1, tiled=True)  28.4 us
    all_to_all x1, blocking collectives, swap_layout(): return lax.all_to_all(values, 'seq', 1, 1, tiled=True)  25.6 us
    unnamed x110, local copies, waits for them, and re-layouts  11 us
    mul x15, local copies, waits for them, and re-layouts, spectral_product(): real_out = left_re * right_re - jnp.where(first_row, 0.0, cross_term)  9.1 us
    all_to_all x1, waiting for transfers between devices, swap_layout(): return lax.all_to_all(values, 'seq', 1, 1, tiled=True)  7.58 us
    all_to_all x1, starting transfers between devices, on_device(): gathered = lax.all_to_all(copies, 'chan', 0, 0, tiled=True)  7.48 us
    all_to_all x1, starting transfers between devices, swap_layout(): return lax.all_to_all(values, 'seq', 1, 1, tiled=True)  7.2 us
    another operation x2, other arithmetic  4.8 us
  transfers between devices with their start and end apart: 5, of which 4 were waited for; matrix products, arithmetic and copies ran while one was open for 20% of the time, Pallas kernels for 0%

profile of v4, /device:TPU:2, one launch (start us, length us, event | category | flops | bytes accessed | tf_op | source)
XLA Modules:
  0.0 158.3 jit_solution(13015088894688641314)
XLA Ops:
  7.2 1.0 fusion.123
  8.2 1.1 broadcast_in_dim.729
  9.3 7.5 %all-to-all-start = ((bf16[16,128,256]{2,1,0:T(8,128)(2,1)}), bf16[16,128,256]{2,1,0:T(8,128)(2,1)}, u32[]{:S(2)}, u32[]{:S(2)}) async-start(bf16[16,128,256]{2,1,0:T(8,128)(2,1)} %broadcast_in_dim.729), calls=%async_computation | async-start | bytes 2097152 | tf_op jit(solution)/shard_map/all_to_all | solution.py:86
  16.8 0.7 copy.51
  17.6 1.3 constant_dynamic-slice_fusion
  20.2 2.2 %copy.33 = bf16[15,256,16]{1,2,0:T(8,128)(2,1)} copy(bf16[15,256,16]{2,1,0:T(8,128)(2,1)} %bitcast.174) | data formatting | bytes 245760 | tf_op jit(solution)/shard_map/slice | solution.py:132
  22.4 1.0 copy.35
  23.4 2.1 %negate_select_fusion.2 = (f32[256,512]{1,0:T(8,128)S(1)}, f32[256,512]{1,0:T(8,128)S(1)}) fusion(f32[512]{0:T(512)S(1)} %fusion.71, pred[256]{0:T(512)(128)(4,1)S(1)} %iota_compare_fusion.31), kind=kLoop, calls=%fused_computation.123 | loop fusion | flops 2097152 | bytes 1050880 | tf_op jit(solution)/shard_map/jit(_where)/select_n | solution.py:23
  26.3 0.7 slice_convert_fusion.45
  36.0 0.6 slice_bitcast_fusion.5
  36.7 4.1 %fusion = bf16[128,3,256]{2,0,1:T(8,128)(2,1)S(1)} fusion(bf16[16,256,3,256]{3,1,0,2:T(8,128)(2,1)} %bitcast.171, bf16[16,128,256]{2,1,0:T(8,128)(2,1)} %all-to-all-done), kind=kOutput, calls=%fused_computation.5 | convolution fusion | flops 805404672 | bytes 7536640 | tf_op jit(solution)/shard_map/stf,sfqc->tqc/dot_general | solution.py:96
  40.8 2.6 %collective-permute-start = (bf16[2,768]{1,0:T(2,128)(2,1)S(1)}, bf16[2,768]{1,0:T(2,128)(2,1)S(1)}, u32[]{:S(2)}, u32[]{:S(2)}) collective-permute-start(bf16[2,768]{1,0:T(2,128)(2,1)S(1)} %bitcast.191), channel_id=1, source_target_pairs={{0,16},{16,32},{32,48},{48,64},{64,80},{80,96},{96,112},{112,128},... | collective-permute-start | bytes 9224 | tf_op jit(solution)/shard_map/ppermute | solution.py:12
  44.9 28.4 %all-gather.2.cloned.1.call-done = bf16[128,4096]{0,1:T(8,128)(2,1)} async-done(((bf16[128,256]{0,1:T(8,128)(2,1)}), bf16[128,4096]{0,1:T(8,128)(2,1)}) %all-gather.2.cloned.1.call-update) | async-done | bytes 1048592 | tf_op jit(solution)/shard_map/all_gather | solution.py:84
  73.3 4.2 %fusion.1 = bf16[128,3,256]{2,0,1:T(8,128)(2,1)S(1)} fusion(bf16[128,16,256,1]{0,2,1,3:T(8,128)(2,1)} %bitcast.182, bf16[16,256,3,256]{3,1,0,2:T(8,128)(2,1)} %bitcast.172), kind=kOutput, calls=%fused_computation.6 | convolution fusion | flops 805404672 | bytes 7536640 | tf_op jit(solution)/shard_map/tsf,sfqc->tqc/dot_general | solution.py:90
  78.8 0.7 pad_maximum_fusion.3
  79.6 7.2 %all-to-all-start.1 = ((bf16[256,16,32]{0,2,1:T(8,128)(2,1)}), bf16[256,16,32]{0,2,1:T(8,128)(2,1)}, u32[]{:S(2)}, u32[]{:S(2)}) async-start(bf16[256,16,32]{0,2,1:T(8,128)(2,1)} %pad_maximum_fusion.3), calls=%async_computation.1 | async-start | bytes 524288 | tf_op jit(solution)/shard_map/all_to_all | solution.py:70
  86.8 2.4 %select_convert_fusion = bf16[256,256]{1,0:T(8,128)(2,1)} fusion(bf16[256]{0:T(256)(128)(2,1)S(1)} %fusion.108, s32[256]{0:T(256)} %iota_add_fusion, pred[256]{0:T(512)(128)(4,1)S(1)} %iota_compare_fusion.31), kind=kLoop, calls=%fused_computation.168 | loop fusion | flops 1048576 | bytes 132864 | tf_op jit(solution)/shard_map/convert.1
  89.2 2.4 %multiply_convert_fusion.1 = bf16[256,256]{1,0:T(8,128)(2,1)} fusion(f32[256]{0:T(256)} %select_multiply_fusion, s32[256]{0:T(256)} %iota_add_fusion), kind=kLoop, calls=%fused_computation.169 | loop fusion | flops 1048576 | bytes 133120 | tf_op jit(solution)/shard_map/convert
  91.6 7.6 %all-to-all-done.1 = bf16[256,16,32]{0,2,1:T(8,128)(2,1)} async-done(((bf16[256,16,32]{0,2,1:T(8,128)(2,1)}), bf16[256,16,32]{0,2,1:T(8,128)(2,1)}, u32[]{:S(2)}, u32[]{:S(2)}) %all-to-all-start.1) | async-done | bytes 262176 | tf_op jit(solution)/shard_map/all_to_all | solution.py:70
  99.2 1.3 fusion.125
  100.6 1.1 fusion.126
  110.5 1.0 fusion.4
  111.7 0.9 copy-done.4
  113.5 25.6 %all_to_all.15 = f32[256,16,48]{0,2,1:T(8,128)S(1)} all-to-all(f32[256,16,48]{0,2,1:T(8,128)S(1)} %pad_maximum_fusion.2), channel_id=1, replica_groups=mesh['seq'=16,'chan'=16] {'seq'}, dimensions={1} | all-to-all | bytes 1572864 | tf_op jit(solution)/shard_map/all_to_all | solution.py:70
  139.1 0.8 fusion.122
  140.1 0.7 slice.991
  140.8 1.3 collective-permute-start.1
  142.1 0.8 copy.37
  142.9 1.8 %copy.39 = f32[256,256]{1,0:T(8,128)} copy(f32[256,256]{0,1:T(8,128)} %bitcast.183) | data formatting | bytes 524288
  144.6 4.0 %collective-permute-done.1 = bf16[2,768]{0,1:T(8,128)(2,1)} collective-permute-done((bf16[2,768]{0,1:T(8,128)(2,1)}, bf16[2,768]{0,1:T(8,128)(2,1)}, u32[]{:S(2)}, u32[]{:S(2)}) %collective-permute-start.1) | collective-permute-done | bytes 3104 | tf_op jit(solution)/shard_map/ppermute | solution.py:12
  148.6 1.0 maximum_convert_fusion.2
  150.5 0.9 copy.38
  (215 shorter events, 24.1 us)
Async XLA Ops:
  7.2 10.4 %copy-start = (bf16[4096,256]{1,0:T(8,128)(2,1)S(1)}, bf16[4096,256]{1,0:T(8,128)(2,1)}, u32[]{:S(2)}) copy-start(bf16[4096,256]{1,0:T(8,128)(2,1)} %param.8) | copy-start | bytes 6291460
  9.3 27.4 %all-to-all-start = ((bf16[16,128,256]{2,1,0:T(8,128)(2,1)}), bf16[16,128,256]{2,1,0:T(8,128)(2,1)}, u32[]{:S(2)}, u32[]{:S(2)}) async-start(bf16[16,128,256]{2,1,0:T(8,128)(2,1)} %broadcast_in_dim.729), calls=%async_computation | async-start | bytes 2097152 | tf_op jit(solution)/shard_map/all_to_all | solution.py:86
  16.8 56.5 %all-gather.2.cloned.1.call-start = ((), (), s32[]{:S(2)}) async-start(), calls=%async_computation.3 | async-start | bytes 1114112 | tf_op jit(solution)/shard_map/all_gather | solution.py:84
  23.3 2.2 %copy-start.7 = (bf16[16,256,16]{1,2,0:T(8,128)(2,1)S(1)}, bf16[16,256,16]{1,2,0:T(8,128)(2,1)}, u32[]{:S(2)}) copy-start(bf16[16,256,16]{1,2,0:T(8,128)(2,1)} %copy.35) | copy-start | bytes 393220
  23.3 2.2 %copy-start.10 = (bf16[15,256,16]{1,2,0:T(8,128)(2,1)S(1)}, bf16[15,256,16]{1,2,0:T(8,128)(2,1)}, u32[]{:S(2)}) copy-start(bf16[15,256,16]{1,2,0:T(8,128)(2,1)} %copy.33) | copy-start | bytes 368644
  25.5 0.8 copy-start.1
  25.6 2.6 %copy-start.3 = (bf16[512,512]{1,0:T(8,128)(2,1)}, bf16[512,512]{1,0:T(8,128)(2,1)S(1)}, u32[]{:S(2)}) copy-start(bf16[512,512]{1,0:T(8,128)(2,1)S(1)} %fusion.7) | copy-start | bytes 1572868
  25.6 7.4 %copy-start.42 = (f32[3,1,256]{2,1,0:T(1,128)S(1)}, f32[3,1,256]{2,1,0:T(1,128)}, u32[]{:S(2)}) copy-start(f32[3,1,256]{2,1,0:T(1,128)} %get-tuple-element.231) | copy-start | bytes 9220
  36.6 7.4 %copy-start.9 = (bf16[256,256]{1,0:T(8,128)(2,1)S(1)}, bf16[256,256]{1,0:T(8,128)(2,1)}, u32[]{:S(2)}) copy-start(bf16[256,256]{1,0:T(8,128)(2,1)} %param.9) | copy-start | bytes 393220
  36.6 7.5 %copy-start.41 = (f32[3,1,256]{2,1,0:T(1,128)S(1)}, f32[3,1,256]{2,1,0:T(1,128)}, u32[]{:S(2)}) copy-start(f32[3,1,256]{2,1,0:T(1,128)} %get-tuple-element.229) | copy-start | bytes 9220
  40.8 3.9 %collective-permute-start = (bf16[2,768]{1,0:T(2,128)(2,1)S(1)}, bf16[2,768]{1,0:T(2,128)(2,1)S(1)}, u32[]{:S(2)}, u32[]{:S(2)}) collective-permute-start(bf16[2,768]{1,0:T(2,128)(2,1)S(1)} %bitcast.191), channel_id=1, source_target_pairs={{0,16},{16,32},{32,48},{48,64},{64,80},{80,96},{96,112},{112,128},... | collective-permute-start | bytes 9224 | tf_op jit(solution)/shard_map/ppermute | solution.py:12
  79.6 19.6 %all-to-all-start.1 = ((bf16[256,16,32]{0,2,1:T(8,128)(2,1)}), bf16[256,16,32]{0,2,1:T(8,128)(2,1)}, u32[]{:S(2)}, u32[]{:S(2)}) async-start(bf16[256,16,32]{0,2,1:T(8,128)(2,1)} %pad_maximum_fusion.3), calls=%async_computation.1 | async-start | bytes 524288 | tf_op jit(solution)/shard_map/all_to_all | solution.py:70
  99.2 1.4 copy-start.5
  99.2 1.4 copy-start.6
  103.1 0.7 copy-start.30
  103.8 0.7 copy-start.28
  104.6 0.7 copy-start.26
  105.3 0.7 copy-start.24
  106.0 0.7 copy-start.22
  106.3 0.8 copy-start.19
  106.3 0.8 copy-start.20
  107.2 0.7 copy-start.15
  107.2 0.7 copy-start.16
  108.6 0.7 copy-start.40
  108.8 0.7 copy-start.38
  108.9 0.7 copy-start.35
  108.9 0.7 copy-start.36
  109.3 0.7 copy-start.34
  109.5 1.0 copy-start.2
  110.5 1.1 copy-start.8
  111.6 1.0 copy-start.4
  140.8 7.9 %collective-permute-start.1 = (bf16[2,768]{0,1:T(8,128)(2,1)}, bf16[2,768]{0,1:T(8,128)(2,1)}, u32[]{:S(2)}, u32[]{:S(2)}) collective-permute-start(bf16[2,768]{0,1:T(8,128)(2,1)} %bitcast.73), channel_id=1, source_target_pairs={{16,0},{32,16},{48,32},{64,48},{80,64},{96,80},{112,96},{128,112},... | collective-permute-start | bytes 9224 | tf_op jit(solution)/shard_map/ppermute | solution.py:12
  (17 other events, 12.2 us)
Sparse Core Ops, SparseCore 0:
  20.9 52.3 all-gather.1

commit v5 on v3

--- a/solution.py
+++ b/solution.py
@@ -81,23 +81,20 @@
     half_table = full_table[:, :row_count]
     back_table = inverse.astype(jnp.bfloat16)
 
-    prev_tokens = neighbour_rows(tokens[row_count - 2 :], 1)
-    next_rows = neighbour_rows(jnp.concatenate([tokens[:2], cotangent[:2]], axis=1), -1)
-    next_tokens, next_cot = (next_rows[:, :local_width], next_rows[:, local_width:])
-    edge_tokens = lax.all_gather(
-        jnp.concatenate([prev_tokens, next_tokens], axis=0), "chan", axis=0, tiled=False
-    )
     copies = jnp.broadcast_to(tokens[None], (chan_count,) + tokens.shape)
     gathered = lax.all_to_all(copies, "chan", 0, 0, tiled=True)
     weight_parts = in_weight.reshape(chan_count, local_width, 3, local_width)
     streams = jnp.einsum(
         "stf,sfqc->tqc", gathered, weight_parts, preferred_element_type=jnp.float32
     ).astype(jnp.bfloat16)
-    edge_streams = jnp.einsum(
-        "stf,sfqc->tqc", edge_tokens, weight_parts, preferred_element_type=jnp.float32
-    ).astype(jnp.bfloat16)
-    extended = jnp.concatenate([edge_streams[:2], streams, edge_streams[2:]], axis=0).astype(
-        jnp.float32
+    streams = streams.reshape(row_count, 3 * local_width)
+    before = neighbour_rows(streams[row_count - 2 :], 1)
+    after = neighbour_rows(jnp.concatenate([streams[:2], cotangent[:2]], axis=1), -1)
+    next_streams, next_cot = (after[:, : 3 * local_width], after[:, 3 * local_width :])
+    extended = (
+        jnp.concatenate([before, streams, next_streams], axis=0)
+        .astype(jnp.float32)
+        .reshape(row_count + 4, 3, local_width)
     )
     conv_out = (
         short_weight[:, 0] * extended[2:]
@@ -160,9 +157,7 @@
     tap_cols = tap_spec[:, :, row_count:] + jnp.concatenate(
         [tap_spec[1:, :, :row_count], jnp.zeros((1, group, row_count), jnp.float32)], axis=0
     )
-    tap_cols = tap_cols.transpose(2, 0, 1)
-    tap_high = tap_cols.astype(jnp.bfloat16)
-    tap_low = (tap_cols - tap_high.astype(jnp.float32)).astype(jnp.bfloat16)
+    tap_cols = tap_cols.transpose(2, 0, 1).astype(jnp.bfloat16)
 
     def with_next_rows(cols):
         following = jnp.concatenate(
@@ -170,14 +165,12 @@
         )
         return jnp.concatenate([cols, following], axis=0)
 
-    edge_pad = jnp.zeros((2, seq_count, group), jnp.bfloat16)
     returned = swap_layout(
         jnp.concatenate(
             [
                 with_next_rows(long_cols),
                 with_next_rows(gated_grad_cols),
-                jnp.concatenate([tap_high, edge_pad], axis=0),
-                jnp.concatenate([tap_low, edge_pad], axis=0),
+                jnp.concatenate([tap_cols, jnp.zeros((2, seq_count, group), jnp.bfloat16)], axis=0),
             ],
             axis=2,
         )
@@ -185,10 +178,7 @@
     wide_rows = row_count + 2
     long_out = returned[..., :group].reshape(wide_rows, local_width).astype(jnp.float32)
     gated_wide = returned[..., group : 2 * group].reshape(wide_rows, local_width).astype(jnp.float32)
-    tap_grads = (
-        returned[:row_count, :, 2 * group : 3 * group].astype(jnp.float32)
-        + returned[:row_count, :, 3 * group :].astype(jnp.float32)
-    ).reshape(row_count, local_width)
+    tap_grads = returned[:row_count, :, 2 * group :].astype(jnp.float32).reshape(row_count, local_width)
 
     operator_out = (query_conv[:row_count] * long_out[:row_count]).astype(jnp.bfloat16)
     grad_query = cot_wide * long_out

time: 149 us -> 137 us (0.919)
  the two profiles are of different devices: /device:TPU:1 before, /device:TPU:2 now
where the time goes in v5:
time: 137 us; the launch traced here: 135 us
  local copies, waits for them, and re-layouts  37.8 us (28%)
  waiting for transfers between devices  36.2 us (26%)
  starting transfers between devices  28.1 us (21%)
  other arithmetic  21.5 us (16%)
  matrix products  9.8 us (7%)
  between operations  1.79 us (1%)
    all_to_all x2, waiting for transfers between devices, swap_layout(): return lax.all_to_all(values, 'seq', 1, 1, tiled=True)  22.7 us
    all_to_all x2, starting transfers between devices, swap_layout(): return lax.all_to_all(values, 'seq', 1, 1, tiled=True)  14.8 us
    all_to_all x1, waiting for transfers between devices, on_device(): gathered = lax.all_to_all(copies, 'chan', 0, 0, tiled=True)  12.9 us
    mul x15, local copies, waits for them, and re-layouts, spectral_product(): real_out = left_re * right_re - jnp.where(first_row, 0.0, cross_term)  8 us
    all_to_all x1, starting transfers between devices, on_device(): gathered = lax.all_to_all(copies, 'chan', 0, 0, tiled=True)  7.48 us
    unnamed x110, local copies, waits for them, and re-layouts  6.5 us
    ppermute x2, starting transfers between devices, passed_along(): return lax.ppermute(block, axis, route)  5.84 us
    another operation x4, other arithmetic  5.38 us
  transfers between devices with their start and end apart: 5, of which 4 were waited for; matrix products, arithmetic and copies ran while one was open for 15% of the time, Pallas kernels for 0%

profile of v5, /device:TPU:2, one launch (start us, length us, event | category | flops | bytes accessed | tf_op | source)
XLA Modules:
  0.0 135.2 jit_solution(15341562047494144762)
XLA Ops:
  0.6 2.6 %broadcast_in_dim.730 = bf16[16,256,256]{2,1,0:T(8,128)(2,1)} broadcast(bf16[256,256]{1,0:T(8,128)(2,1)} %param.5), dimensions={1,2} | broadcast | bytes 2228224 | tf_op jit(solution)/shard_map/broadcast_in_dim | solution.py:84
  3.3 7.5 %all-to-all-start = ((bf16[16,256,256]{2,1,0:T(8,128)(2,1)}), bf16[16,256,256]{2,1,0:T(8,128)(2,1)}, u32[]{:S(2)}, u32[]{:S(2)}) async-start(bf16[16,256,256]{2,1,0:T(8,128)(2,1)} %broadcast_in_dim.730), calls=%async_computation | async-start | bytes 4194304 | tf_op jit(solution)/shard_map/all_to_all | solution.py:85
  10.8 1.3 constant_dynamic-slice_fusion
  12.8 1.5 %copy.103 = bf16[15,256,16]{1,2,0:T(8,128)(2,1)S(1)} copy(bf16[15,256,16]{2,1,0:T(8,128)(2,1)} %bitcast.169) | data formatting | bytes 245760 | tf_op jit(solution)/shard_map/slice | solution.py:122
  14.6 2.1 %negate_select_fusion.2 = (f32[256,512]{1,0:T(8,128)S(1)}, f32[256,512]{1,0:T(8,128)S(1)}) fusion(f32[512]{0:T(512)S(1)} %fusion.90, pred[256]{0:T(512)(128)(4,1)S(1)} %iota_compare_fusion.36), kind=kLoop, calls=%fused_computation.139 | loop fusion | flops 2097152 | bytes 1050880 | tf_op jit(solution)/shard_map/jit(_where)/select_n | solution.py:23
  26.4 12.9 %all-to-all-done = bf16[16,256,256]{2,1,0:T(8,128)(2,1)} async-done(((bf16[16,256,256]{2,1,0:T(8,128)(2,1)}), bf16[16,256,256]{2,1,0:T(8,128)(2,1)}, u32[]{:S(2)}, u32[]{:S(2)}) %all-to-all-start) | async-done | bytes 2097184 | tf_op jit(solution)/shard_map/all_to_all | solution.py:85
  39.4 5.2 %fusion.5 = bf16[256,3,256]{2,0,1:T(8,128)(2,1)S(1)} fusion(bf16[16,256,3,256]{3,1,0,2:T(8,128)(2,1)} %bitcast.180, bf16[16,256,256]{2,1,0:T(8,128)(2,1)} %all-to-all-done), kind=kOutput, calls=%fused_computation.5 | convolution fusion | flops 1610809344 | bytes 8781824 | tf_op jit(solution)/shard_map/stf,sfqc->tqc/dot_general | solution.py:87
  44.7 1.3 collective-permute-start.1
  46.0 4.5 %collective-permute-start = (bf16[2,768]{1,0:T(2,128)(2,1)S(1)}, bf16[2,768]{1,0:T(2,128)(2,1)S(1)}, u32[]{:S(2)}, u32[]{:S(2)}) collective-permute-start(bf16[2,768]{1,0:T(2,128)(2,1)S(1)} %bitcast.179), channel_id=1, source_target_pairs={{0,16},{16,32},{32,48},{48,64},{64,80},{80,96},{96,112},{112,128},... | collective-permute-start | bytes 9224 | tf_op jit(solution)/shard_map/ppermute | solution.py:12
  52.5 2.1 %fusion.139 = (f32[258,768]{0,1:T(8,128)S(1)}, f32[258,768]{0,1:T(8,128)}, f32[258,768]{0,1:T(8,128)}) fusion(f32[260,768]{0,1:T(8,128)S(1)} %maximum_convert_fusion), kind=kLoop, calls=%fused_computation.470 | loop fusion | bytes 4755456 | tf_op jit(solution)/shard_map/slice | solution.py:100
  54.7 2.5 %copy.101 = f32[258,3,256]{2,0,1:T(8,128)} copy(f32[258,3,256]{0,2,1:T(8,128)} %bitcast.167) | data formatting | bytes 1585152 | tf_op jit(solution)/shard_map/slice | solution.py:102
  57.2 2.5 %copy.99 = f32[258,3,256]{2,0,1:T(8,128)} copy(f32[258,3,256]{0,2,1:T(8,128)} %bitcast.166) | data formatting | bytes 1585152 | tf_op jit(solution)/shard_map/slice | solution.py:101
  59.7 1.2 copy.97
  61.0 1.8 %multiply_add_fusion = f32[258,3,256]{2,0,1:T(8,128)S(1)} fusion(f32[258,3,256]{2,0,1:T(8,128)} %copy.101, f32[258,3,256]{2,0,1:T(8,128)} %copy.99, f32[258,3,256]{2,0,1:T(8,128)} %copy.97, f32[3,256]{1,0:T(4,128)S(1)} %get-tuple-element.245, f32[3,256]{1,0:T(4,128)S(1)} %get-tuple-element.246, f32[3,256]{1,0:T(4,128)S(1)} %bitcast.176), kind=kLoop, calls=%fused_computation.26 | loop fusion | flops 990720 | bytes 3179520 | tf_op jit(solution)/shard_map/add | solution.py:100
  64.2 1.7 %copy.107 = bf16[256,256]{0,1:T(8,128)(2,1)} copy(bf16[256,256]{1,0:T(8,128)(2,1)} %multiply_convert_fusion.2) | data formatting | bytes 262144 | tf_op jit(solution)/shard_map/convert_element_type | solution.py:107
  65.8 1.7 %copy.106 = bf16[256,1,256]{0,2,1:T(8,128)(2,1)} copy(bf16[256,1,256]{2,0,1:T(8,128)(2,1)} %fusion.74) | data formatting | bytes 262144 | tf_op jit(solution)/shard_map/convert_element_type | solution.py:105
  67.5 1.7 %pad_maximum_fusion.2 = bf16[256,16,32]{0,2,1:T(8,128)(2,1)} fusion(bf16[256,16,16]{0,2,1:T(8,128)(2,1)} %bitcast.174, bf16[256,16,16]{0,2,1:T(8,128)(2,1)} %bitcast.175), kind=kLoop, calls=%fused_computation.174 | loop fusion | flops 524288 | bytes 524288 | tf_op jit(solution)/shard_map/concatenate | solution.py:110
  69.2 11.2 %all-to-all-start.1 = ((bf16[256,16,32]{0,2,1:T(8,128)(2,1)}), bf16[256,16,32]{0,2,1:T(8,128)(2,1)}, u32[]{:S(2)}, u32[]{:S(2)}) async-start(bf16[256,16,32]{0,2,1:T(8,128)(2,1)} %pad_maximum_fusion.2), calls=%async_computation.1 | async-start | bytes 524288 | tf_op jit(solution)/shard_map/all_to_all | solution.py:70
  80.5 1.7 %select_convert_fusion = bf16[256,256]{1,0:T(8,128)(2,1)} fusion(bf16[256]{0:T(256)(128)(2,1)S(1)} %fusion.127, s32[256]{0:T(256)S(1)} %copy-done.43, pred[256]{0:T(512)(128)(4,1)S(1)} %iota_compare_fusion.36), kind=kLoop, calls=%fused_computation.185 | loop fusion | flops 1048576 | bytes 132864 | tf_op jit(solution)/shard_map/convert.10
  82.2 1.7 %multiply_convert_fusion.3 = bf16[256,256]{1,0:T(8,128)(2,1)} fusion(f32[256]{0:T(256)S(1)} %copy-done.45, s32[256]{0:T(256)S(1)} %copy-done.43), kind=kLoop, calls=%fused_computation.186 | loop fusion | flops 1048576 | bytes 133120 | tf_op jit(solution)/shard_map/convert.9
  83.9 7.7 %all-to-all-done.1 = bf16[256,16,32]{0,2,1:T(8,128)(2,1)} async-done(((bf16[256,16,32]{0,2,1:T(8,128)(2,1)}), bf16[256,16,32]{0,2,1:T(8,128)(2,1)}, u32[]{:S(2)}, u32[]{:S(2)}) %all-to-all-start.1) | async-done | bytes 262176 | tf_op jit(solution)/shard_map/all_to_all | solution.py:70
  91.6 1.2 fusion.144
  92.9 1.1 fusion.145
  102.4 1.0 fusion.16
  104.5 0.9 fusion.22
  105.4 3.6 %all-to-all-start.2 = ((bf16[258,16,48]{0,2,1:T(8,128)(2,1)}), bf16[258,16,48]{0,2,1:T(8,128)(2,1)S(1)}, u32[]{:S(2)}, u32[]{:S(2)}) async-start(bf16[258,16,48]{0,2,1:T(8,128)(2,1)} %fusion.22), calls=%async_computation.2 | async-start | bytes 1179648 | tf_op jit(solution)/shard_map/all_to_all | solution.py:70
  109.6 15.0 %all-to-all-done.2 = bf16[258,16,48]{0,2,1:T(8,128)(2,1)S(1)} async-done(((bf16[258,16,48]{0,2,1:T(8,128)(2,1)}), bf16[258,16,48]{0,2,1:T(8,128)(2,1)S(1)}, u32[]{:S(2)}, u32[]{:S(2)}) %all-to-all-start.2) | async-done | bytes 396320 | tf_op jit(solution)/shard_map/all_to_all | solution.py:70
  126.1 1.8 %copy.108 = f32[256,256]{1,0:T(8,128)} copy(f32[256,256]{0,1:T(8,128)} %bitcast_convert_fusion.3) | data formatting | bytes 524288 | tf_op jit(solution)/shard_map/slice | solution.py:183
  127.9 1.6 %multiply_convert_fusion.1 = bf16[256,256]{1,0:T(8,128)(2,1)} fusion(f32[256,256]{1,0:T(8,128)} %copy.108, f32[258,3,256]{2,0,1:T(8,128)S(1)} %multiply_add_fusion), kind=kLoop, calls=%fused_computation.176 | loop fusion | flops 131072 | bytes 655360 | tf_op jit(solution)/shard_map/convert_element_type | solution.py:183
  131.1 1.0 fusion.67
  132.3 0.9 multiply_convert_fusion
  133.3 1.0 fusion.20
  (228 shorter events, 27.5 us)
Async XLA Ops:
  0.6 10.1 %copy-start = (bf16[4096,256]{1,0:T(8,128)(2,1)S(1)}, bf16[4096,256]{1,0:T(8,128)(2,1)}, u32[]{:S(2)}) copy-start(bf16[4096,256]{1,0:T(8,128)(2,1)} %param.8) | copy-start | bytes 6291460
  3.3 36.1 %all-to-all-start = ((bf16[16,256,256]{2,1,0:T(8,128)(2,1)}), bf16[16,256,256]{2,1,0:T(8,128)(2,1)}, u32[]{:S(2)}, u32[]{:S(2)}) async-start(bf16[16,256,256]{2,1,0:T(8,128)(2,1)} %broadcast_in_dim.730), calls=%async_computation | async-start | bytes 4194304 | tf_op jit(solution)/shard_map/all_to_all | solution.py:85
  16.8 0.8 copy-start.1
  16.8 1.0 copy-start.3
  16.9 2.2 %copy-start.5 = (bf16[512,512]{1,0:T(8,128)(2,1)}, bf16[512,512]{1,0:T(8,128)(2,1)S(1)}, u32[]{:S(2)}) copy-start(bf16[512,512]{1,0:T(8,128)(2,1)S(1)} %fusion.18) | copy-start | bytes 1572868
  22.1 38.8 %copy-start.38 = (f32[3,256]{1,0:T(4,128)}, f32[3,256]{1,0:T(4,128)S(1)}, u32[]{:S(2)}) copy-start(f32[3,256]{1,0:T(4,128)S(1)} %get-tuple-element.246) | copy-start | bytes 9220
  39.4 5.2 %slice-start = ((bf16[256,256]{1,0:T(8,128)(2,1)}), bf16[2,256]{1,0:T(2,128)(2,1)S(1)}, s32[]{:S(2)}) async-start(bf16[256,256]{1,0:T(8,128)(2,1)} %param.9), calls=%async_computation.3 | async-start | bytes 2048 | tf_op jit(solution)/shard_map/slice | solution.py:92
  44.7 7.3 %collective-permute-start.1 = (bf16[2,1024]{1,0:T(2,128)(2,1)S(1)}, bf16[2,1024]{1,0:T(2,128)(2,1)S(1)}, u32[]{:S(2)}, u32[]{:S(2)}) collective-permute-start(bf16[2,1024]{1,0:T(2,128)(2,1)S(1)} %pad_maximum_fusion.3), channel_id=1, source_target_pairs={{16,0},{32,16},{48,32},{64,48},{80,64},{96,80},{112,96},{128,112},... | collective-permute-start | bytes 12296 | tf_op jit(solution)/shard_map/ppermute | solution.py:12
  46.0 5.9 %collective-permute-start = (bf16[2,768]{1,0:T(2,128)(2,1)S(1)}, bf16[2,768]{1,0:T(2,128)(2,1)S(1)}, u32[]{:S(2)}, u32[]{:S(2)}) collective-permute-start(bf16[2,768]{1,0:T(2,128)(2,1)S(1)} %bitcast.179), channel_id=1, source_target_pairs={{0,16},{16,32},{32,48},{48,64},{64,80},{80,96},{96,112},{112,128},... | collective-permute-start | bytes 9224 | tf_op jit(solution)/shard_map/ppermute | solution.py:12
  51.1 9.9 %copy-start.40 = (f32[3,1,256]{2,0,1:T(4,128)}, f32[3,1,256]{2,0,1:T(4,128)S(1)}, u32[]{:S(2)}) copy-start(f32[3,1,256]{2,0,1:T(4,128)S(1)} %copy.130) | copy-start | bytes 9220
  52.0 2.7 %copy-start.44 = (bf16[2,1024]{1,0:T(2,128)(2,1)}, bf16[2,1024]{1,0:T(2,128)(2,1)S(1)}, u32[]{:S(2)}) copy-start(bf16[2,1024]{1,0:T(2,128)(2,1)S(1)} %collective-permute-done.1) | copy-start | bytes 12292
  61.0 1.8 %copy-start.8 = (bf16[256,256]{1,0:T(8,128)(2,1)S(1)}, bf16[256,256]{1,0:T(8,128)(2,1)}, u32[]{:S(2)}) copy-start(bf16[256,256]{1,0:T(8,128)(2,1)} %param.9) | copy-start | bytes 393220
  63.5 16.9 %copy-start.43 = (s32[256]{0:T(256)S(1)}, s32[256]{0:T(256)}, u32[]{:S(2)}) copy-start(s32[256]{0:T(256)} %iota_add_fusion) | copy-start | bytes 3076
  63.5 18.7 %copy-start.45 = (f32[256]{0:T(256)S(1)}, f32[256]{0:T(256)}, u32[]{:S(2)}) copy-start(f32[256]{0:T(256)} %select_multiply_fusion) | copy-start | bytes 3076
  63.5 28.1 %copy-start.6 = (bf16[512,512]{1,0:T(8,128)(2,1)S(1)}, bf16[512,512]{1,0:T(8,128)(2,1)}, u32[]{:S(2)}) copy-start(bf16[512,512]{1,0:T(8,128)(2,1)} %copy-done.5) | copy-start | bytes 1572868
  69.2 22.4 %all-to-all-start.1 = ((bf16[256,16,32]{0,2,1:T(8,128)(2,1)}), bf16[256,16,32]{0,2,1:T(8,128)(2,1)}, u32[]{:S(2)}, u32[]{:S(2)}) async-start(bf16[256,16,32]{0,2,1:T(8,128)(2,1)} %pad_maximum_fusion.2), calls=%async_computation.1 | async-start | bytes 524288 | tf_op jit(solution)/shard_map/all_to_all | solution.py:70
  91.6 1.3 copy-start.9
  91.6 1.3 copy-start.10
  95.4 0.7 copy-start.27
  96.1 0.7 copy-start.25
  96.9 0.7 copy-start.23
  97.6 0.7 copy-start.21
  98.5 0.8 copy-start.16
  98.6 0.8 copy-start.17
  101.1 0.7 copy-start.31
  101.2 1.0 copy-start.2
  101.2 1.2 copy-start.4
  105.4 19.3 %all-to-all-start.2 = ((bf16[258,16,48]{0,2,1:T(8,128)(2,1)}), bf16[258,16,48]{0,2,1:T(8,128)(2,1)S(1)}, u32[]{:S(2)}, u32[]{:S(2)}) async-start(bf16[258,16,48]{0,2,1:T(8,128)(2,1)} %fusion.22), calls=%async_computation.2 | async-start | bytes 1179648 | tf_op jit(solution)/shard_map/all_to_all | solution.py:70
  130.2 1.9 %copy-start.7 = (bf16[258,16,16]{0,2,1:T(8,128)(2,1)S(1)}, bf16[258,16,16]{0,2,1:T(8,128)(2,1)}, u32[]{:S(2)}) copy-start(bf16[258,16,16]{0,2,1:T(8,128)(2,1)} %get-tuple-element.44) | copy-start | bytes 396292
  132.1 1.2 copy-start.39
  132.1 1.2 copy-start.41
  133.3 1.0 copy-start.11
  (20 other events, 14.4 us)

commit v6 on v5

--- a/solution.py
+++ b/solution.py
@@ -85,23 +85,19 @@
     gathered = lax.all_to_all(copies, "chan", 0, 0, tiled=True)
     weight_parts = in_weight.reshape(chan_count, local_width, 3, local_width)
     streams = jnp.einsum(
-        "stf,sfqc->tqc", gathered, weight_parts, preferred_element_type=jnp.float32
-    ).astype(jnp.bfloat16)
-    streams = streams.reshape(row_count, 3 * local_width)
-    before = neighbour_rows(streams[row_count - 2 :], 1)
-    after = neighbour_rows(jnp.concatenate([streams[:2], cotangent[:2]], axis=1), -1)
-    next_streams, next_cot = (after[:, : 3 * local_width], after[:, 3 * local_width :])
-    extended = (
-        jnp.concatenate([before, streams, next_streams], axis=0)
-        .astype(jnp.float32)
-        .reshape(row_count + 4, 3, local_width)
-    )
+        "stf,sfqc->qtc", gathered, weight_parts, preferred_element_type=jnp.float32
+    ).astype(jnp.bfloat16)
+    before = neighbour_rows(streams[:, row_count - 2 :], 1)
+    after = neighbour_rows(jnp.concatenate([streams[:, :2], cotangent[None, :2]], axis=0), -1)
+    next_streams, next_cot = (after[:3], after[3])
+    extended = jnp.concatenate([before, streams, next_streams], axis=1).astype(jnp.float32)
+    conv_weight = short_weight[:, :, None, :]
     conv_out = (
-        short_weight[:, 0] * extended[2:]
-        + short_weight[:, 1] * extended[1:-1]
-        + short_weight[:, 2] * extended[:-2]
-    )
-    query_conv, key_conv, value_conv = (conv_out[:, 0], conv_out[:, 1], conv_out[:, 2])
+        conv_weight[:, 0] * extended[:, 2:]
+        + conv_weight[:, 1] * extended[:, 1:-1]
+        + conv_weight[:, 2] * extended[:, :-2]
+    )
+    query_conv, key_conv, value_conv = (conv_out[0], conv_out[1], conv_out[2])
     gated = (key_conv[:row_count] * value_conv[:row_count]).astype(jnp.bfloat16)
     cot_wide = jnp.concatenate([cotangent, next_cot], axis=0).astype(jnp.float32)
     grad_long = (cot_wide[:row_count] * query_conv[:row_count]).astype(jnp.bfloat16)
@@ -183,13 +179,13 @@
     operator_out = (query_conv[:row_count] * long_out[:row_count]).astype(jnp.bfloat16)
     grad_query = cot_wide * long_out
     grad_streams = jnp.stack(
-        [grad_query, gated_wide * value_conv, gated_wide * key_conv], axis=1
+        [grad_query, gated_wide * value_conv, gated_wide * key_conv], axis=0
     ).astype(jnp.bfloat16).astype(jnp.float32)
     stream_grads = (
-        short_weight[:, 0] * grad_streams[:row_count]
-        + short_weight[:, 1] * grad_streams[1 : row_count + 1]
-        + short_weight[:, 2] * grad_streams[2:]
-    ).astype(jnp.bfloat16)
+        conv_weight[:, 0] * grad_streams[:, :row_count]
+        + conv_weight[:, 1] * grad_streams[:, 1 : row_count + 1]
+        + conv_weight[:, 2] * grad_streams[:, 2:]
+    ).astype(jnp.bfloat16).transpose(1, 0, 2)
     return (operator_out, stream_grads, tap_grads)
 
 

time: 137 us -> 128 us (0.934)
  local copies, waits for them, and re-layouts: 37.8 us -> 33.5 us
  waiting for transfers between devices: 36.2 us -> 32.8 us
  other arithmetic: 21.5 us -> 18.6 us
    slice x10 -> x5, local copies, waits for them, and re-layouts: 8.63 us -> 0.6 us  [the longest x1 0.58 us: on_device(): conv_weight[:, 0] * extended[:, 2:] + conv_weight[:, 1] * extended[:, 1:-1]]
    all_to_all x1, waiting for transfers between devices: 12.9 us -> 10 us  [on_device(): gathered = lax.all_to_all(copies, 'chan', 0, 0, tiled=True)]
    unnamed x110 -> x108, local copies, waits for them, and re-layouts: 6.5 us -> 8.98 us
    slice x1, local copies, waits for them, and re-layouts: 1.79 us -> 0.13 us  [on_device(): long_out[:row_count]]
    add x1, other arithmetic: 1.83 us -> 0.25 us  [on_device(): conv_weight[:, 0] * extended[:, 2:] + conv_weight[:, 1] * extended[:, 1:-1]]
  transfers between devices with their start and end apart: 5 -> 5, of which waited for: 4 -> 4; matrix products, arithmetic and copies ran while one was open for 15% -> 18% of each run, Pallas kernels for 0% -> 0%
where the time goes in v6:
time: 128 us; the launch traced here: 125 us
  local copies, waits for them, and re-layouts  33.5 us (26%)
  waiting for transfers between devices  32.8 us (26%)
  starting transfers between devices  28.8 us (22%)
  other arithmetic  18.6 us (15%)
  matrix products  9.85 us (8%)
  between operations  1.79 us (1%)
    all_to_all x2, waiting for transfers between devices, swap_layout(): return lax.all_to_all(values, 'seq', 1, 1, tiled=True)  22.1 us
    all_to_all x2, starting transfers between devices, swap_layout(): return lax.all_to_all(values, 'seq', 1, 1, tiled=True)  15.5 us
    all_to_all x1, waiting for transfers between devices, on_device(): gathered = lax.all_to_all(copies, 'chan', 0, 0, tiled=True)  10 us
    unnamed x108, local copies, waits for them, and re-layouts  8.98 us
    mul x15, local copies, waits for them, and re-layouts, spectral_product(): real_out = left_re * right_re - jnp.where(first_row, 0.0, cross_term)  7.95 us
    all_to_all x1, starting transfers between devices, on_device(): gathered = lax.all_to_all(copies, 'chan', 0, 0, tiled=True)  7.48 us
    another operation x4, other arithmetic  5.85 us
    ppermute x2, starting transfers between devices, passed_along(): return lax.ppermute(block, axis, route)  5.84 us
  transfers between devices with their start and end apart: 5, of which 4 were waited for; matrix products, arithmetic and copies ran while one was open for 18% of the time, Pallas kernels for 0%

profile of v6, /device:TPU:2, one launch (start us, length us, event | category | flops | bytes accessed | tf_op | source)
XLA Modules:
  0.0 125.4 jit_solution(12749247906108257508)
XLA Ops:
  0.6 2.6 %broadcast_in_dim.737 = bf16[16,256,256]{2,1,0:T(8,128)(2,1)} broadcast(bf16[256,256]{1,0:T(8,128)(2,1)} %param.5), dimensions={1,2} | broadcast | bytes 2228224 | tf_op jit(solution)/shard_map/broadcast_in_dim | solution.py:84
  3.2 7.5 %all-to-all-start = ((bf16[16,256,256]{2,1,0:T(8,128)(2,1)}), bf16[16,256,256]{2,1,0:T(8,128)(2,1)}, u32[]{:S(2)}, u32[]{:S(2)}) async-start(bf16[16,256,256]{2,1,0:T(8,128)(2,1)} %broadcast_in_dim.737), calls=%async_computation | async-start | bytes 4194304 | tf_op jit(solution)/shard_map/all_to_all | solution.py:85
  10.7 1.3 %constant_dynamic-slice_fusion = bf16[3840,16]{1,0:T(8,128)(2,1)} fusion(bf16[4096,256]{1,0:T(8,128)(2,1)S(1)} %copy-done, s32[]{:T(128)S(6)} %select_n.380), kind=kLoop, calls=%fused_computation.464 | loop fusion | bytes 245764 | tf_op jit(solution)/shard_map/slice | solution.py:118
  13.4 2.2 %copy.15 = bf16[15,256,16]{1,2,0:T(8,128)(2,1)} copy(bf16[15,256,16]{2,1,0:T(8,128)(2,1)} %bitcast.167) | data formatting | bytes 245760 | tf_op jit(solution)/shard_map/slice | solution.py:118
  15.5 1.0 copy.17
  16.5 2.1 %negate_select_fusion.2 = (f32[256,512]{1,0:T(8,128)S(1)}, f32[256,512]{1,0:T(8,128)S(1)}) fusion(f32[512]{0:T(512)S(1)} %fusion.96, pred[256]{0:T(512)(128)(4,1)S(1)} %iota_compare_fusion.36), kind=kLoop, calls=%fused_computation.143 | loop fusion | flops 2097152 | bytes 1050880 | tf_op jit(solution)/shard_map/jit(_where)/select_n | solution.py:23
  24.4 0.7 slice_bitcast_fusion.34
  29.3 10.0 %all-to-all-done = bf16[16,256,256]{2,1,0:T(8,128)(2,1)} async-done(((bf16[16,256,256]{2,1,0:T(8,128)(2,1)}), bf16[16,256,256]{2,1,0:T(8,128)(2,1)}, u32[]{:S(2)}, u32[]{:S(2)}) %all-to-all-start) | async-done | bytes 2097184 | tf_op jit(solution)/shard_map/all_to_all | solution.py:85
  39.4 5.2 %fusion.8 = bf16[3,256,256]{2,1,0:T(8,128)(2,1)S(1)} fusion(bf16[16,256,3,256]{3,1,0,2:T(8,128)(2,1)} %bitcast.174, bf16[16,256,256]{2,1,0:T(8,128)(2,1)} %all-to-all-done), kind=kOutput, calls=%fused_computation.9 | convolution fusion | flops 1610809344 | bytes 8781824 | tf_op jit(solution)/shard_map/stf,sfqc->qtc/dot_general | solution.py:87
  44.6 1.3 %collective-permute-start.1 = (bf16[4,2,256]{2,1,0:T(2,128)(2,1)S(1)}, bf16[4,2,256]{2,1,0:T(2,128)(2,1)S(1)}, u32[]{:S(2)}, u32[]{:S(2)}) collective-permute-start(bf16[4,2,256]{2,1,0:T(2,128)(2,1)S(1)} %pad_maximum_fusion.3), channel_id=1, source_target_pairs={{16,0},{32,16},{48,32},{64,48},{80,64},{96,80},{112,96},{128,112},... | collective-permute-start | bytes 12296 | tf_op jit(solution)/shard_map/ppermute | solution.py:12
  45.9 4.5 %collective-permute-start = (bf16[3,2,256]{2,1,0:T(2,128)(2,1)S(1)}, bf16[3,2,256]{2,1,0:T(2,128)(2,1)S(1)}, u32[]{:S(2)}, u32[]{:S(2)}) collective-permute-start(bf16[3,2,256]{2,1,0:T(2,128)(2,1)S(1)} %get-tuple-element.81), channel_id=1, source_target_pairs={{0,16},{16,32},{32,48},{48,64},{64,80},{80,96},{96,112},{112,128},... | collective-permute-start | bytes 9224 | tf_op jit(solution)/shard_map/ppermute | solution.py:12
  52.8 0.7 multiply_convert_fusion.2
  54.2 1.7 %copy.19 = bf16[256,256]{0,1:T(8,128)(2,1)} copy(bf16[256,256]{1,0:T(8,128)(2,1)} %multiply_convert_fusion.2) | data formatting | bytes 262144 | tf_op jit(solution)/shard_map/convert_element_type | solution.py:103
  55.8 1.7 %copy.18 = bf16[1,256,256]{1,2,0:T(8,128)(2,1)} copy(bf16[1,256,256]{2,1,0:T(8,128)(2,1)} %fusion.80) | data formatting | bytes 262144 | tf_op jit(solution)/shard_map/convert_element_type | solution.py:101
  57.5 1.7 %pad_maximum_fusion.2 = bf16[256,16,32]{0,2,1:T(8,128)(2,1)} fusion(bf16[256,16,16]{0,2,1:T(8,128)(2,1)} %bitcast.169, bf16[256,16,16]{0,2,1:T(8,128)(2,1)} %bitcast.170), kind=kLoop, calls=%fused_computation.180 | loop fusion | flops 524288 | bytes 524288 | tf_op jit(solution)/shard_map/concatenate | solution.py:106
  59.2 11.2 %all-to-all-start.1 = ((bf16[256,16,32]{0,2,1:T(8,128)(2,1)}), bf16[256,16,32]{0,2,1:T(8,128)(2,1)}, u32[]{:S(2)}, u32[]{:S(2)}) async-start(bf16[256,16,32]{0,2,1:T(8,128)(2,1)} %pad_maximum_fusion.2), calls=%async_computation.1 | async-start | bytes 524288 | tf_op jit(solution)/shard_map/all_to_all | solution.py:70
  70.4 2.4 %select_convert_fusion = bf16[256,256]{1,0:T(8,128)(2,1)} fusion(bf16[256]{0:T(256)(128)(2,1)S(1)} %fusion.133, s32[256]{0:T(256)} %iota_add_fusion, pred[256]{0:T(512)(128)(4,1)S(1)} %iota_compare_fusion.36), kind=kLoop, calls=%fused_computation.191 | loop fusion | flops 1048576 | bytes 132864 | tf_op jit(solution)/shard_map/convert.10
  72.8 2.4 %multiply_convert_fusion.3 = bf16[256,256]{1,0:T(8,128)(2,1)} fusion(f32[256]{0:T(256)} %select_multiply_fusion, s32[256]{0:T(256)} %iota_add_fusion), kind=kLoop, calls=%fused_computation.192 | loop fusion | flops 1048576 | bytes 133120 | tf_op jit(solution)/shard_map/convert.9
  75.2 6.4 %all-to-all-done.1 = bf16[256,16,32]{0,2,1:T(8,128)(2,1)} async-done(((bf16[256,16,32]{0,2,1:T(8,128)(2,1)}), bf16[256,16,32]{0,2,1:T(8,128)(2,1)}, u32[]{:S(2)}, u32[]{:S(2)}) %all-to-all-start.1) | async-done | bytes 262176 | tf_op jit(solution)/shard_map/all_to_all | solution.py:70
  81.6 1.3 %fusion.149 = (f32[16,16,512]{2,1,0:T(8,128)S(1)}, bf16[16,16,512]{2,1,0:T(8,128)(2,1)S(1)}) fusion(bf16[512,512]{1,0:T(8,128)(2,1)} %copy-done.3, bf16[256,16,32]{0,2,1:T(8,128)(2,1)} %all-to-all-done.1), kind=kOutput, calls=%fused_computation.480 | convolution fusion | flops 67371008 | bytes 1179648 | tf_op jit(solution)/shard_map/tbc,kt->bck/dot_general | solution.py:112
  83.0 1.1 fusion.150
  92.4 1.1 fusion.19
  93.6 0.9 copy-done.4
  95.4 0.9 fusion.27
  96.2 4.3 %all-to-all-start.2 = ((bf16[258,16,48]{0,2,1:T(8,128)(2,1)}), bf16[258,16,48]{0,2,1:T(8,128)(2,1)}, u32[]{:S(2)}, u32[]{:S(2)}) async-start(bf16[258,16,48]{0,2,1:T(8,128)(2,1)} %fusion.27), calls=%async_computation.2 | async-start | bytes 1179648 | tf_op jit(solution)/shard_map/all_to_all | solution.py:70
  100.5 15.7 %all-to-all-done.2 = bf16[258,16,48]{0,2,1:T(8,128)(2,1)} async-done(((bf16[258,16,48]{0,2,1:T(8,128)(2,1)}), bf16[258,16,48]{0,2,1:T(8,128)(2,1)}, u32[]{:S(2)}, u32[]{:S(2)}) %all-to-all-start.2) | async-done | bytes 396320 | tf_op jit(solution)/shard_map/all_to_all | solution.py:70
  116.2 1.7 %fusion.145 = (bf16[256,16,16]{0,2,1:T(8,128)(2,1)}, bf16[256,16,16]{0,2,1:T(8,128)(2,1)S(1)}) fusion(bf16[258,16,48]{0,2,1:T(8,128)(2,1)} %all-to-all-done.2), kind=kLoop, calls=%fused_computation.476 | loop fusion | bytes 524288 | tf_op jit(solution)/shard_map/slice | solution.py:177
  118.7 1.7 %fusion.146 = (bf16[258,16,16]{0,2,1:T(8,128)(2,1)}, bf16[258,16,16]{0,2,1:T(8,128)(2,1)S(1)}) fusion(bf16[258,16,48]{0,2,1:T(8,128)(2,1)} %all-to-all-done.2), kind=kLoop, calls=%fused_computation.477 | loop fusion | bytes 528384 | tf_op jit(solution)/shard_map/slice | solution.py:175
  120.5 0.8 copy.22
  121.4 1.0 fusion.73
  123.5 1.0 fusion.71
  124.5 0.8 copy.24
  (219 shorter events, 24.6 us)
Async XLA Ops:
  0.6 10.1 %copy-start = (bf16[4096,256]{1,0:T(8,128)(2,1)S(1)}, bf16[4096,256]{1,0:T(8,128)(2,1)}, u32[]{:S(2)}) copy-start(bf16[4096,256]{1,0:T(8,128)(2,1)} %param.8) | copy-start | bytes 6291460
  3.2 36.1 %all-to-all-start = ((bf16[16,256,256]{2,1,0:T(8,128)(2,1)}), bf16[16,256,256]{2,1,0:T(8,128)(2,1)}, u32[]{:S(2)}, u32[]{:S(2)}) async-start(bf16[16,256,256]{2,1,0:T(8,128)(2,1)} %broadcast_in_dim.737), calls=%async_computation | async-start | bytes 4194304 | tf_op jit(solution)/shard_map/all_to_all | solution.py:85
  16.5 2.2 %copy-start.11 = (bf16[16,256,16]{1,2,0:T(8,128)(2,1)S(1)}, bf16[16,256,16]{1,2,0:T(8,128)(2,1)}, u32[]{:S(2)}) copy-start(bf16[16,256,16]{1,2,0:T(8,128)(2,1)} %copy.17) | copy-start | bytes 393220
  16.5 2.2 %copy-start.12 = (bf16[15,256,16]{1,2,0:T(8,128)(2,1)S(1)}, bf16[15,256,16]{1,2,0:T(8,128)(2,1)}, u32[]{:S(2)}) copy-start(bf16[15,256,16]{1,2,0:T(8,128)(2,1)} %copy.15) | copy-start | bytes 368644
  18.6 0.8 copy-start.1
  18.7 2.0 %copy-start.3 = (bf16[512,512]{1,0:T(8,128)(2,1)}, bf16[512,512]{1,0:T(8,128)(2,1)S(1)}, u32[]{:S(2)}) copy-start(bf16[512,512]{1,0:T(8,128)(2,1)S(1)} %fusion.21) | copy-start | bytes 1572868
  39.4 11.7 %copy-start.42 = (f32[3,1,1,256]{3,1,0,2:T(1,128)S(1)}, f32[3,1,1,256]{3,1,0,2:T(1,128)}, u32[]{:S(2)}) copy-start(f32[3,1,1,256]{3,1,0,2:T(1,128)} %get-tuple-element.221) | copy-start | bytes 9220
  44.6 7.3 %copy-start.38 = (f32[3,256]{1,0:T(4,128)S(1)}, f32[3,256]{1,0:T(4,128)}, u32[]{:S(2)}) copy-start(f32[3,256]{1,0:T(4,128)} %get-tuple-element.231) | copy-start | bytes 9220
  44.6 6.4 %collective-permute-start.1 = (bf16[4,2,256]{2,1,0:T(2,128)(2,1)S(1)}, bf16[4,2,256]{2,1,0:T(2,128)(2,1)S(1)}, u32[]{:S(2)}, u32[]{:S(2)}) collective-permute-start(bf16[4,2,256]{2,1,0:T(2,128)(2,1)S(1)} %pad_maximum_fusion.3), channel_id=1, source_target_pairs={{16,0},{32,16},{48,32},{64,48},{80,64},{96,80},{112,96},{128,112},... | collective-permute-start | bytes 12296 | tf_op jit(solution)/shard_map/ppermute | solution.py:12
  45.9 5.9 %collective-permute-start = (bf16[3,2,256]{2,1,0:T(2,128)(2,1)S(1)}, bf16[3,2,256]{2,1,0:T(2,128)(2,1)S(1)}, u32[]{:S(2)}, u32[]{:S(2)}) collective-permute-start(bf16[3,2,256]{2,1,0:T(2,128)(2,1)S(1)} %get-tuple-element.81), channel_id=1, source_target_pairs={{0,16},{16,32},{32,48},{48,64},{64,80},{80,96},{96,112},{112,128},... | collective-permute-start | bytes 9224 | tf_op jit(solution)/shard_map/ppermute | solution.py:12
  51.1 1.1 copy-start.40
  51.1 0.8 copy-start.44
  51.9 0.9 copy-start.6
  59.2 22.4 %all-to-all-start.1 = ((bf16[256,16,32]{0,2,1:T(8,128)(2,1)}), bf16[256,16,32]{0,2,1:T(8,128)(2,1)}, u32[]{:S(2)}, u32[]{:S(2)}) async-start(bf16[256,16,32]{0,2,1:T(8,128)(2,1)} %pad_maximum_fusion.2), calls=%async_computation.1 | async-start | bytes 524288 | tf_op jit(solution)/shard_map/all_to_all | solution.py:70
  81.6 1.4 %copy-start.8 = (bf16[256,256]{1,0:T(8,128)(2,1)S(1)}, bf16[256,256]{1,0:T(8,128)(2,1)}, u32[]{:S(2)}) copy-start(bf16[256,256]{1,0:T(8,128)(2,1)} %select_convert_fusion) | copy-start | bytes 393220
  81.6 1.4 %copy-start.9 = (bf16[256,256]{1,0:T(8,128)(2,1)S(1)}, bf16[256,256]{1,0:T(8,128)(2,1)}, u32[]{:S(2)}) copy-start(bf16[256,256]{1,0:T(8,128)(2,1)} %multiply_convert_fusion.3) | copy-start | bytes 393220
  85.5 0.7 copy-start.27
  86.2 0.7 copy-start.25
  87.0 0.7 copy-start.23
  87.7 0.7 copy-start.21
  88.7 0.8 copy-start.16
  88.7 0.8 copy-start.17
  91.2 0.7 copy-start.31
  91.3 1.0 copy-start.2
  93.4 1.0 copy-start.4
  96.2 20.0 %all-to-all-start.2 = ((bf16[258,16,48]{0,2,1:T(8,128)(2,1)}), bf16[258,16,48]{0,2,1:T(8,128)(2,1)}, u32[]{:S(2)}, u32[]{:S(2)}) async-start(bf16[258,16,48]{0,2,1:T(8,128)(2,1)} %fusion.27), calls=%async_computation.2 | async-start | bytes 1179648 | tf_op jit(solution)/shard_map/all_to_all | solution.py:70
  121.4 1.1 copy-start.5
  121.4 1.3 %slice-start = ((bf16[4,2,256]{2,1,0:T(2,128)(2,1)}), bf16[1,2,256]{2,1,0:T(2,128)(2,1)S(1)}, s32[]{:S(2)}) async-start(bf16[4,2,256]{2,1,0:T(2,128)(2,1)} %copy-done.44), calls=%async_computation.3 | async-start | bytes 2048 | tf_op jit(solution)/shard_map/slice | solution.py:92
  122.4 0.9 copy-start.7
  122.5 0.9 copy-start.39
  122.5 0.9 copy-start.41
  123.5 1.0 copy-start.10
  (19 other events, 13.7 us)

commit v7 on v6

--- a/solution.py
+++ b/solution.py
@@ -88,9 +88,7 @@
         "stf,sfqc->qtc", gathered, weight_parts, preferred_element_type=jnp.float32
     ).astype(jnp.bfloat16)
     before = neighbour_rows(streams[:, row_count - 2 :], 1)
-    after = neighbour_rows(jnp.concatenate([streams[:, :2], cotangent[None, :2]], axis=0), -1)
-    next_streams, next_cot = (after[:3], after[3])
-    extended = jnp.concatenate([before, streams, next_streams], axis=1).astype(jnp.float32)
+    extended = jnp.concatenate([before, streams], axis=1).astype(jnp.float32)
     conv_weight = short_weight[:, :, None, :]
     conv_out = (
         conv_weight[:, 0] * extended[:, 2:]
@@ -98,9 +96,8 @@
         + conv_weight[:, 2] * extended[:, :-2]
     )
     query_conv, key_conv, value_conv = (conv_out[0], conv_out[1], conv_out[2])
-    gated = (key_conv[:row_count] * value_conv[:row_count]).astype(jnp.bfloat16)
-    cot_wide = jnp.concatenate([cotangent, next_cot], axis=0).astype(jnp.float32)
-    grad_long = (cot_wide[:row_count] * query_conv[:row_count]).astype(jnp.bfloat16)
+    gated = (key_conv * value_conv).astype(jnp.bfloat16)
+    grad_long = (cotangent.astype(jnp.float32) * query_conv).astype(jnp.bfloat16)
 
     both_cols = swap_layout(
         jnp.concatenate(
@@ -109,6 +106,22 @@
         )
     )
     gated_cols, grad_long_cols = (both_cols[..., :group], both_cols[..., group:])
+
+    after_rows, _ = lax.optimization_barrier(
+        (jnp.concatenate([streams[:, :2], cotangent[None, :2]], axis=0), both_cols)
+    )
+    after = neighbour_rows(after_rows, -1)
+    next_streams, next_cot = (after[:3], after[3])
+    edge = jnp.concatenate([streams[:, row_count - 2 :], next_streams], axis=1).astype(jnp.float32)
+    edge_out = (
+        conv_weight[:, 0] * edge[:, 2:]
+        + conv_weight[:, 1] * edge[:, 1:-1]
+        + conv_weight[:, 2] * edge[:, :-2]
+    )
+    query_conv = jnp.concatenate([query_conv, edge_out[0]], axis=0)
+    key_conv = jnp.concatenate([key_conv, edge_out[1]], axis=0)
+    value_conv = jnp.concatenate([value_conv, edge_out[2]], axis=0)
+    cot_wide = jnp.concatenate([cotangent, next_cot], axis=0).astype(jnp.float32)
     own_spec = jnp.einsum(
         "tbc,kt->bck", gated_cols, half_table, preferred_element_type=jnp.float32
     ).astype(jnp.bfloat16)

time: 128 us -> 122 us (0.953)
  local copies, waits for them, and re-layouts: 33.5 us -> 28.4 us
  other arithmetic: 18.6 us -> 21.8 us
  starting transfers between devices: 28.8 us -> 27.2 us
    all_to_all x2, waiting for transfers between devices: 22.1 us -> 16.2 us  [swap_layout(): return lax.all_to_all(values, 'seq', 1, 1, tiled=True)]
    ppermute x2, waiting for transfers between devices: 0.68 us -> 4.99 us  [passed_along(): return lax.ppermute(block, axis, route)]
    ppermute x2, starting transfers between devices: 5.84 us -> 3.86 us  [passed_along(): return lax.ppermute(block, axis, route)]
    unnamed x108 -> x124, local copies, waits for them, and re-layouts: 8.98 us -> 7.1 us
    convert_element_type x2, local copies, waits for them, and re-layouts: 3.33 us -> 1.76 us  [the longest x1 1 us: on_device(): (cotangent.astype(jnp.float32) * query_conv).astype(jnp.bfloat16)]
    mul x15, local copies, waits for them, and re-layouts: 7.95 us -> 9.25 us  [spectral_product(): real_out = left_re * right_re - jnp.where(first_row, 0.0, cross_term)]
  transfers between devices with their start and end apart: 5 -> 5, of which waited for: 4 -> 5; matrix products, arithmetic and copies ran while one was open for 18% -> 20% of each run, Pallas kernels for 0% -> 0%
where the time goes in v7:
time: 122 us; the launch traced here: 120 us
  waiting for transfers between devices  32.3 us (26%)
  local copies, waits for them, and re-layouts  28.4 us (23%)
  starting transfers between devices  27.2 us (22%)
  other arithmetic  21.8 us (18%)
  matrix products  8.83 us (7%)
  between operations  1.91 us (2%)
    all_to_all x2, waiting for transfers between devices, swap_layout(): return lax.all_to_all(values, 'seq', 1, 1, tiled=True)  16.2 us
    all_to_all x2, starting transfers between devices, swap_layout(): return lax.all_to_all(values, 'seq', 1, 1, tiled=True)  15.9 us
    all_to_all x1, waiting for transfers between devices, on_device(): gathered = lax.all_to_all(copies, 'chan', 0, 0, tiled=True)  11 us
    mul x15, local copies, waits for them, and re-layouts, spectral_product(): real_out = left_re * right_re - jnp.where(first_row, 0.0, cross_term)  9.25 us
    all_to_all x1, starting transfers between devices, on_device(): gathered = lax.all_to_all(copies, 'chan', 0, 0, tiled=True)  7.48 us
    unnamed x124, local copies, waits for them, and re-layouts  7.1 us
    another operation x4, other arithmetic  6.46 us
    dot_general x1, matrix products, on_device(): jnp.einsum('stf,sfqc->qtc', gathered, weight_parts, preferred_element_typ...  5.22 us
  transfers between devices with their start and end apart: 5, of which 5 were waited for; matrix products, arithmetic and copies ran while one was open for 20% of the time, Pallas kernels for 0%

profile of v7, /device:TPU:2, one launch (start us, length us, event | category | flops | bytes accessed | tf_op | source)
XLA Modules:
  0.0 120.4 jit_solution(6733147665631590905)
XLA Ops:
  0.6 2.6 %broadcast_in_dim.737 = bf16[16,256,256]{2,1,0:T(8,128)(2,1)} broadcast(bf16[256,256]{1,0:T(8,128)(2,1)} %param.5), dimensions={1,2} | broadcast | bytes 2228224 | tf_op jit(solution)/shard_map/broadcast_in_dim | solution.py:84
  3.3 7.5 %all-to-all-start = ((bf16[16,256,256]{2,1,0:T(8,128)(2,1)}), bf16[16,256,256]{2,1,0:T(8,128)(2,1)}, u32[]{:S(2)}, u32[]{:S(2)}) async-start(bf16[16,256,256]{2,1,0:T(8,128)(2,1)} %broadcast_in_dim.737), calls=%async_computation | async-start | bytes 4194304 | tf_op jit(solution)/shard_map/all_to_all | solution.py:85
  10.8 1.3 %constant_dynamic-slice_fusion = bf16[3840,16]{1,0:T(8,128)(2,1)} fusion(bf16[4096,256]{1,0:T(8,128)(2,1)S(1)} %copy-done, s32[]{:T(128)S(6)} %select_n.380), kind=kLoop, calls=%fused_computation.469 | loop fusion | bytes 245764 | tf_op jit(solution)/shard_map/slice | solution.py:131
  13.4 1.5 %copy.15 = bf16[15,256,16]{1,2,0:T(8,128)(2,1)S(1)} copy(bf16[15,256,16]{2,1,0:T(8,128)(2,1)} %bitcast.167) | data formatting | bytes 245760 | tf_op jit(solution)/shard_map/slice | solution.py:131
  15.2 2.1 %negate_select_fusion.2 = (f32[256,512]{1,0:T(8,128)S(1)}, f32[256,512]{1,0:T(8,128)S(1)}) fusion(f32[512]{0:T(512)S(1)} %fusion.97, pred[256]{0:T(512)(128)(4,1)S(1)} %iota_compare_fusion.36), kind=kLoop, calls=%fused_computation.143 | loop fusion | flops 2097152 | bytes 1050880 | tf_op jit(solution)/shard_map/jit(_where)/select_n | solution.py:23
  28.3 11.0 %all-to-all-done = bf16[16,256,256]{2,1,0:T(8,128)(2,1)} async-done(((bf16[16,256,256]{2,1,0:T(8,128)(2,1)}), bf16[16,256,256]{2,1,0:T(8,128)(2,1)}, u32[]{:S(2)}, u32[]{:S(2)}) %all-to-all-start) | async-done | bytes 2097184 | tf_op jit(solution)/shard_map/all_to_all | solution.py:85
  39.4 5.2 %fusion.8 = bf16[3,256,256]{2,1,0:T(8,128)(2,1)S(1)} fusion(bf16[16,256,3,256]{3,1,0,2:T(8,128)(2,1)} %bitcast.175, bf16[16,256,256]{2,1,0:T(8,128)(2,1)} %all-to-all-done), kind=kOutput, calls=%fused_computation.9 | convolution fusion | flops 1610809344 | bytes 8781824 | tf_op jit(solution)/shard_map/stf,sfqc->qtc/dot_general | solution.py:87
  45.2 2.6 %collective-permute-start = (bf16[3,2,256]{2,1,0:T(2,128)(2,1)S(1)}, bf16[3,2,256]{2,1,0:T(2,128)(2,1)S(1)}, u32[]{:S(2)}, u32[]{:S(2)}) collective-permute-start(bf16[3,2,256]{2,1,0:T(2,128)(2,1)S(1)} %get-tuple-element.85), channel_id=1, source_target_pairs={{0,16},{16,32},{32,48},{48,64},{64,80},{80,96},{96,112},{112,128},... | collective-permute-start | bytes 9224 | tf_op jit(solution)/shard_map/ppermute | solution.py:12
  48.4 0.7 collective-permute-done
  49.4 0.8 fusion.146
  51.2 1.0 copy.19
  52.2 0.8 copy.18
  53.0 1.6 %pad_maximum_fusion.2 = bf16[256,16,32]{0,2,1:T(8,128)(2,1)} fusion(bf16[256,16,16]{0,2,1:T(8,128)(2,1)S(1)} %bitcast.169, bf16[256,16,16]{0,2,1:T(8,128)(2,1)} %bitcast.170), kind=kLoop, calls=%fused_computation.178 | loop fusion | flops 524288 | bytes 524288 | tf_op jit(solution)/shard_map/concatenate | solution.py:103
  54.6 12.3 %all-to-all-start.1 = ((bf16[256,16,32]{0,2,1:T(8,128)(2,1)}), bf16[256,16,32]{0,2,1:T(8,128)(2,1)S(1)}, u32[]{:S(2)}, u32[]{:S(2)}) async-start(bf16[256,16,32]{0,2,1:T(8,128)(2,1)} %pad_maximum_fusion.2), calls=%async_computation.1 | async-start | bytes 524288 | tf_op jit(solution)/shard_map/all_to_all | solution.py:70
  66.9 2.4 %select_convert_fusion = bf16[256,256]{1,0:T(8,128)(2,1)} fusion(bf16[256]{0:T(256)(128)(2,1)S(1)} %fusion.134, s32[256]{0:T(256)} %iota_add_fusion, pred[256]{0:T(512)(128)(4,1)S(1)} %iota_compare_fusion.36), kind=kLoop, calls=%fused_computation.190 | loop fusion | flops 1048576 | bytes 132864 | tf_op jit(solution)/shard_map/convert.9
  69.3 2.4 %multiply_convert_fusion.4 = bf16[256,256]{1,0:T(8,128)(2,1)} fusion(f32[256]{0:T(256)} %select_multiply_fusion, s32[256]{0:T(256)} %iota_add_fusion), kind=kLoop, calls=%fused_computation.191 | loop fusion | flops 1048576 | bytes 133120 | tf_op jit(solution)/shard_map/convert.8
  71.7 6.3 %all-to-all-done.1 = bf16[256,16,32]{0,2,1:T(8,128)(2,1)S(1)} async-done(((bf16[256,16,32]{0,2,1:T(8,128)(2,1)}), bf16[256,16,32]{0,2,1:T(8,128)(2,1)S(1)}, u32[]{:S(2)}, u32[]{:S(2)}) %all-to-all-start.1) | async-done | bytes 262176 | tf_op jit(solution)/shard_map/all_to_all | solution.py:70
  78.0 1.3 %fusion.152 = (f32[16,16,512]{2,1,0:T(8,128)S(1)}, bf16[16,16,512]{2,1,0:T(8,128)(2,1)S(1)}) fusion(bf16[512,512]{1,0:T(8,128)(2,1)} %copy-done.2, bf16[256,16,32]{0,2,1:T(8,128)(2,1)S(1)} %all-to-all-done.1), kind=kOutput, calls=%fused_computation.487 | convolution fusion | flops 67371008 | bytes 1179648 | tf_op jit(solution)/shard_map/tbc,kt->bck/dot_general | solution.py:125
  88.0 1.1 fusion.19
  89.2 0.9 copy-done.3
  90.9 0.9 fusion.27
  91.8 3.6 %all-to-all-start.2 = ((bf16[258,16,48]{0,2,1:T(8,128)(2,1)}), bf16[258,16,48]{0,2,1:T(8,128)(2,1)S(1)}, u32[]{:S(2)}, u32[]{:S(2)}) async-start(bf16[258,16,48]{0,2,1:T(8,128)(2,1)} %fusion.27), calls=%async_computation.2 | async-start | bytes 1179648 | tf_op jit(solution)/shard_map/all_to_all | solution.py:70
  95.5 1.3 %collective-permute-start.1 = (bf16[4,2,256]{2,1,0:T(2,128)(2,1)S(1)}, bf16[4,2,256]{2,1,0:T(2,128)(2,1)S(1)}, u32[]{:S(2)}, u32[]{:S(2)}) collective-permute-start(bf16[4,2,256]{2,1,0:T(2,128)(2,1)S(1)} %pad_maximum_fusion.3), channel_id=1, source_target_pairs={{16,0},{32,16},{48,32},{64,48},{80,64},{96,80},{112,96},{128,112},... | collective-permute-start | bytes 12296 | tf_op jit(solution)/shard_map/ppermute | solution.py:12
  96.8 4.3 %collective-permute-done.1 = bf16[4,2,256]{2,1,0:T(2,128)(2,1)S(1)} collective-permute-done((bf16[4,2,256]{2,1,0:T(2,128)(2,1)S(1)}, bf16[4,2,256]{2,1,0:T(2,128)(2,1)S(1)}, u32[]{:S(2)}, u32[]{:S(2)}) %collective-permute-start.1) | collective-permute-done | bytes 4128 | tf_op jit(solution)/shard_map/ppermute | solution.py:12
  102.3 9.9 %all-to-all-done.2 = bf16[258,16,48]{0,2,1:T(8,128)(2,1)S(1)} async-done(((bf16[258,16,48]{0,2,1:T(8,128)(2,1)}), bf16[258,16,48]{0,2,1:T(8,128)(2,1)S(1)}, u32[]{:S(2)}, u32[]{:S(2)}) %all-to-all-start.2) | async-done | bytes 396320 | tf_op jit(solution)/shard_map/all_to_all | solution.py:70
  113.1 1.6 %multiply_convert_fusion.1 = bf16[256,256]{1,0:T(8,128)(2,1)} fusion(f32[256,256]{1,0:T(8,128)S(1)} %copy.20, f32[3,256,256]{2,1,0:T(8,128)} %copy-done.1), kind=kLoop, calls=%fused_computation.180 | loop fusion | flops 131072 | bytes 655360 | tf_op jit(solution)/shard_map/convert_element_type | solution.py:192
  114.7 0.7 fusion.148
  115.6 1.0 bitcast_convert_fusion
  116.7 0.9 multiply_convert_fusion
  117.7 0.7 fusion.72
  118.6 1.0 fusion.71
  119.6 0.8 copy.24
  (237 shorter events, 26.3 us)
Async XLA Ops:
  0.6 10.1 %copy-start = (bf16[4096,256]{1,0:T(8,128)(2,1)S(1)}, bf16[4096,256]{1,0:T(8,128)(2,1)}, u32[]{:S(2)}) copy-start(bf16[4096,256]{1,0:T(8,128)(2,1)} %param.8) | copy-start | bytes 6291460
  3.3 36.1 %all-to-all-start = ((bf16[16,256,256]{2,1,0:T(8,128)(2,1)}), bf16[16,256,256]{2,1,0:T(8,128)(2,1)}, u32[]{:S(2)}, u32[]{:S(2)}) async-start(bf16[16,256,256]{2,1,0:T(8,128)(2,1)} %broadcast_in_dim.737), calls=%async_computation | async-start | bytes 4194304 | tf_op jit(solution)/shard_map/all_to_all | solution.py:85
  17.5 2.3 %copy-start.2 = (bf16[512,512]{1,0:T(8,128)(2,1)}, bf16[512,512]{1,0:T(8,128)(2,1)S(1)}, u32[]{:S(2)}) copy-start(bf16[512,512]{1,0:T(8,128)(2,1)S(1)} %fusion.21) | copy-start | bytes 1572868
  17.5 5.3 %copy-start.48 = (f32[3,1,1,256]{3,1,0,2:T(1,128)S(1)}, f32[3,1,1,256]{3,1,0,2:T(1,128)}, u32[]{:S(2)}) copy-start(f32[3,1,1,256]{3,1,0,2:T(1,128)} %get-tuple-element.228) | copy-start | bytes 9220
  22.8 78.8 %copy-start.11 = (f32[3,256]{1,0:T(4,128)}, f32[3,256]{1,0:T(4,128)S(1)}, u32[]{:S(2)}) copy-start(f32[3,256]{1,0:T(4,128)S(1)} %get-tuple-element.237) | copy-start | bytes 9220
  22.8 78.8 %copy-start.13 = (f32[3,256]{1,0:T(4,128)}, f32[3,256]{1,0:T(4,128)S(1)}, u32[]{:S(2)}) copy-start(f32[3,256]{1,0:T(4,128)S(1)} %get-tuple-element.238) | copy-start | bytes 9220
  39.4 9.0 %copy-start.47 = (f32[3,1,1,256]{3,1,0,2:T(1,128)S(1)}, f32[3,1,1,256]{3,1,0,2:T(1,128)}, u32[]{:S(2)}) copy-start(f32[3,1,1,256]{3,1,0,2:T(1,128)} %get-tuple-element.226) | copy-start | bytes 9220
  45.2 4.0 %copy-start.49 = (bf16[3,2,256]{2,1,0:T(2,128)(2,1)}, bf16[3,2,256]{2,1,0:T(2,128)(2,1)S(1)}, u32[]{:S(2)}) copy-start(bf16[3,2,256]{2,1,0:T(2,128)(2,1)S(1)} %get-tuple-element.85) | copy-start | bytes 9220
  45.2 3.9 %collective-permute-start = (bf16[3,2,256]{2,1,0:T(2,128)(2,1)S(1)}, bf16[3,2,256]{2,1,0:T(2,128)(2,1)S(1)}, u32[]{:S(2)}, u32[]{:S(2)}) collective-permute-start(bf16[3,2,256]{2,1,0:T(2,128)(2,1)S(1)} %get-tuple-element.85), channel_id=1, source_target_pairs={{0,16},{16,32},{32,48},{48,64},{64,80},{80,96},{96,112},{112,128},... | collective-permute-start | bytes 9224 | tf_op jit(solution)/shard_map/ppermute | solution.py:12
  48.4 53.3 %copy-start.15 = (f32[3,1,1,256]{3,0,1,2:T(4,128)}, f32[3,1,1,256]{3,0,1,2:T(4,128)S(1)}, u32[]{:S(2)}) copy-start(f32[3,1,1,256]{3,0,1,2:T(4,128)S(1)} %copy.36) | copy-start | bytes 9220
  49.4 1.1 copy-start.1
  49.4 1.1 copy-start.6
  54.6 23.4 %all-to-all-start.1 = ((bf16[256,16,32]{0,2,1:T(8,128)(2,1)}), bf16[256,16,32]{0,2,1:T(8,128)(2,1)S(1)}, u32[]{:S(2)}, u32[]{:S(2)}) async-start(bf16[256,16,32]{0,2,1:T(8,128)(2,1)} %pad_maximum_fusion.2), calls=%async_computation.1 | async-start | bytes 524288 | tf_op jit(solution)/shard_map/all_to_all | solution.py:70
  78.0 1.4 %copy-start.7 = (bf16[256,256]{1,0:T(8,128)(2,1)S(1)}, bf16[256,256]{1,0:T(8,128)(2,1)}, u32[]{:S(2)}) copy-start(bf16[256,256]{1,0:T(8,128)(2,1)} %select_convert_fusion) | copy-start | bytes 393220
  78.0 1.4 %copy-start.8 = (bf16[256,256]{1,0:T(8,128)(2,1)S(1)}, bf16[256,256]{1,0:T(8,128)(2,1)}, u32[]{:S(2)}) copy-start(bf16[256,256]{1,0:T(8,128)(2,1)} %multiply_convert_fusion.4) | copy-start | bytes 393220
  84.1 0.8 copy-start.25
  84.1 0.8 copy-start.26
  86.7 0.7 copy-start.41
  86.8 0.7 copy-start.42
  87.2 0.7 copy-start.40
  88.0 1.2 copy-start.10
  89.1 1.0 copy-start.3
  90.9 4.5 %copy-start.51 = (bf16[3,2,256]{2,1,0:T(2,128)(2,1)S(1)}, bf16[3,2,256]{2,1,0:T(2,128)(2,1)}, u32[]{:S(2)}) copy-start(bf16[3,2,256]{2,1,0:T(2,128)(2,1)} %get-tuple-element.84) | copy-start | bytes 9220
  90.9 10.7 %copy-start.50 = (bf16[3,2,256]{2,1,0:T(2,128)(2,1)S(1)}, bf16[3,2,256]{2,1,0:T(2,128)(2,1)}, u32[]{:S(2)}) copy-start(bf16[3,2,256]{2,1,0:T(2,128)(2,1)} %copy-done.49) | copy-start | bytes 9220
  91.8 20.4 %all-to-all-start.2 = ((bf16[258,16,48]{0,2,1:T(8,128)(2,1)}), bf16[258,16,48]{0,2,1:T(8,128)(2,1)S(1)}, u32[]{:S(2)}, u32[]{:S(2)}) async-start(bf16[258,16,48]{0,2,1:T(8,128)(2,1)} %fusion.27), calls=%async_computation.2 | async-start | bytes 1179648 | tf_op jit(solution)/shard_map/all_to_all | solution.py:70
  95.5 5.6 %collective-permute-start.1 = (bf16[4,2,256]{2,1,0:T(2,128)(2,1)S(1)}, bf16[4,2,256]{2,1,0:T(2,128)(2,1)S(1)}, u32[]{:S(2)}, u32[]{:S(2)}) collective-permute-start(bf16[4,2,256]{2,1,0:T(2,128)(2,1)S(1)} %pad_maximum_fusion.3), channel_id=1, source_target_pairs={{16,0},{32,16},{48,32},{64,48},{80,64},{96,80},{112,96},{128,112},... | collective-permute-start | bytes 12296 | tf_op jit(solution)/shard_map/ppermute | solution.py:12
  115.5 2.2 %copy-start.4 = (f32[1,256,256]{2,1,0:T(8,128)S(1)}, f32[1,256,256]{2,1,0:T(8,128)}, u32[]{:S(2)}) copy-start(f32[1,256,256]{2,1,0:T(8,128)} %get-tuple-element.21) | copy-start | bytes 786436
  115.5 2.2 %copy-start.5 = (f32[1,256,256]{2,1,0:T(8,128)S(1)}, f32[1,256,256]{2,1,0:T(8,128)}, u32[]{:S(2)}) copy-start(f32[1,256,256]{2,1,0:T(8,128)} %get-tuple-element.23) | copy-start | bytes 786436
  117.7 0.9 copy-start.12
  117.7 0.9 copy-start.14
  117.7 0.9 copy-start.16
  118.6 1.0 copy-start.9
  (26 other events, 18.8 us)

commit v8 on v7

--- a/solution.py
+++ b/solution.py
@@ -87,41 +87,67 @@
     streams = jnp.einsum(
         "stf,sfqc->qtc", gathered, weight_parts, preferred_element_type=jnp.float32
     ).astype(jnp.bfloat16)
-    before = neighbour_rows(streams[:, row_count - 2 :], 1)
-    extended = jnp.concatenate([before, streams], axis=1).astype(jnp.float32)
     conv_weight = short_weight[:, :, None, :]
-    conv_out = (
-        conv_weight[:, 0] * extended[:, 2:]
-        + conv_weight[:, 1] * extended[:, 1:-1]
-        + conv_weight[:, 2] * extended[:, :-2]
-    )
+
+    def short_conv(rows):
+        return (
+            conv_weight[:, 0] * rows[:, 2:]
+            + conv_weight[:, 1] * rows[:, 1:-1]
+            + conv_weight[:, 2] * rows[:, :-2]
+        )
+
+    lead = jnp.zeros((3, 2, local_width), jnp.bfloat16)
+    conv_out = short_conv(jnp.concatenate([lead, streams], axis=1).astype(jnp.float32))
     query_conv, key_conv, value_conv = (conv_out[0], conv_out[1], conv_out[2])
     gated = (key_conv * value_conv).astype(jnp.bfloat16)
     grad_long = (cotangent.astype(jnp.float32) * query_conv).astype(jnp.bfloat16)
+    edge_rows = jnp.concatenate([streams[:, :2], streams[:, row_count - 2 :]], axis=1)
+    edge_rows = edge_rows.reshape(12, local_width)
+    plane_a = jnp.concatenate([gated, edge_rows], axis=0)
+    plane_b = jnp.concatenate(
+        [grad_long, cotangent[:2], jnp.zeros((10, local_width), jnp.bfloat16)], axis=0
+    )
+    wide_in = row_count + 12
 
     both_cols = swap_layout(
         jnp.concatenate(
-            [gated.reshape(row_count, seq_count, group), grad_long.reshape(row_count, seq_count, group)],
+            [plane_a.reshape(wide_in, seq_count, group), plane_b.reshape(wide_in, seq_count, group)],
             axis=2,
         )
     )
-    gated_cols, grad_long_cols = (both_cols[..., :group], both_cols[..., group:])
-
-    after_rows, _ = lax.optimization_barrier(
-        (jnp.concatenate([streams[:, :2], cotangent[None, :2]], axis=0), both_cols)
-    )
-    after = neighbour_rows(after_rows, -1)
+    own_weight = lax.dynamic_slice_in_dim(short_weight, own_block * group, group, axis=2)
+    edge_cols = both_cols[row_count:, :, :group].reshape(3, 4, seq_count, group).astype(jnp.float32)
+    first, second = (edge_cols[:, 0], edge_cols[:, 1])
+    zero_block = jnp.zeros((3, 1, group), jnp.float32)
+    last_but_one = jnp.concatenate([zero_block, edge_cols[:, 2, :-1]], axis=1)
+    last = jnp.concatenate([zero_block, edge_cols[:, 3, :-1]], axis=1)
+    cols_weight = own_weight[:, :, None, :]
+    head0 = cols_weight[:, 0] * first + cols_weight[:, 1] * last + cols_weight[:, 2] * last_but_one
+    head1 = cols_weight[:, 0] * second + cols_weight[:, 1] * first + cols_weight[:, 2] * last
+    head = jnp.stack([head0, head1], axis=1)
+    head_cot = both_cols[row_count : row_count + 2, :, group:].astype(jnp.float32)
+    gated_cols = jnp.concatenate(
+        [(head[1] * head[2]).astype(jnp.bfloat16), both_cols[2:row_count, :, :group]], axis=0
+    )
+    grad_long_cols = jnp.concatenate(
+        [(head_cot * head[0]).astype(jnp.bfloat16), both_cols[2:row_count, :, group:]], axis=0
+    )
+
+    edge_send, _ = lax.optimization_barrier(
+        ((streams[:, row_count - 2 :], jnp.concatenate([streams[:, :2], cotangent[None, :2]], axis=0)), both_cols)
+    )
+    before = neighbour_rows(edge_send[0], 1)
+    after = neighbour_rows(edge_send[1], -1)
     next_streams, next_cot = (after[:3], after[3])
-    edge = jnp.concatenate([streams[:, row_count - 2 :], next_streams], axis=1).astype(jnp.float32)
-    edge_out = (
-        conv_weight[:, 0] * edge[:, 2:]
-        + conv_weight[:, 1] * edge[:, 1:-1]
-        + conv_weight[:, 2] * edge[:, :-2]
-    )
-    query_conv = jnp.concatenate([query_conv, edge_out[0]], axis=0)
-    key_conv = jnp.concatenate([key_conv, edge_out[1]], axis=0)
-    value_conv = jnp.concatenate([value_conv, edge_out[2]], axis=0)
+    fixed = short_conv(jnp.concatenate([before, streams[:, :2]], axis=1).astype(jnp.float32))
+    edge_out = short_conv(
+        jnp.concatenate([streams[:, row_count - 2 :], next_streams], axis=1).astype(jnp.float32)
+    )
+    query_conv = jnp.concatenate([fixed[0], query_conv[2:], edge_out[0]], axis=0)
+    key_conv = jnp.concatenate([fixed[1], key_conv[2:], edge_out[1]], axis=0)
+    value_conv = jnp.concatenate([fixed[2], value_conv[2:], edge_out[2]], axis=0)
     cot_wide = jnp.concatenate([cotangent, next_cot], axis=0).astype(jnp.float32)
+
     own_spec = jnp.einsum(
         "tbc,kt->bck", gated_cols, half_table, preferred_element_type=jnp.float32
     ).astype(jnp.bfloat16)

time: 122 us -> 137 us (1.12)
  local copies, waits for them, and re-layouts: 28.4 us -> 45.6 us
  starting transfers between devices: 27.2 us -> 24.6 us
  waiting for transfers between devices: 32.3 us -> 30.1 us
    all_to_all x1, waiting for transfers between devices: 11 us -> 3.84 us  [on_device(): gathered = lax.all_to_all(copies, 'chan', 0, 0, tiled=True)]
    slice x2 -> x8, local copies, waits for them, and re-layouts: 1.18 us -> 7.43 us  [the longest x1 1.81 us: on_device(): both_cols[2:row_count, :, :group]]
    all_to_all x2, waiting for transfers between devices: 16.2 us -> 22.1 us  [swap_layout(): return lax.all_to_all(values, 'seq', 1, 1, tiled=True)]
    unnamed x124 -> x162, local copies, waits for them, and re-layouts: 7.1 us -> 12.9 us
    all_to_all x2, starting transfers between devices: 15.9 us -> 13.3 us  [swap_layout(): return lax.all_to_all(values, 'seq', 1, 1, tiled=True)]
    concatenate x0 -> x4, local copies, waits for them, and re-layouts: none -> 2.36 us  [the longest x2 1.46 us: on_device(): jnp.concatenate([grad_long, cotangent[:2], jnp.zeros((10, local_width), j...]
    convert_element_type x1 -> x6, other arithmetic: 0.08 us -> 2.13 us  [the longest x1 1.33 us: on_device(): (head_cot * head[0]).astype(jnp.bfloat16)]
    convert_element_type x15, other arithmetic: 0.35 us -> 1.96 us  [spectral_product(): right_spec = right_spec.astype(jnp.float32)]
  transfers between devices with their start and end apart: 5 -> 5, of which waited for: 5 -> 4; matrix products, arithmetic and copies ran while one was open for 20% -> 22% of each run, Pallas kernels for 0% -> 0%
where the time goes in v8:
time: 137 us; the launch traced here: 135 us
  local copies, waits for them, and re-layouts  45.6 us (33%)
  waiting for transfers between devices  30.1 us (22%)
  starting transfers between devices  24.6 us (18%)
  other arithmetic  22.7 us (17%)
  matrix products  9.87 us (7%)
  between operations  2.05 us (1%)
    all_to_all x2, waiting for transfers between devices, swap_layout(): return lax.all_to_all(values, 'seq', 1, 1, tiled=True)  22.1 us
    all_to_all x2, starting transfers between devices, swap_layout(): return lax.all_to_all(values, 'seq', 1, 1, tiled=True)  13.3 us
    unnamed x162, local copies, waits for them, and re-layouts  12.9 us
    mul x15, local copies, waits for them, and re-layouts, spectral_product(): real_out = left_re * right_re - jnp.where(first_row, 0.0, cross_term)  9.1 us
    all_to_all x1, starting transfers between devices, on_device(): gathered = lax.all_to_all(copies, 'chan', 0, 0, tiled=True)  7.48 us
    another operation x4, other arithmetic  5.42 us
    dot_general x1, matrix products, on_device(): jnp.einsum('stf,sfqc->qtc', gathered, weight_parts, preferred_element_typ...  5.21 us
    ppermute x2, waiting for transfers between devices, passed_along(): return lax.ppermute(block, axis, route)  4.17 us
  transfers between devices with their start and end apart: 5, of which 4 were waited for; matrix products, arithmetic and copies ran while one was open for 22% of the time, Pallas kernels for 0%

profile of v8, /device:TPU:2, one launch (start us, length us, event | category | flops | bytes accessed | tf_op | source)
XLA Modules:
  0.0 135.0 jit_solution(395577871020372832)
XLA Ops:
  0.6 2.6 %broadcast_in_dim.745 = bf16[16,256,256]{2,1,0:T(8,128)(2,1)} broadcast(bf16[256,256]{1,0:T(8,128)(2,1)} %param.5), dimensions={1,2} | broadcast | bytes 2228224 | tf_op jit(solution)/shard_map/broadcast_in_dim | solution.py:84
  3.3 7.5 %all-to-all-start = ((bf16[16,256,256]{2,1,0:T(8,128)(2,1)}), bf16[16,256,256]{2,1,0:T(8,128)(2,1)}, u32[]{:S(2)}, u32[]{:S(2)}) async-start(bf16[16,256,256]{2,1,0:T(8,128)(2,1)} %broadcast_in_dim.745), calls=%async_computation | async-start | bytes 4194304 | tf_op jit(solution)/shard_map/all_to_all | solution.py:85
  10.8 1.3 constant_dynamic-slice_fusion
  14.9 2.2 %copy.115 = bf16[15,256,16]{1,2,0:T(8,128)(2,1)} copy(bf16[15,256,16]{2,1,0:T(8,128)(2,1)} %bitcast.220) | data formatting | bytes 245760 | tf_op jit(solution)/shard_map/slice | solution.py:157
  17.1 1.0 copy.117
  18.1 2.1 %negate_select_fusion.2 = (f32[256,512]{1,0:T(8,128)S(1)}, f32[256,512]{1,0:T(8,128)S(1)}) fusion(f32[512]{0:T(512)S(1)} %fusion.119, pred[256]{0:T(512)(128)(4,1)S(1)} %iota_compare_fusion.36), kind=kLoop, calls=%fused_computation.143 | loop fusion | flops 2097152 | bytes 1050880 | tf_op jit(solution)/shard_map/jit(_where)/select_n | solution.py:23
  32.1 1.7 %select_convert_fusion = bf16[256,256]{1,0:T(8,128)(2,1)} fusion(bf16[256]{0:T(256)(128)(2,1)S(1)} %fusion.156, s32[256]{0:T(256)S(1)} %copy-done.66, pred[256]{0:T(512)(128)(4,1)S(1)} %iota_compare_fusion.36), kind=kLoop, calls=%fused_computation.194 | loop fusion | flops 1048576 | bytes 132864 | tf_op jit(solution)/shard_map/convert.10
  33.8 1.7 %multiply_convert_fusion.1 = bf16[256,256]{1,0:T(8,128)(2,1)} fusion(f32[256]{0:T(256)S(1)} %select_multiply_fusion, s32[256]{0:T(256)S(1)} %copy-done.66), kind=kLoop, calls=%fused_computation.195 | loop fusion | flops 1048576 | bytes 133120 | tf_op jit(solution)/shard_map/convert.9
  35.5 3.8 %all-to-all-done = bf16[16,256,256]{2,1,0:T(8,128)(2,1)} async-done(((bf16[16,256,256]{2,1,0:T(8,128)(2,1)}), bf16[16,256,256]{2,1,0:T(8,128)(2,1)}, u32[]{:S(2)}, u32[]{:S(2)}) %all-to-all-start) | async-done | bytes 2097184 | tf_op jit(solution)/shard_map/all_to_all | solution.py:85
  39.4 5.2 %fusion.8 = bf16[3,256,256]{2,1,0:T(8,128)(2,1)S(1)} fusion(bf16[16,256,3,256]{3,1,0,2:T(8,128)(2,1)} %bitcast.230, bf16[16,256,256]{2,1,0:T(8,128)(2,1)} %all-to-all-done), kind=kOutput, calls=%fused_computation.9 | convolution fusion | flops 1610809344 | bytes 8781824 | tf_op jit(solution)/shard_map/stf,sfqc->qtc/dot_general | solution.py:87
  48.9 1.0 copy.111
  49.9 1.7 %pad_maximum_fusion.2 = bf16[268,16,32]{0,2,1:T(8,128)(2,1)} fusion(bf16[268,16,16]{0,2,1:T(8,128)(2,1)} %bitcast.221, bf16[12,16,16]{0,2,1:T(8,128)(2,1)} %copy.112, bf16[256,16,16]{0,2,1:T(8,128)(2,1)S(1)} %bitcast.223), kind=kLoop, calls=%fused_computation.154 | loop fusion | flops 823296 | bytes 548864 | tf_op jit(solution)/shard_map/concatenate | solution.py:113
  51.6 8.7 %all-to-all-start.1 = ((bf16[268,16,32]{0,2,1:T(8,128)(2,1)}), bf16[268,16,32]{0,2,1:T(8,128)(2,1)}, u32[]{:S(2)}, u32[]{:S(2)}) async-start(bf16[268,16,32]{0,2,1:T(8,128)(2,1)} %pad_maximum_fusion.2), calls=%async_computation.1 | async-start | bytes 786432 | tf_op jit(solution)/shard_map/all_to_all | solution.py:70
  61.1 1.3 pad_maximum_fusion.5
  63.2 11.7 %all-to-all-done.1 = bf16[268,16,32]{0,2,1:T(8,128)(2,1)} async-done(((bf16[268,16,32]{0,2,1:T(8,128)(2,1)}), bf16[268,16,32]{0,2,1:T(8,128)(2,1)}, u32[]{:S(2)}, u32[]{:S(2)}) %all-to-all-start.1) | async-done | bytes 274464 | tf_op jit(solution)/shard_map/all_to_all | solution.py:70
  76.8 1.8 %fusion.172 = (bf16[254,16,16]{0,2,1:T(8,128)(2,1)S(1)}, bf16[254,16,16]{0,2,1:T(8,128)(2,1)}) fusion(bf16[268,16,32]{0,2,1:T(8,128)(2,1)} %all-to-all-done.1), kind=kLoop, calls=%fused_computation.528 | loop fusion | bytes 520192 | tf_op jit(solution)/shard_map/slice | solution.py:130
  78.7 1.2 fusion.178
  81.6 1.5 %slice.1081 = bf16[2,16,16]{0,2,1:T(8,128)(2,1)} slice(bf16[268,16,32]{0,2,1:T(8,128)(2,1)} %all-to-all-done.1), slice={[256:258], [0:16], [16:32]} | slice | bytes 2048 | tf_op jit(solution)/shard_map/slice | solution.py:128
  83.1 1.6 %copy.145 = bf16[2,16,16]{2,1,0:T(8,128)(2,1)} copy(bf16[2,16,16]{0,2,1:T(8,128)(2,1)} %slice.1081) | data formatting | bytes 2048
  84.7 1.3 fusion.111
  86.0 1.5 %copy.124 = bf16[2,16,16]{0,2,1:T(8,128)(2,1)} copy(bf16[2,16,16]{2,1,0:T(8,128)(2,1)} %fusion.111) | data formatting | bytes 2048 | tf_op jit(solution)/shard_map/convert_element_type | solution.py:133
  87.5 1.3 fusion.179
  98.1 1.0 fusion.19
  99.3 0.9 copy-done.6
  101.8 2.6 %collective-permute-start = (bf16[3,2,256]{2,1,0:T(2,128)(2,1)S(1)}, bf16[3,2,256]{2,1,0:T(2,128)(2,1)S(1)}, u32[]{:S(2)}, u32[]{:S(2)}) collective-permute-start(bf16[3,2,256]{2,1,0:T(2,128)(2,1)S(1)} %copy-done.58), channel_id=1, source_target_pairs={{0,16},{16,32},{32,48},{48,64},{64,80},{80,96},{96,112},{112,128},... | collective-permute-start | bytes 9224 | tf_op jit(solution)/shard_map/ppermute | solution.py:12
  105.2 4.6 %all-to-all-start.2 = ((bf16[258,16,48]{0,2,1:T(8,128)(2,1)}), bf16[258,16,48]{0,2,1:T(8,128)(2,1)S(1)}, u32[]{:S(2)}, u32[]{:S(2)}) async-start(bf16[258,16,48]{0,2,1:T(8,128)(2,1)} %fusion.27), calls=%async_computation.2 | async-start | bytes 1179648 | tf_op jit(solution)/shard_map/all_to_all | solution.py:70
  109.8 1.3 collective-permute-start.1
  111.1 4.2 %collective-permute-done.1 = bf16[4,2,256]{2,1,0:T(2,128)(2,1)S(1)} collective-permute-done((bf16[4,2,256]{2,1,0:T(2,128)(2,1)S(1)}, bf16[4,2,256]{2,1,0:T(2,128)(2,1)S(1)}, u32[]{:S(2)}, u32[]{:S(2)}) %collective-permute-start.1) | collective-permute-done | bytes 4128 | tf_op jit(solution)/shard_map/ppermute | solution.py:12
  117.2 10.4 %all-to-all-done.2 = bf16[258,16,48]{0,2,1:T(8,128)(2,1)S(1)} async-done(((bf16[258,16,48]{0,2,1:T(8,128)(2,1)}), bf16[258,16,48]{0,2,1:T(8,128)(2,1)S(1)}, u32[]{:S(2)}, u32[]{:S(2)}) %all-to-all-start.2) | async-done | bytes 396320 | tf_op jit(solution)/shard_map/all_to_all | solution.py:70
  130.3 0.9 multiply_convert_fusion
  131.2 1.1 fusion.72
  132.4 1.0 fusion.71
  (296 shorter events, 41.2 us)
Async XLA Ops:
  0.6 10.1 %copy-start = (bf16[4096,256]{1,0:T(8,128)(2,1)S(1)}, bf16[4096,256]{1,0:T(8,128)(2,1)}, u32[]{:S(2)}) copy-start(bf16[4096,256]{1,0:T(8,128)(2,1)} %param.8) | copy-start | bytes 6291460
  3.3 36.1 %all-to-all-start = ((bf16[16,256,256]{2,1,0:T(8,128)(2,1)}), bf16[16,256,256]{2,1,0:T(8,128)(2,1)}, u32[]{:S(2)}, u32[]{:S(2)}) async-start(bf16[16,256,256]{2,1,0:T(8,128)(2,1)} %broadcast_in_dim.745), calls=%async_computation | async-start | bytes 4194304 | tf_op jit(solution)/shard_map/all_to_all | solution.py:85
  12.1 1.6 %copy-start.59 = (f32[3,3,256]{2,1,0:T(4,128)S(1)}, f32[3,3,256]{2,1,0:T(4,128)}, u32[]{:S(2)}) copy-start(f32[3,3,256]{2,1,0:T(4,128)} %param.7) | copy-start | bytes 27652
  18.1 2.2 %copy-start.16 = (bf16[16,256,16]{1,2,0:T(8,128)(2,1)S(1)}, bf16[16,256,16]{1,2,0:T(8,128)(2,1)}, u32[]{:S(2)}) copy-start(bf16[16,256,16]{1,2,0:T(8,128)(2,1)} %copy.117) | copy-start | bytes 393220
  18.1 2.2 %copy-start.18 = (bf16[15,256,16]{1,2,0:T(8,128)(2,1)S(1)}, bf16[15,256,16]{1,2,0:T(8,128)(2,1)}, u32[]{:S(2)}) copy-start(bf16[15,256,16]{1,2,0:T(8,128)(2,1)} %copy.115) | copy-start | bytes 368644
  20.3 1.4 %copy-start.5 = (bf16[512,512]{1,0:T(8,128)(2,1)}, bf16[512,512]{1,0:T(8,128)(2,1)S(1)}, u32[]{:S(2)}) copy-start(bf16[512,512]{1,0:T(8,128)(2,1)S(1)} %fusion.21) | copy-start | bytes 1572868
  20.3 6.8 %copy-start.61 = (f32[3,1,1,256]{3,1,0,2:T(1,128)S(1)}, f32[3,1,1,256]{3,1,0,2:T(1,128)}, u32[]{:S(2)}) copy-start(f32[3,1,1,256]{3,1,0,2:T(1,128)} %get-tuple-element.254) | copy-start | bytes 9220
  20.3 6.8 %copy-start.62 = (f32[3,1,1,256]{3,1,0,2:T(1,128)S(1)}, f32[3,1,1,256]{3,1,0,2:T(1,128)}, u32[]{:S(2)}) copy-start(f32[3,1,1,256]{3,1,0,2:T(1,128)} %get-tuple-element.255) | copy-start | bytes 9220
  20.3 6.9 %copy-start.60 = (f32[3,1,1,256]{3,1,0,2:T(1,128)S(1)}, f32[3,1,1,256]{3,1,0,2:T(1,128)}, u32[]{:S(2)}) copy-start(f32[3,1,1,256]{3,1,0,2:T(1,128)} %get-tuple-element.253) | copy-start | bytes 9220
  20.4 6.9 %copy-start.65 = (f32[3,1,1,16]{3,1,0,2:T(1,128)S(1)}, f32[3,1,1,16]{3,1,0,2:T(1,128)}, u32[]{:S(2)}) copy-start(f32[3,1,1,16]{3,1,0,2:T(1,128)} %get-tuple-element.261) | copy-start | bytes 580
  21.0 11.1 %copy-start.66 = (s32[256]{0:T(256)S(1)}, s32[256]{0:T(256)}, u32[]{:S(2)}) copy-start(s32[256]{0:T(256)} %iota_add_fusion) | copy-start | bytes 3076
  27.2 18.1 %copy-start.43 = (f32[3,256]{1,0:T(4,128)}, f32[3,256]{1,0:T(4,128)S(1)}, u32[]{:S(2)}) copy-start(f32[3,256]{1,0:T(4,128)S(1)} %get-tuple-element.271) | copy-start | bytes 9220
  27.2 88.7 %copy-start.41 = (f32[3,256]{1,0:T(4,128)}, f32[3,256]{1,0:T(4,128)S(1)}, u32[]{:S(2)}) copy-start(f32[3,256]{1,0:T(4,128)S(1)} %get-tuple-element.270) | copy-start | bytes 9220
  27.2 18.1 %copy-start.46 = (f32[3,1,1,256]{3,0,1,2:T(4,128)}, f32[3,1,1,256]{3,0,1,2:T(4,128)S(1)}, u32[]{:S(2)}) copy-start(f32[3,1,1,256]{3,0,1,2:T(4,128)S(1)} %copy.152) | copy-start | bytes 9220
  47.2 13.9 %copy-start.57 = (bf16[3,2,256]{2,1,0:T(2,128)(2,1)S(1)}, bf16[3,2,256]{2,1,0:T(2,128)(2,1)}, u32[]{:S(2)}) copy-start(bf16[3,2,256]{2,1,0:T(2,128)(2,1)} %get-tuple-element.103) | copy-start | bytes 9220
  51.6 23.3 %all-to-all-start.1 = ((bf16[268,16,32]{0,2,1:T(8,128)(2,1)}), bf16[268,16,32]{0,2,1:T(8,128)(2,1)}, u32[]{:S(2)}, u32[]{:S(2)}) async-start(bf16[268,16,32]{0,2,1:T(8,128)(2,1)} %pad_maximum_fusion.2), calls=%async_computation.1 | async-start | bytes 786432 | tf_op jit(solution)/shard_map/all_to_all | solution.py:70
  60.4 15.6 %copy-start.63 = (f32[3,1,1,16]{3,0,1,2:T(4,128)S(1)}, f32[3,1,1,16]{3,0,1,2:T(4,128)}, u32[]{:S(2)}) copy-start(f32[3,1,1,16]{3,0,1,2:T(4,128)} %copy.153) | copy-start | bytes 580
  79.9 7.6 %copy-start.11 = (bf16[256,256]{1,0:T(8,128)(2,1)S(1)}, bf16[256,256]{1,0:T(8,128)(2,1)}, u32[]{:S(2)}) copy-start(bf16[256,256]{1,0:T(8,128)(2,1)} %select_convert_fusion) | copy-start | bytes 393220
  97.0 1.0 copy-start.2
  98.1 1.1 copy-start.17
  101.4 8.3 %copy-start.69 = (bf16[4,2,256]{2,1,0:T(2,128)(2,1)S(1)}, bf16[4,2,256]{2,1,0:T(2,128)(2,1)}, u32[]{:S(2)}) copy-start(bf16[4,2,256]{2,1,0:T(2,128)(2,1)} %pad_maximum_fusion.5) | copy-start | bytes 12292
  101.8 14.2 %copy-start.44 = (f32[3,256]{1,0:T(4,128)S(1)}, f32[3,256]{1,0:T(4,128)}, u32[]{:S(2)}) copy-start(f32[3,256]{1,0:T(4,128)} %copy-done.43) | copy-start | bytes 9220
  101.8 14.2 %copy-start.47 = (f32[3,1,1,256]{3,0,1,2:T(4,128)S(1)}, f32[3,1,1,256]{3,0,1,2:T(4,128)}, u32[]{:S(2)}) copy-start(f32[3,1,1,256]{3,0,1,2:T(4,128)} %copy-done.46) | copy-start | bytes 9220
  101.8 9.3 %collective-permute-start = (bf16[3,2,256]{2,1,0:T(2,128)(2,1)S(1)}, bf16[3,2,256]{2,1,0:T(2,128)(2,1)S(1)}, u32[]{:S(2)}, u32[]{:S(2)}) collective-permute-start(bf16[3,2,256]{2,1,0:T(2,128)(2,1)S(1)} %copy-done.58), channel_id=1, source_target_pairs={{0,16},{16,32},{32,48},{48,64},{64,80},{80,96},{96,112},{112,128},... | collective-permute-start | bytes 9224 | tf_op jit(solution)/shard_map/ppermute | solution.py:12
  105.2 22.3 %all-to-all-start.2 = ((bf16[258,16,48]{0,2,1:T(8,128)(2,1)}), bf16[258,16,48]{0,2,1:T(8,128)(2,1)S(1)}, u32[]{:S(2)}, u32[]{:S(2)}) async-start(bf16[258,16,48]{0,2,1:T(8,128)(2,1)} %fusion.27), calls=%async_computation.2 | async-start | bytes 1179648 | tf_op jit(solution)/shard_map/all_to_all | solution.py:70
  109.8 5.5 %collective-permute-start.1 = (bf16[4,2,256]{2,1,0:T(2,128)(2,1)S(1)}, bf16[4,2,256]{2,1,0:T(2,128)(2,1)S(1)}, u32[]{:S(2)}, u32[]{:S(2)}) collective-permute-start(bf16[4,2,256]{2,1,0:T(2,128)(2,1)S(1)} %copy-done.69), channel_id=1, source_target_pairs={{16,0},{32,16},{48,32},{64,48},{80,64},{96,80},{112,96},{128,112},... | collective-permute-start | bytes 12296 | tf_op jit(solution)/shard_map/ppermute | solution.py:12
  129.2 2.0 %copy-start.8 = (f32[1,254,256]{2,1,0:T(8,128)S(1)}, f32[1,254,256]{2,1,0:T(8,128)}, u32[]{:S(2)}) copy-start(f32[1,254,256]{2,1,0:T(8,128)} %get-tuple-element.38) | copy-start | bytes 780292
  131.2 1.2 copy-start.42
  131.2 1.2 copy-start.45
  131.2 1.2 copy-start.48
  132.4 1.9 %copy-start.7 = (f32[254,256]{1,0:T(8,128)S(1)}, f32[254,256]{1,0:T(8,128)}, u32[]{:S(2)}) copy-start(f32[254,256]{1,0:T(8,128)} %get-tuple-element.39) | copy-start | bytes 780292
  132.4 1.9 %copy-start.64 = (f32[2,256]{1,0:T(2,128)S(1)}, f32[2,256]{1,0:T(2,128)}, u32[]{:S(2)}) copy-start(f32[2,256]{1,0:T(2,128)} %get-tuple-element.258) | copy-start | bytes 6148
  (43 other events, 34.1 us)

commit v9 on v7

--- a/solution.py
+++ b/solution.py
@@ -81,11 +81,20 @@
     half_table = full_table[:, :row_count]
     back_table = inverse.astype(jnp.bfloat16)
 
-    copies = jnp.broadcast_to(tokens[None], (chan_count,) + tokens.shape)
-    gathered = lax.all_to_all(copies, "chan", 0, 0, tiled=True)
-    weight_parts = in_weight.reshape(chan_count, local_width, 3, local_width)
-    streams = jnp.einsum(
-        "stf,sfqc->qtc", gathered, weight_parts, preferred_element_type=jnp.float32
+    half_count = chan_count // 2
+    core = lax.axis_index("chan") % 2
+    groups = [[2 * j + k for j in range(half_count)] for k in range(2)]
+    copies = jnp.broadcast_to(tokens[None], (half_count,) + tokens.shape)
+    same_core = lax.all_to_all(copies, "chan", 0, 0, tiled=True, axis_index_groups=groups)
+    other_core = lax.ppermute(same_core, "chan", [(i, i ^ 1) for i in range(chan_count)])
+    weight_pairs = in_weight.reshape(half_count, 2, local_width, 3, local_width)
+    own_weights = lax.dynamic_index_in_dim(weight_pairs, core, axis=1, keepdims=False)
+    other_weights = lax.dynamic_index_in_dim(weight_pairs, 1 - core, axis=1, keepdims=False)
+    streams = (
+        jnp.einsum("stf,sfqc->qtc", same_core, own_weights, preferred_element_type=jnp.float32)
+        + jnp.einsum(
+            "stf,sfqc->qtc", other_core, other_weights, preferred_element_type=jnp.float32
+        )
     ).astype(jnp.bfloat16)
     before = neighbour_rows(streams[:, row_count - 2 :], 1)
     extended = jnp.concatenate([before, streams], axis=1).astype(jnp.float32)

time: 122 us -> 113 us (0.926)
  waiting for transfers between devices: 32.3 us -> 24.6 us
  local copies, waits for them, and re-layouts: 28.4 us -> 26.6 us
    all_to_all x1, waiting for transfers between devices: 11 us -> 1.16 us  [on_device(): lax.all_to_all(copies, 'chan', 0, 0, tiled=True, axis_index_groups=groups)]
    all_to_all x2, waiting for transfers between devices: 16.2 us -> 18.5 us  [swap_layout(): return lax.all_to_all(values, 'seq', 1, 1, tiled=True)]
    dot_general x1 -> x2, matrix products: 5.22 us -> 6.09 us  [the longest x1 3.19 us: on_device(): jnp.einsum('stf,sfqc->qtc', same_core, own_weights, preferred_element_typ...]
    unnamed x124 -> x112, local copies, waits for them, and re-layouts: 7.1 us -> 7.1 us
  transfers between devices with their start and end apart: 5 -> 6, of which waited for: 5 -> 5; matrix products, arithmetic and copies ran while one was open for 20% -> 23% of each run, Pallas kernels for 0% -> 0%
where the time goes in v9:
time: 113 us; the launch traced here: 111 us
  starting transfers between devices  27.2 us (24%)
  local copies, waits for them, and re-layouts  26.6 us (24%)
  waiting for transfers between devices  24.6 us (22%)
  other arithmetic  21.1 us (19%)
  matrix products  9.79 us (9%)
  between operations  1.84 us (2%)
    all_to_all x2, waiting for transfers between devices, swap_layout(): return lax.all_to_all(values, 'seq', 1, 1, tiled=True)  18.5 us
    all_to_all x2, starting transfers between devices, swap_layout(): return lax.all_to_all(values, 'seq', 1, 1, tiled=True)  15.9 us
    mul x15, local copies, waits for them, and re-layouts, spectral_product(): real_out = left_re * right_re - jnp.where(first_row, 0.0, cross_term)  9.1 us
    all_to_all x1, starting transfers between devices, on_device(): lax.all_to_all(copies, 'chan', 0, 0, tiled=True, axis_index_groups=groups)  7.46 us
    unnamed x112, local copies, waits for them, and re-layouts  7.1 us
    another operation x4, other arithmetic  5.83 us
    ppermute x2, waiting for transfers between devices, passed_along(): return lax.ppermute(block, axis, route)  4.91 us
    ppermute x2, starting transfers between devices, passed_along(): return lax.ppermute(block, axis, route)  3.86 us
  transfers between devices with their start and end apart: 6, of which 5 were waited for; matrix products, arithmetic and copies ran while one was open for 23% of the time, Pallas kernels for 0%

profile of v9, /device:TPU:2, one launch (start us, length us, event | category | flops | bytes accessed | tf_op | source)
XLA Modules:
  0.0 111.1 jit_solution(14287854944775974349)
XLA Ops:
  0.6 2.1 %broadcast_in_dim.737 = bf16[8,256,256]{2,1,0:T(8,128)(2,1)} broadcast(bf16[256,256]{1,0:T(8,128)(2,1)} %param.5), dimensions={1,2} | broadcast | bytes 1179648 | tf_op jit(solution)/shard_map/broadcast_in_dim | solution.py:87
  2.7 7.5 %all-to-all-start = ((bf16[8,256,256]{2,1,0:T(8,128)(2,1)}), bf16[8,256,256]{2,1,0:T(8,128)(2,1)}, u32[]{:S(2)}, u32[]{:S(2)}) async-start(bf16[8,256,256]{2,1,0:T(8,128)(2,1)} %broadcast_in_dim.737), calls=%async_computation | async-start | bytes 2097152 | tf_op jit(solution)/shard_map/all_to_all | solution.py:88
  10.2 1.3 %constant_dynamic-slice_fusion = bf16[3840,16]{1,0:T(8,128)(2,1)} fusion(bf16[4096,256]{1,0:T(8,128)(2,1)S(1)} %copy-done, s32[]{:T(128)S(6)} %select_n.396), kind=kLoop, calls=%fused_computation.477 | loop fusion | bytes 245764 | tf_op jit(solution)/shard_map/slice | solution.py:140
  12.8 1.5 %copy.19 = bf16[15,256,16]{1,2,0:T(8,128)(2,1)S(1)} copy(bf16[15,256,16]{2,1,0:T(8,128)(2,1)} %bitcast.188) | data formatting | bytes 245760 | tf_op jit(solution)/shard_map/slice | solution.py:140
  14.6 2.1 %negate_select_fusion.2 = (f32[256,512]{1,0:T(8,128)S(1)}, f32[256,512]{1,0:T(8,128)S(1)}) fusion(f32[512]{0:T(512)S(1)} %fusion.109, pred[256]{0:T(512)(128)(4,1)S(1)} %iota_compare_fusion.36), kind=kLoop, calls=%fused_computation.151 | loop fusion | flops 2097152 | bytes 1050880 | tf_op jit(solution)/shard_map/jit(_where)/select_n | solution.py:23
  25.2 1.2 %all-to-all-done = bf16[8,256,256]{2,1,0:T(8,128)(2,1)} async-done(((bf16[8,256,256]{2,1,0:T(8,128)(2,1)}), bf16[8,256,256]{2,1,0:T(8,128)(2,1)}, u32[]{:S(2)}, u32[]{:S(2)}) %all-to-all-start) | async-done | bytes 1048608 | tf_op jit(solution)/shard_map/all_to_all | solution.py:88
  28.8 3.2 %fusion.6 = f32[3,256,256]{1,2,0:T(8,128)S(1)} fusion(bf16[8,2,256,3,256]{4,2,1,0,3:T(8,128)(2,1)} %bitcast.196, s32[]{:T(128)S(6)} %select_n.390, bf16[8,256,256]{2,1,0:T(8,128)(2,1)} %all-to-all-done), kind=kOutput, calls=%fused_computation.8 | convolution fusion | flops 805306368 | bytes 4980740 | tf_op jit(solution)/shard_map/stf,sfqc->qtc/dot_general | solution.py:94
  32.0 2.9 %fusion.18 = bf16[3,256,256]{2,1,0:T(8,128)(2,1)S(1)} fusion(f32[3,256,256]{1,2,0:T(8,128)S(1)} %fusion.6, bf16[8,2,256,3,256]{4,2,1,0,3:T(8,128)(2,1)} %bitcast.197, s32[]{:T(128)S(6)} %select_n.391, bf16[8,256,256]{2,1,0:T(8,128)(2,1)S(1)} %collective-permute-done), kind=kOutput, calls=%fused_computation.12 | convolution fusion | flops 805699584 | bytes 5373956 | tf_op jit(solution)/shard_map/stf,sfqc->qtc/dot_general | solution.py:95
  35.5 2.6 %collective-permute-start.1 = (bf16[3,2,256]{2,1,0:T(2,128)(2,1)S(1)}, bf16[3,2,256]{2,1,0:T(2,128)(2,1)S(1)}, u32[]{:S(2)}, u32[]{:S(2)}) collective-permute-start(bf16[3,2,256]{2,1,0:T(2,128)(2,1)S(1)} %get-tuple-element.85), channel_id=1, source_target_pairs={{0,16},{16,32},{32,48},{48,64},{64,80},{80,96},{96,112},{112,128},... | collective-permute-start | bytes 9224 | tf_op jit(solution)/shard_map/ppermute | solution.py:12
  38.7 0.7 collective-permute-done.1
  39.7 0.8 fusion.160
  41.5 1.0 copy.23
  42.5 0.8 copy.22
  43.2 1.6 %pad_maximum_fusion.2 = bf16[256,16,32]{0,2,1:T(8,128)(2,1)} fusion(bf16[256,16,16]{0,2,1:T(8,128)(2,1)S(1)} %bitcast.190, bf16[256,16,16]{0,2,1:T(8,128)(2,1)} %bitcast.191), kind=kLoop, calls=%fused_computation.186 | loop fusion | flops 524288 | bytes 524288 | tf_op jit(solution)/shard_map/concatenate | solution.py:112
  44.9 12.3 %all-to-all-start.1 = ((bf16[256,16,32]{0,2,1:T(8,128)(2,1)}), bf16[256,16,32]{0,2,1:T(8,128)(2,1)S(1)}, u32[]{:S(2)}, u32[]{:S(2)}) async-start(bf16[256,16,32]{0,2,1:T(8,128)(2,1)} %pad_maximum_fusion.2), calls=%async_computation.1 | async-start | bytes 524288 | tf_op jit(solution)/shard_map/all_to_all | solution.py:70
  57.2 2.4 %select_convert_fusion = bf16[256,256]{1,0:T(8,128)(2,1)} fusion(bf16[256]{0:T(256)(128)(2,1)S(1)} %fusion.146, s32[256]{0:T(256)} %iota_add_fusion, pred[256]{0:T(512)(128)(4,1)S(1)} %iota_compare_fusion.36), kind=kLoop, calls=%fused_computation.198 | loop fusion | flops 1048576 | bytes 132864 | tf_op jit(solution)/shard_map/convert.9
  59.6 2.4 %multiply_convert_fusion.4 = bf16[256,256]{1,0:T(8,128)(2,1)} fusion(f32[256]{0:T(256)} %select_multiply_fusion, s32[256]{0:T(256)} %iota_add_fusion), kind=kLoop, calls=%fused_computation.199 | loop fusion | flops 1048576 | bytes 133120 | tf_op jit(solution)/shard_map/convert.8
  62.0 6.9 %all-to-all-done.1 = bf16[256,16,32]{0,2,1:T(8,128)(2,1)S(1)} async-done(((bf16[256,16,32]{0,2,1:T(8,128)(2,1)}), bf16[256,16,32]{0,2,1:T(8,128)(2,1)S(1)}, u32[]{:S(2)}, u32[]{:S(2)}) %all-to-all-start.1) | async-done | bytes 262176 | tf_op jit(solution)/shard_map/all_to_all | solution.py:70
  68.8 1.3 %fusion.166 = (f32[16,16,512]{2,1,0:T(8,128)S(1)}, bf16[16,16,512]{2,1,0:T(8,128)(2,1)S(1)}) fusion(bf16[512,512]{1,0:T(8,128)(2,1)} %copy-done.2, bf16[256,16,32]{0,2,1:T(8,128)(2,1)S(1)} %all-to-all-done.1), kind=kOutput, calls=%fused_computation.497 | convolution fusion | flops 67371008 | bytes 1179648 | tf_op jit(solution)/shard_map/tbc,kt->bck/dot_general | solution.py:134
  78.8 1.1 fusion.29
  80.0 0.9 copy-done.3
  81.8 0.9 fusion.39
  82.7 3.6 %all-to-all-start.2 = ((bf16[258,16,48]{0,2,1:T(8,128)(2,1)}), bf16[258,16,48]{0,2,1:T(8,128)(2,1)S(1)}, u32[]{:S(2)}, u32[]{:S(2)}) async-start(bf16[258,16,48]{0,2,1:T(8,128)(2,1)} %fusion.39), calls=%async_computation.2 | async-start | bytes 1179648 | tf_op jit(solution)/shard_map/all_to_all | solution.py:70
  86.3 1.3 %collective-permute-start.2 = (bf16[4,2,256]{2,1,0:T(2,128)(2,1)S(1)}, bf16[4,2,256]{2,1,0:T(2,128)(2,1)S(1)}, u32[]{:S(2)}, u32[]{:S(2)}) collective-permute-start(bf16[4,2,256]{2,1,0:T(2,128)(2,1)S(1)} %pad_maximum_fusion.3), channel_id=1, source_target_pairs={{16,0},{32,16},{48,32},{64,48},{80,64},{96,80},{112,96},{128,112},... | collective-permute-start | bytes 12296 | tf_op jit(solution)/shard_map/ppermute | solution.py:12
  87.6 4.2 %collective-permute-done.2 = bf16[4,2,256]{2,1,0:T(2,128)(2,1)S(1)} collective-permute-done((bf16[4,2,256]{2,1,0:T(2,128)(2,1)S(1)}, bf16[4,2,256]{2,1,0:T(2,128)(2,1)S(1)}, u32[]{:S(2)}, u32[]{:S(2)}) %collective-permute-start.2) | collective-permute-done | bytes 4128 | tf_op jit(solution)/shard_map/ppermute | solution.py:12
  91.9 11.6 %all-to-all-done.2 = bf16[258,16,48]{0,2,1:T(8,128)(2,1)S(1)} async-done(((bf16[258,16,48]{0,2,1:T(8,128)(2,1)}), bf16[258,16,48]{0,2,1:T(8,128)(2,1)S(1)}, u32[]{:S(2)}, u32[]{:S(2)}) %all-to-all-start.2) | async-done | bytes 396320 | tf_op jit(solution)/shard_map/all_to_all | solution.py:70
  104.4 1.6 %multiply_convert_fusion.1 = bf16[256,256]{1,0:T(8,128)(2,1)} fusion(f32[256,256]{1,0:T(8,128)S(1)} %copy.24, f32[3,256,256]{2,1,0:T(8,128)} %copy-done.1), kind=kLoop, calls=%fused_computation.188 | loop fusion | flops 131072 | bytes 655360 | tf_op jit(solution)/shard_map/convert_element_type | solution.py:201
  106.0 0.7 fusion.162
  107.0 1.0 bitcast_convert_fusion
  108.1 1.0 fusion.84
  109.2 1.0 fusion.83
  110.3 0.8 copy.28
  (229 shorter events, 25.1 us)
Async XLA Ops:
  0.6 9.6 %copy-start = (bf16[4096,256]{1,0:T(8,128)(2,1)S(1)}, bf16[4096,256]{1,0:T(8,128)(2,1)}, u32[]{:S(2)}) copy-start(bf16[4096,256]{1,0:T(8,128)(2,1)} %param.8) | copy-start | bytes 6291460
  2.7 23.6 %all-to-all-start = ((bf16[8,256,256]{2,1,0:T(8,128)(2,1)}), bf16[8,256,256]{2,1,0:T(8,128)(2,1)}, u32[]{:S(2)}, u32[]{:S(2)}) async-start(bf16[8,256,256]{2,1,0:T(8,128)(2,1)} %broadcast_in_dim.737), calls=%async_computation | async-start | bytes 2097152 | tf_op jit(solution)/shard_map/all_to_all | solution.py:88
  16.9 2.2 %copy-start.2 = (bf16[512,512]{1,0:T(8,128)(2,1)}, bf16[512,512]{1,0:T(8,128)(2,1)S(1)}, u32[]{:S(2)}) copy-start(bf16[512,512]{1,0:T(8,128)(2,1)S(1)} %fusion.33) | copy-start | bytes 1572868
  16.9 5.9 %copy-start.41 = (f32[3,1,1,256]{3,1,0,2:T(1,128)S(1)}, f32[3,1,1,256]{3,1,0,2:T(1,128)}, u32[]{:S(2)}) copy-start(f32[3,1,1,256]{3,1,0,2:T(1,128)} %get-tuple-element.228) | copy-start | bytes 9220
  26.3 5.6 %collective-permute-start = (bf16[8,256,256]{2,1,0:T(8,128)(2,1)}, bf16[8,256,256]{2,1,0:T(8,128)(2,1)S(1)}, u32[]{:S(2)}, u32[]{:S(2)}) collective-permute-start(bf16[8,256,256]{2,1,0:T(8,128)(2,1)} %all-to-all-done), channel_id=1, source_target_pairs={{0,1},{1,0},{2,3},{3,2},{4,5},{5,4},{6,7},{7,6},{8,9},{9,8},{10,11... | collective-permute-start | bytes 3145736 | tf_op jit(solution)/shard_map/ppermute | solution.py:89
  32.0 6.7 %copy-start.40 = (f32[3,1,1,256]{3,1,0,2:T(1,128)S(1)}, f32[3,1,1,256]{3,1,0,2:T(1,128)}, u32[]{:S(2)}) copy-start(f32[3,1,1,256]{3,1,0,2:T(1,128)} %get-tuple-element.226) | copy-start | bytes 9220
  35.5 3.2 %copy-start.42 = (bf16[3,2,256]{2,1,0:T(2,128)(2,1)}, bf16[3,2,256]{2,1,0:T(2,128)(2,1)S(1)}, u32[]{:S(2)}) copy-start(bf16[3,2,256]{2,1,0:T(2,128)(2,1)S(1)} %get-tuple-element.85) | copy-start | bytes 9220
  35.5 3.9 %collective-permute-start.1 = (bf16[3,2,256]{2,1,0:T(2,128)(2,1)S(1)}, bf16[3,2,256]{2,1,0:T(2,128)(2,1)S(1)}, u32[]{:S(2)}, u32[]{:S(2)}) collective-permute-start(bf16[3,2,256]{2,1,0:T(2,128)(2,1)S(1)} %get-tuple-element.85), channel_id=1, source_target_pairs={{0,16},{16,32},{32,48},{48,64},{64,80},{80,96},{96,112},{112,128},... | collective-permute-start | bytes 9224 | tf_op jit(solution)/shard_map/ppermute | solution.py:12
  39.7 1.1 copy-start.1
  39.7 1.1 copy-start.5
  44.9 24.0 %all-to-all-start.1 = ((bf16[256,16,32]{0,2,1:T(8,128)(2,1)}), bf16[256,16,32]{0,2,1:T(8,128)(2,1)S(1)}, u32[]{:S(2)}, u32[]{:S(2)}) async-start(bf16[256,16,32]{0,2,1:T(8,128)(2,1)} %pad_maximum_fusion.2), calls=%async_computation.1 | async-start | bytes 524288 | tf_op jit(solution)/shard_map/all_to_all | solution.py:70
  68.8 1.4 %copy-start.6 = (bf16[256,256]{1,0:T(8,128)(2,1)S(1)}, bf16[256,256]{1,0:T(8,128)(2,1)}, u32[]{:S(2)}) copy-start(bf16[256,256]{1,0:T(8,128)(2,1)} %select_convert_fusion) | copy-start | bytes 393220
  68.8 1.4 %copy-start.7 = (bf16[256,256]{1,0:T(8,128)(2,1)S(1)}, bf16[256,256]{1,0:T(8,128)(2,1)}, u32[]{:S(2)}) copy-start(bf16[256,256]{1,0:T(8,128)(2,1)} %multiply_convert_fusion.4) | copy-start | bytes 393220
  71.8 0.7 copy-start.29
  72.5 0.7 copy-start.27
  75.8 0.7 copy-start.20
  75.8 0.7 copy-start.21
  77.2 0.7 copy-start.39
  77.5 0.7 copy-start.37
  77.5 0.7 copy-start.34
  77.6 0.7 copy-start.35
  78.0 0.7 copy-start.33
  78.8 1.2 %copy-start.9 = (f32[1,16,512]{2,1,0:T(8,128)S(1)}, f32[1,16,512]{2,1,0:T(8,128)}, u32[]{:S(2)}) copy-start(f32[1,16,512]{2,1,0:T(8,128)} %get-tuple-element.125) | copy-start | bytes 98308
  79.9 1.0 copy-start.3
  81.8 4.5 %copy-start.44 = (bf16[3,2,256]{2,1,0:T(2,128)(2,1)S(1)}, bf16[3,2,256]{2,1,0:T(2,128)(2,1)}, u32[]{:S(2)}) copy-start(bf16[3,2,256]{2,1,0:T(2,128)(2,1)} %get-tuple-element.84) | copy-start | bytes 9220
  81.8 10.0 %copy-start.43 = (bf16[3,2,256]{2,1,0:T(2,128)(2,1)S(1)}, bf16[3,2,256]{2,1,0:T(2,128)(2,1)}, u32[]{:S(2)}) copy-start(bf16[3,2,256]{2,1,0:T(2,128)(2,1)} %copy-done.42) | copy-start | bytes 9220
  82.7 20.8 %all-to-all-start.2 = ((bf16[258,16,48]{0,2,1:T(8,128)(2,1)}), bf16[258,16,48]{0,2,1:T(8,128)(2,1)S(1)}, u32[]{:S(2)}, u32[]{:S(2)}) async-start(bf16[258,16,48]{0,2,1:T(8,128)(2,1)} %fusion.39), calls=%async_computation.2 | async-start | bytes 1179648 | tf_op jit(solution)/shard_map/all_to_all | solution.py:70
  86.3 5.5 %collective-permute-start.2 = (bf16[4,2,256]{2,1,0:T(2,128)(2,1)S(1)}, bf16[4,2,256]{2,1,0:T(2,128)(2,1)S(1)}, u32[]{:S(2)}, u32[]{:S(2)}) collective-permute-start(bf16[4,2,256]{2,1,0:T(2,128)(2,1)S(1)} %pad_maximum_fusion.3), channel_id=1, source_target_pairs={{16,0},{32,16},{48,32},{64,48},{80,64},{96,80},{112,96},{128,112},... | collective-permute-start | bytes 12296 | tf_op jit(solution)/shard_map/ppermute | solution.py:12
  91.8 14.9 %copy-start.46 = (bf16[4,2,256]{2,1,0:T(2,128)(2,1)}, bf16[4,2,256]{2,1,0:T(2,128)(2,1)S(1)}, u32[]{:S(2)}) copy-start(bf16[4,2,256]{2,1,0:T(2,128)(2,1)S(1)} %collective-permute-done.2) | copy-start | bytes 12292
  106.8 1.3 %slice-start = ((bf16[4,2,256]{2,1,0:T(2,128)(2,1)}), bf16[1,2,256]{2,1,0:T(2,128)(2,1)S(1)}, s32[]{:S(2)}) async-start(bf16[4,2,256]{2,1,0:T(2,128)(2,1)} %copy-done.46), calls=%async_computation.3 | async-start | bytes 2048 | tf_op jit(solution)/shard_map/slice | solution.py:123
  106.8 1.3 %copy-start.4 = (f32[1,256,256]{2,1,0:T(8,128)S(1)}, f32[1,256,256]{2,1,0:T(8,128)}, u32[]{:S(2)}) copy-start(f32[1,256,256]{2,1,0:T(8,128)} %get-tuple-element.21) | copy-start | bytes 786436
  109.2 1.0 copy-start.8
  (22 other events, 15.9 us)

commit v10 on v9

--- a/solution.py
+++ b/solution.py
@@ -16,21 +16,21 @@
     length = 2 * row_count
     sample = jnp.arange(length, dtype=jnp.int32)
     frequency = jnp.arange(row_count, dtype=jnp.int32)
-    angles = (frequency[:, None] * sample[None, :] % length).astype(jnp.float32) * (
-        2.0 * math.pi / length
-    )
+    base = sample.astype(jnp.float32) * (2.0 * math.pi / length)
+    cos_base, sin_base = (jnp.cos(base), jnp.sin(base))
+    phase = frequency[:, None] * sample[None, :] % length
     parity = 1.0 - 2.0 * (sample % 2).astype(jnp.float32)
-    lower_rows = jnp.where(frequency[:, None] == 0, parity[None, :], -jnp.sin(angles))
-    forward = jnp.concatenate([jnp.cos(angles), lower_rows], axis=0)
+    lower_rows = jnp.where(frequency[:, None] == 0, parity[None, :], -jnp.take(sin_base, phase))
+    forward = jnp.concatenate([jnp.take(cos_base, phase), lower_rows], axis=0)
     out_index = row_count + frequency
-    back_angles = (out_index[:, None] * frequency[None, :] % length).astype(jnp.float32) * (
-        2.0 * math.pi / length
-    )
+    back_phase = out_index[:, None] * frequency[None, :] % length
     factor = jnp.where(frequency == 0, 1.0, 2.0) / length
     out_parity = 1.0 - 2.0 * (out_index % 2).astype(jnp.float32)
-    real_part = jnp.cos(back_angles) * factor[None, :]
+    real_part = jnp.take(cos_base, back_phase) * factor[None, :]
     imag_part = jnp.where(
-        frequency[None, :] == 0, out_parity[:, None] / length, -2.0 * jnp.sin(back_angles) / length
+        frequency[None, :] == 0,
+        out_parity[:, None] / length,
+        -2.0 * jnp.take(sin_base, back_phase) / length,
     )
     inverse = jnp.concatenate([real_part, imag_part], axis=1)
     return (forward, inverse)

time: 113 us -> 3120 us (27.61)
  local copies, waits for them, and re-layouts: 26.6 us -> 3040 us
    gather x0 -> x8, local copies, waits for them, and re-layouts: none -> 3010 us  [the longest x2 1380 us: dft_tables(): forward = jnp.concatenate([jnp.take(cos_base, phase), lower_rows], axis=0)]
  transfers between devices with their start and end apart: 6 -> 6, of which waited for: 5 -> 3; matrix products, arithmetic and copies ran while one was open for 23% -> 97% of each run, Pallas kernels for 0% -> 0%
where the time goes in v10:
time: 3120 us
  local copies, waits for them, and re-layouts  3040 us (97%)
  starting transfers between devices  31.7 us (1%)
    gather x2, local copies, waits for them, and re-layouts, dft_tables(): forward = jnp.concatenate([jnp.take(cos_base, phase), lower_rows], axis=0)  1380 us
    gather x2, local copies, waits for them, and re-layouts, dft_tables(): jnp.take(sin_base, phase)  817 us
    gather x2, local copies, waits for them, and re-layouts, dft_tables(): real_part = jnp.take(cos_base, back_phase) * factor[None, :]  408 us
    gather x2, local copies, waits for them, and re-layouts, dft_tables(): jnp.take(sin_base, back_phase)  408 us
  transfers between devices with their start and end apart: 6, of which 3 were waited for; matrix products, arithmetic and copies ran while one was open for 97% of the time, Pallas kernels for 0%

profile of v10, /device:TPU:2, one launch (start us, length us, event | category | flops | bytes accessed | tf_op | source)
XLA Modules:
  0.0 3115.6 jit_solution(8995050695533825414)
XLA Ops:
  0.6 2.1 broadcast_in_dim.749
  2.7 7.5 all-to-all-start
  12.3 1.3 constant_dynamic-slice_fusion
  13.6 1.4 constant_dynamic-slice_fusion.1
  15.8 816.0 %gather_fusion.3 = f32[131072]{0:T(1024)S(1)} fusion(f32[512]{0:T(512)S(1)} %fusion.143, s32[131072]{0:T(1024)S(1)} %broadcast_clamp_fusion), kind=kCustom, calls=%fused_computation.3.clone | custom fusion | bytes 1572864 | tf_op jit(solution)/shard_map/jit(_take)/gather | solution.py:23
  831.7 0.9 reshape.275
  832.7 1374.3 %gather_fusion.2 = f32[131072]{0:T(1024)} fusion(f32[512]{0:T(512)S(1)} %copy-done.3, s32[131072]{0:T(1024)S(1)} %broadcast_clamp_fusion), kind=kCustom, calls=%fused_computation.1.clone | custom fusion | bytes 1572864 | tf_op jit(solution)/shard_map/jit(_take)/gather | solution.py:24
  2207.0 2.0 reshape.271
  2209.0 1.5 copy.19
  2210.9 1.6 fusion.77
  2223.8 3.2 fusion.6
  2227.0 2.9 fusion.18
  2230.6 2.6 collective-permute-start.1
  2233.7 0.7 collective-permute-done.1
  2234.8 0.8 fusion.163
  2236.9 12.3 all-to-all-start.1
  2249.7 408.2 %gather_fusion.1 = f32[65536]{0:T(1024)S(1)} fusion(f32[512]{0:T(512)S(1)} %copy-done.2, s32[65536]{0:T(1024)S(1)} %broadcast_clamp_fusion.1), kind=kCustom, calls=%fused_computation.2.clone | custom fusion | bytes 786432 | tf_op jit(solution)/shard_map/jit(_take)/gather | solution.py:33
  2658.0 408.2 %gather_fusion = f32[65536]{0:T(1024)S(1)} fusion(f32[512]{0:T(512)S(1)} %copy-done.3, s32[65536]{0:T(1024)S(1)} %broadcast_clamp_fusion.1), kind=kCustom, calls=%fused_computation.clone | custom fusion | bytes 786432 | tf_op jit(solution)/shard_map/jit(_take)/gather | solution.py:29
  3067.3 1.2 fusion.169
  3068.6 1.1 fusion.170
  3078.6 1.0 fusion.29
  3080.7 0.9 fusion.39
  3081.6 8.1 all-to-all-start.2
  3090.4 1.3 collective-permute-start.2
  3091.7 4.2 collective-permute-done.2
  3097.2 10.4 all-to-all-done.2
  3108.4 1.6 multiply_convert_fusion.1
  3110.0 0.7 fusion.165
  3111.9 0.9 multiply_convert_fusion
  3112.9 0.8 fusion.83
  3113.8 1.0 fusion.82
  3114.8 0.8 copy.28
  (286 shorter events, 31.9 us)
Async XLA Ops:
  0.6 11.7 copy-start
  2.7 2219.2 %all-to-all-start = ((bf16[8,256,256]{2,1,0:T(8,128)(2,1)}), bf16[8,256,256]{2,1,0:T(8,128)(2,1)}, u32[]{:S(2)}, u32[]{:S(2)}) async-start(bf16[8,256,256]{2,1,0:T(8,128)(2,1)} %broadcast_in_dim.749), calls=%async_computation | async-start | bytes 2097152 | tf_op jit(solution)/shard_map/all_to_all | solution.py:88
  10.2 5.5 copy-start.1
  2207.0 3.5 copy-start.9
  2209.0 1.9 copy-start.17
  2209.0 1.9 copy-start.64
  2212.5 2.4 copy-start.10
  2212.6 2.2 copy-start.62
  2213.5 6.0 copy-start.65
  2222.0 5.1 collective-permute-start
  2222.0 12.6 copy-start.20
  2222.0 12.6 copy-start.23
  2230.6 4.0 copy-start.59
  2230.6 3.9 collective-permute-start.1
  2234.8 1.1 copy-start.8
  2234.8 1.1 copy-start.15
  2235.9 13.8 copy-start.2
  2236.9 830.3 %all-to-all-start.1 = ((bf16[256,16,32]{0,2,1:T(8,128)(2,1)}), bf16[256,16,32]{0,2,1:T(8,128)(2,1)}, u32[]{:S(2)}, u32[]{:S(2)}) async-start(bf16[256,16,32]{0,2,1:T(8,128)(2,1)} %pad_maximum_fusion.2), calls=%async_computation.1 | async-start | bytes 524288 | tf_op jit(solution)/shard_map/all_to_all | solution.py:70
  2658.0 408.5 %copy-start.18 = (pred[256]{0:T(512)(128)(4,1)S(1)}, pred[256]{0:T(512)(128)(4,1)}, u32[]{:S(2)}) copy-start(pred[256]{0:T(512)(128)(4,1)} %iota_compare_fusion.36) | copy-start | bytes 772
  2658.0 408.5 %copy-start.63 = (s32[256]{0:T(256)S(1)}, s32[256]{0:T(256)}, u32[]{:S(2)}) copy-start(s32[256]{0:T(256)} %iota_add_fusion) | copy-start | bytes 3076
  2658.0 408.5 %copy-start.67 = (bf16[256]{0:T(256)(128)(2,1)S(1)}, bf16[256]{0:T(256)(128)(2,1)}, u32[]{:S(2)}) copy-start(bf16[256]{0:T(256)(128)(2,1)} %fusion.149) | copy-start | bytes 1540
  3077.4 1.2 copy-start.7
  3078.6 1.1 copy-start.19
  3080.7 9.7 copy-start.61
  3080.7 15.8 copy-start.60
  3080.7 15.8 copy-start.21
  3080.7 15.8 copy-start.24
  3080.7 15.8 copy-start.27
  3081.6 25.9 all-to-all-start.2
  3090.4 5.5 collective-permute-start.2
  3110.8 2.0 copy-start.12
  3110.8 2.0 copy-start.13
  (42 other events, 33.0 us)

commit v11 on v9

--- a/solution.py
+++ b/solution.py
@@ -12,10 +12,8 @@
     return lax.ppermute(block, axis, route)
 
 
-def dft_tables(row_count):
+def dft_tables(row_count, sample, frequency):
     length = 2 * row_count
-    sample = jnp.arange(length, dtype=jnp.int32)
-    frequency = jnp.arange(row_count, dtype=jnp.int32)
     angles = (frequency[:, None] * sample[None, :] % length).astype(jnp.float32) * (
         2.0 * math.pi / length
     )
@@ -76,10 +74,11 @@
     chan_count = lax.axis_size("chan")
     group = local_width // seq_count
     own_block = lax.axis_index("seq")
-    forward, inverse = dft_tables(row_count)
+    forward = dft_tables(
+        row_count, jnp.arange(2 * row_count, dtype=jnp.int32), jnp.arange(row_count, dtype=jnp.int32)
+    )[0]
     full_table = forward.astype(jnp.bfloat16)
     half_table = full_table[:, :row_count]
-    back_table = inverse.astype(jnp.bfloat16)
 
     half_count = chan_count // 2
     core = lax.axis_index("chan") % 2
@@ -108,12 +107,19 @@
     gated = (key_conv * value_conv).astype(jnp.bfloat16)
     grad_long = (cotangent.astype(jnp.float32) * query_conv).astype(jnp.bfloat16)
 
-    both_cols = swap_layout(
-        jnp.concatenate(
-            [gated.reshape(row_count, seq_count, group), grad_long.reshape(row_count, seq_count, group)],
-            axis=2,
-        )
-    )
+    inbound = jnp.concatenate(
+        [gated.reshape(row_count, seq_count, group), grad_long.reshape(row_count, seq_count, group)],
+        axis=2,
+    )
+    both_cols = swap_layout(inbound)
+    indices, _ = lax.optimization_barrier(
+        (
+            (jnp.arange(2 * row_count, dtype=jnp.int32), jnp.arange(row_count, dtype=jnp.int32)),
+            inbound,
+        )
+    )
+    inverse = dft_tables(row_count, *indices)[1]
+    back_table = inverse.astype(jnp.bfloat16)
     gated_cols, grad_long_cols = (both_cols[..., :group], both_cols[..., group:])
 
     after_rows, _ = lax.optimization_barrier(

time: 113 us -> 113 us (level)
  other arithmetic: 21.1 us -> 19.3 us
  waiting for transfers between devices: 24.6 us -> 26.1 us
    unnamed x112 -> x120, local copies, waits for them, and re-layouts: 7.1 us -> 6.79 us
  transfers between devices with their start and end apart: 6 -> 6, of which waited for: 5 -> 5; matrix products, arithmetic and copies ran while one was open for 23% -> 21% of each run, Pallas kernels for 0% -> 0%
where the time goes in v11:
time: 113 us; the launch traced here: 112 us
  starting transfers between devices  27.2 us (24%)
  local copies, waits for them, and re-layouts  27 us (24%)
  waiting for transfers between devices  26.1 us (23%)
  other arithmetic  19.3 us (17%)
  matrix products  10.1 us (9%)
  between operations  1.97 us (2%)
    all_to_all x2, waiting for transfers between devices, swap_layout(): return lax.all_to_all(values, 'seq', 1, 1, tiled=True)  18.6 us
    all_to_all x2, starting transfers between devices, swap_layout(): return lax.all_to_all(values, 'seq', 1, 1, tiled=True)  15.9 us
    mul x15, local copies, waits for them, and re-layouts, spectral_product(): real_out = left_re * right_re - jnp.where(first_row, 0.0, cross_term)  9.21 us
    all_to_all x1, starting transfers between devices, on_device(): lax.all_to_all(copies, 'chan', 0, 0, tiled=True, axis_index_groups=groups)  7.46 us
    unnamed x120, local copies, waits for them, and re-layouts  6.79 us
    ppermute x2, waiting for transfers between devices, passed_along(): return lax.ppermute(block, axis, route)  5.45 us
    another operation x4, other arithmetic  5.15 us
    ppermute x2, starting transfers between devices, passed_along(): return lax.ppermute(block, axis, route)  3.86 us
  transfers between devices with their start and end apart: 6, of which 5 were waited for; matrix products, arithmetic and copies ran while one was open for 21% of the time, Pallas kernels for 0%

profile of v11, /device:TPU:2, one launch (start us, length us, event | category | flops | bytes accessed | tf_op | source)
XLA Modules:
  0.0 111.7 jit_solution(4353788616576434466)
XLA Ops:
  0.6 2.1 %broadcast_in_dim.737 = bf16[8,256,256]{2,1,0:T(8,128)(2,1)} broadcast(bf16[256,256]{1,0:T(8,128)(2,1)} %param.5), dimensions={1,2} | broadcast | bytes 1179648 | tf_op jit(solution)/shard_map/broadcast_in_dim | solution.py:86
  2.7 7.5 %all-to-all-start = ((bf16[8,256,256]{2,1,0:T(8,128)(2,1)}), bf16[8,256,256]{2,1,0:T(8,128)(2,1)}, u32[]{:S(2)}, u32[]{:S(2)}) async-start(bf16[8,256,256]{2,1,0:T(8,128)(2,1)} %broadcast_in_dim.737), calls=%async_computation | async-start | bytes 2097152 | tf_op jit(solution)/shard_map/all_to_all | solution.py:87
  10.2 1.3 %constant_dynamic-slice_fusion = bf16[3840,16]{1,0:T(8,128)(2,1)} fusion(bf16[4096,256]{1,0:T(8,128)(2,1)S(1)} %copy-done, s32[]{:T(128)S(6)} %select_n.386), kind=kLoop, calls=%fused_computation.475 | loop fusion | bytes 245764 | tf_op jit(solution)/shard_map/slice | solution.py:146
  11.9 1.5 %copy.21 = bf16[15,256,16]{1,2,0:T(8,128)(2,1)S(1)} copy(bf16[15,256,16]{2,1,0:T(8,128)(2,1)} %bitcast.188) | data formatting | bytes 245760 | tf_op jit(solution)/shard_map/slice | solution.py:146
  13.7 2.1 %negate_select_fusion.2 = (f32[256,512]{1,0:T(8,128)S(1)}, f32[256,512]{1,0:T(8,128)S(1)}) fusion(f32[512]{0:T(512)S(1)} %fusion.106, pred[256]{0:T(512)(128)(4,1)S(1)} %iota_compare_fusion.36), kind=kLoop, calls=%fused_computation.151 | loop fusion | flops 2097152 | bytes 1050880 | tf_op jit(solution)/shard_map/jit(_where)/select_n | solution.py:21
  24.4 2.0 %all-to-all-done = bf16[8,256,256]{2,1,0:T(8,128)(2,1)} async-done(((bf16[8,256,256]{2,1,0:T(8,128)(2,1)}), bf16[8,256,256]{2,1,0:T(8,128)(2,1)}, u32[]{:S(2)}, u32[]{:S(2)}) %all-to-all-start) | async-done | bytes 1048608 | tf_op jit(solution)/shard_map/all_to_all | solution.py:87
  28.2 3.2 %fusion.6 = f32[3,256,256]{1,2,0:T(8,128)S(1)} fusion(bf16[8,2,256,3,256]{4,2,1,0,3:T(8,128)(2,1)} %bitcast.196, s32[]{:T(128)S(6)} %select_n.380, bf16[8,256,256]{2,1,0:T(8,128)(2,1)} %all-to-all-done), kind=kOutput, calls=%fused_computation.8 | convolution fusion | flops 805306368 | bytes 4980740 | tf_op jit(solution)/shard_map/stf,sfqc->qtc/dot_general | solution.py:93
  31.4 3.2 %fusion.18 = bf16[3,256,256]{2,1,0:T(8,128)(2,1)S(1)} fusion(f32[3,256,256]{1,2,0:T(8,128)S(1)} %fusion.6, bf16[8,2,256,3,256]{4,2,1,0,3:T(8,128)(2,1)} %bitcast.197, s32[]{:T(128)S(6)} %select_n.381, bf16[8,256,256]{2,1,0:T(8,128)(2,1)} %collective-permute-done), kind=kOutput, calls=%fused_computation.12 | convolution fusion | flops 805699584 | bytes 5373956 | tf_op jit(solution)/shard_map/stf,sfqc->qtc/dot_general | solution.py:94
  35.3 2.6 %collective-permute-start.1 = (bf16[3,2,256]{2,1,0:T(2,128)(2,1)S(1)}, bf16[3,2,256]{2,1,0:T(2,128)(2,1)S(1)}, u32[]{:S(2)}, u32[]{:S(2)}) collective-permute-start(bf16[3,2,256]{2,1,0:T(2,128)(2,1)S(1)} %get-tuple-element.89), channel_id=1, source_target_pairs={{0,16},{16,32},{32,48},{48,64},{64,80},{80,96},{96,112},{112,128},... | collective-permute-start | bytes 9224 | tf_op jit(solution)/shard_map/ppermute | solution.py:12
  37.9 1.2 %collective-permute-done.1 = bf16[3,2,256]{2,1,0:T(2,128)(2,1)S(1)} collective-permute-done((bf16[3,2,256]{2,1,0:T(2,128)(2,1)S(1)}, bf16[3,2,256]{2,1,0:T(2,128)(2,1)S(1)}, u32[]{:S(2)}, u32[]{:S(2)}) %collective-permute-start.1) | collective-permute-done | bytes 3104 | tf_op jit(solution)/shard_map/ppermute | solution.py:12
  39.5 0.8 fusion.157
  41.3 1.0 copy.19
  42.3 0.8 copy.18
  43.0 1.6 %pad_maximum_fusion.2 = bf16[256,16,32]{0,2,1:T(8,128)(2,1)} fusion(bf16[256,16,16]{0,2,1:T(8,128)(2,1)S(1)} %bitcast.190, bf16[256,16,16]{0,2,1:T(8,128)(2,1)} %bitcast.191), kind=kLoop, calls=%fused_computation.186 | loop fusion | flops 524288 | bytes 524288 | tf_op jit(solution)/shard_map/concatenate | solution.py:110
  44.7 12.3 %all-to-all-start.1 = ((bf16[256,16,32]{0,2,1:T(8,128)(2,1)}), bf16[256,16,32]{0,2,1:T(8,128)(2,1)S(1)}, u32[]{:S(2)}, u32[]{:S(2)}) async-start(bf16[256,16,32]{0,2,1:T(8,128)(2,1)} %pad_maximum_fusion.2), calls=%async_computation.1 | async-start | bytes 524288 | tf_op jit(solution)/shard_map/all_to_all | solution.py:68
  57.0 1.7 %multiply_convert_fusion.2 = bf16[256,256]{1,0:T(8,128)(2,1)} fusion(f32[256]{0:T(256)S(1)} %get-tuple-element.13, s32[256]{0:T(256)S(1)} %iota.310, s32[256]{0:T(256)S(1)} %broadcast_add_fusion), kind=kLoop, calls=%fused_computation.199 | loop fusion | flops 1048576 | bytes 134144 | tf_op jit(solution)/shard_map/convert.8
  58.7 1.7 %select_convert_fusion = bf16[256,256]{1,0:T(8,128)(2,1)} fusion(bf16[256]{0:T(256)(128)(2,1)S(1)} %fusion.143, s32[256]{0:T(256)S(1)} %iota.310, s32[256]{0:T(256)S(1)} %broadcast_add_fusion, pred[256]{0:T(512)(128)(4,1)S(1)} %get-tuple-element.14), kind=kLoop, calls=%fused_computation.198 | loop fusion | flops 1048576 | bytes 133888 | tf_op jit(solution)/shard_map/convert.9
  60.5 8.2 %all-to-all-done.1 = bf16[256,16,32]{0,2,1:T(8,128)(2,1)S(1)} async-done(((bf16[256,16,32]{0,2,1:T(8,128)(2,1)}), bf16[256,16,32]{0,2,1:T(8,128)(2,1)S(1)}, u32[]{:S(2)}, u32[]{:S(2)}) %all-to-all-start.1) | async-done | bytes 262176 | tf_op jit(solution)/shard_map/all_to_all | solution.py:68
  68.6 1.2 %fusion.163 = (f32[16,16,512]{2,1,0:T(8,128)S(1)}, bf16[16,16,512]{2,1,0:T(8,128)(2,1)S(1)}) fusion(bf16[512,512]{1,0:T(8,128)(2,1)} %copy-done.2, bf16[256,16,32]{0,2,1:T(8,128)(2,1)S(1)} %all-to-all-done.1), kind=kOutput, calls=%fused_computation.497 | convolution fusion | flops 67371008 | bytes 1179648 | tf_op jit(solution)/shard_map/tbc,kt->bck/dot_general | solution.py:140
  78.7 1.1 fusion.29
  79.8 0.9 copy-done.3
  81.7 0.9 fusion.39
  82.6 3.6 %all-to-all-start.2 = ((bf16[258,16,48]{0,2,1:T(8,128)(2,1)}), bf16[258,16,48]{0,2,1:T(8,128)(2,1)S(1)}, u32[]{:S(2)}, u32[]{:S(2)}) async-start(bf16[258,16,48]{0,2,1:T(8,128)(2,1)} %fusion.39), calls=%async_computation.2 | async-start | bytes 1179648 | tf_op jit(solution)/shard_map/all_to_all | solution.py:68
  86.2 1.3 %collective-permute-start.2 = (bf16[4,2,256]{2,1,0:T(2,128)(2,1)S(1)}, bf16[4,2,256]{2,1,0:T(2,128)(2,1)S(1)}, u32[]{:S(2)}, u32[]{:S(2)}) collective-permute-start(bf16[4,2,256]{2,1,0:T(2,128)(2,1)S(1)} %pad_maximum_fusion.3), channel_id=1, source_target_pairs={{16,0},{32,16},{48,32},{64,48},{80,64},{96,80},{112,96},{128,112},... | collective-permute-start | bytes 12296 | tf_op jit(solution)/shard_map/ppermute | solution.py:12
  87.5 4.2 %collective-permute-done.2 = bf16[4,2,256]{2,1,0:T(2,128)(2,1)S(1)} collective-permute-done((bf16[4,2,256]{2,1,0:T(2,128)(2,1)S(1)}, bf16[4,2,256]{2,1,0:T(2,128)(2,1)S(1)}, u32[]{:S(2)}, u32[]{:S(2)}) %collective-permute-start.2) | collective-permute-done | bytes 4128 | tf_op jit(solution)/shard_map/ppermute | solution.py:12
  93.0 10.5 %all-to-all-done.2 = bf16[258,16,48]{0,2,1:T(8,128)(2,1)S(1)} async-done(((bf16[258,16,48]{0,2,1:T(8,128)(2,1)}), bf16[258,16,48]{0,2,1:T(8,128)(2,1)S(1)}, u32[]{:S(2)}, u32[]{:S(2)}) %all-to-all-start.2) | async-done | bytes 396320 | tf_op jit(solution)/shard_map/all_to_all | solution.py:68
  104.2 1.6 %multiply_convert_fusion.1 = bf16[256,256]{1,0:T(8,128)(2,1)} fusion(f32[256,256]{1,0:T(8,128)S(1)} %copy.24, f32[3,256,256]{2,1,0:T(8,128)} %copy-done.1), kind=kLoop, calls=%fused_computation.190 | loop fusion | flops 131072 | bytes 655360 | tf_op jit(solution)/shard_map/convert_element_type | solution.py:207
  106.8 1.0 bitcast_convert_fusion
  107.9 0.9 multiply_convert_fusion
  108.9 0.8 fusion.84
  109.8 1.0 fusion.83
  110.8 0.8 copy.28
  (237 shorter events, 25.0 us)
Async XLA Ops:
  0.6 9.6 %copy-start = (bf16[4096,256]{1,0:T(8,128)(2,1)S(1)}, bf16[4096,256]{1,0:T(8,128)(2,1)}, u32[]{:S(2)}) copy-start(bf16[4096,256]{1,0:T(8,128)(2,1)} %param.8) | copy-start | bytes 6291460
  2.7 23.6 %all-to-all-start = ((bf16[8,256,256]{2,1,0:T(8,128)(2,1)}), bf16[8,256,256]{2,1,0:T(8,128)(2,1)}, u32[]{:S(2)}, u32[]{:S(2)}) async-start(bf16[8,256,256]{2,1,0:T(8,128)(2,1)} %broadcast_in_dim.737), calls=%async_computation | async-start | bytes 2097152 | tf_op jit(solution)/shard_map/all_to_all | solution.py:87
  16.0 2.3 %copy-start.2 = (bf16[512,512]{1,0:T(8,128)(2,1)}, bf16[512,512]{1,0:T(8,128)(2,1)S(1)}, u32[]{:S(2)}) copy-start(bf16[512,512]{1,0:T(8,128)(2,1)S(1)} %fusion.33) | copy-start | bytes 1572868
  16.0 10.4 %copy-start.50 = (f32[3,3,256]{2,1,0:T(4,128)S(1)}, f32[3,3,256]{2,1,0:T(4,128)}, u32[]{:S(2)}) copy-start(f32[3,3,256]{2,1,0:T(4,128)} %param.7) | copy-start | bytes 27652
  26.4 5.1 %collective-permute-start = (bf16[8,256,256]{2,1,0:T(8,128)(2,1)}, bf16[8,256,256]{2,1,0:T(8,128)(2,1)}, u32[]{:S(2)}, u32[]{:S(2)}) collective-permute-start(bf16[8,256,256]{2,1,0:T(8,128)(2,1)} %all-to-all-done), channel_id=1, source_target_pairs={{0,1},{1,0},{2,3},{3,2},{4,5},{5,4},{6,7},{7,6},{8,9},{9,8},{10,11... | collective-permute-start | bytes 3145736 | tf_op jit(solution)/shard_map/ppermute | solution.py:88
  35.3 4.0 %copy-start.47 = (bf16[3,2,256]{2,1,0:T(2,128)(2,1)}, bf16[3,2,256]{2,1,0:T(2,128)(2,1)S(1)}, u32[]{:S(2)}) copy-start(bf16[3,2,256]{2,1,0:T(2,128)(2,1)S(1)} %get-tuple-element.89) | copy-start | bytes 9220
  35.3 3.9 %collective-permute-start.1 = (bf16[3,2,256]{2,1,0:T(2,128)(2,1)S(1)}, bf16[3,2,256]{2,1,0:T(2,128)(2,1)S(1)}, u32[]{:S(2)}, u32[]{:S(2)}) collective-permute-start(bf16[3,2,256]{2,1,0:T(2,128)(2,1)S(1)} %get-tuple-element.89), channel_id=1, source_target_pairs={{0,16},{16,32},{32,48},{48,64},{64,80},{80,96},{96,112},{112,128},... | collective-permute-start | bytes 9224 | tf_op jit(solution)/shard_map/ppermute | solution.py:12
  37.9 54.4 %copy-start.11 = (f32[3,256]{1,0:T(4,128)}, f32[3,256]{1,0:T(4,128)S(1)}, u32[]{:S(2)}) copy-start(f32[3,256]{1,0:T(4,128)S(1)} %get-tuple-element.241) | copy-start | bytes 9220
  37.9 54.4 %copy-start.13 = (f32[3,256]{1,0:T(4,128)}, f32[3,256]{1,0:T(4,128)S(1)}, u32[]{:S(2)}) copy-start(f32[3,256]{1,0:T(4,128)S(1)} %get-tuple-element.242) | copy-start | bytes 9220
  37.9 54.4 %copy-start.15 = (f32[3,1,1,256]{3,0,1,2:T(4,128)}, f32[3,1,1,256]{3,0,1,2:T(4,128)S(1)}, u32[]{:S(2)}) copy-start(f32[3,1,1,256]{3,0,1,2:T(4,128)S(1)} %copy.43) | copy-start | bytes 9220
  39.5 1.1 copy-start.1
  39.5 1.1 copy-start.6
  44.7 24.0 %all-to-all-start.1 = ((bf16[256,16,32]{0,2,1:T(8,128)(2,1)}), bf16[256,16,32]{0,2,1:T(8,128)(2,1)S(1)}, u32[]{:S(2)}, u32[]{:S(2)}) async-start(bf16[256,16,32]{0,2,1:T(8,128)(2,1)} %pad_maximum_fusion.2), calls=%async_computation.1 | async-start | bytes 524288 | tf_op jit(solution)/shard_map/all_to_all | solution.py:68
  68.6 1.4 %copy-start.7 = (bf16[256,256]{1,0:T(8,128)(2,1)S(1)}, bf16[256,256]{1,0:T(8,128)(2,1)}, u32[]{:S(2)}) copy-start(bf16[256,256]{1,0:T(8,128)(2,1)} %multiply_convert_fusion.2) | copy-start | bytes 393220
  68.6 1.4 %copy-start.8 = (bf16[256,256]{1,0:T(8,128)(2,1)S(1)}, bf16[256,256]{1,0:T(8,128)(2,1)}, u32[]{:S(2)}) copy-start(bf16[256,256]{1,0:T(8,128)(2,1)} %select_convert_fusion) | copy-start | bytes 393220
  74.7 0.7 copy-start.25
  74.8 0.7 copy-start.26
  77.4 0.7 copy-start.43
  77.4 0.7 copy-start.44
  77.8 0.7 copy-start.42
  78.6 1.2 %copy-start.10 = (f32[1,16,512]{2,1,0:T(8,128)S(1)}, f32[1,16,512]{2,1,0:T(8,128)}, u32[]{:S(2)}) copy-start(f32[1,16,512]{2,1,0:T(8,128)} %get-tuple-element.129) | copy-start | bytes 98308
  79.7 1.0 copy-start.3
  81.6 4.5 %copy-start.49 = (bf16[3,2,256]{2,1,0:T(2,128)(2,1)S(1)}, bf16[3,2,256]{2,1,0:T(2,128)(2,1)}, u32[]{:S(2)}) copy-start(bf16[3,2,256]{2,1,0:T(2,128)(2,1)} %get-tuple-element.88) | copy-start | bytes 9220
  81.7 10.6 %copy-start.48 = (bf16[3,2,256]{2,1,0:T(2,128)(2,1)S(1)}, bf16[3,2,256]{2,1,0:T(2,128)(2,1)}, u32[]{:S(2)}) copy-start(bf16[3,2,256]{2,1,0:T(2,128)(2,1)} %copy-done.47) | copy-start | bytes 9220
  82.6 20.8 %all-to-all-start.2 = ((bf16[258,16,48]{0,2,1:T(8,128)(2,1)}), bf16[258,16,48]{0,2,1:T(8,128)(2,1)S(1)}, u32[]{:S(2)}, u32[]{:S(2)}) async-start(bf16[258,16,48]{0,2,1:T(8,128)(2,1)} %fusion.39), calls=%async_computation.2 | async-start | bytes 1179648 | tf_op jit(solution)/shard_map/all_to_all | solution.py:68
  86.2 5.5 %collective-permute-start.2 = (bf16[4,2,256]{2,1,0:T(2,128)(2,1)S(1)}, bf16[4,2,256]{2,1,0:T(2,128)(2,1)S(1)}, u32[]{:S(2)}, u32[]{:S(2)}) collective-permute-start(bf16[4,2,256]{2,1,0:T(2,128)(2,1)S(1)} %pad_maximum_fusion.3), channel_id=1, source_target_pairs={{16,0},{32,16},{48,32},{64,48},{80,64},{96,80},{112,96},{128,112},... | collective-permute-start | bytes 12296 | tf_op jit(solution)/shard_map/ppermute | solution.py:12
  106.6 2.2 %copy-start.4 = (f32[1,256,256]{2,1,0:T(8,128)S(1)}, f32[1,256,256]{2,1,0:T(8,128)}, u32[]{:S(2)}) copy-start(f32[1,256,256]{2,1,0:T(8,128)} %get-tuple-element.25) | copy-start | bytes 786436
  106.7 2.2 %copy-start.5 = (f32[1,256,256]{2,1,0:T(8,128)S(1)}, f32[1,256,256]{2,1,0:T(8,128)}, u32[]{:S(2)}) copy-start(f32[1,256,256]{2,1,0:T(8,128)} %get-tuple-element.27) | copy-start | bytes 786436
  108.9 0.9 copy-start.12
  108.9 0.9 copy-start.14
  108.9 0.9 copy-start.16
  109.8 1.0 copy-start.9
  (25 other events, 18.1 us)

commit v12 on v9

--- a/solution.py
+++ b/solution.py
@@ -16,12 +16,16 @@
     length = 2 * row_count
     sample = jnp.arange(length, dtype=jnp.int32)
     frequency = jnp.arange(row_count, dtype=jnp.int32)
-    angles = (frequency[:, None] * sample[None, :] % length).astype(jnp.float32) * (
+    first_half = sample[:row_count]
+    angles = (frequency[:, None] * first_half[None, :] % length).astype(jnp.float32) * (
         2.0 * math.pi / length
     )
-    parity = 1.0 - 2.0 * (sample % 2).astype(jnp.float32)
+    parity = 1.0 - 2.0 * (first_half % 2).astype(jnp.float32)
     lower_rows = jnp.where(frequency[:, None] == 0, parity[None, :], -jnp.sin(angles))
-    forward = jnp.concatenate([jnp.cos(angles), lower_rows], axis=0)
+    left = jnp.concatenate([jnp.cos(angles), lower_rows], axis=0)
+    row_sign = 1.0 - 2.0 * (frequency % 2).astype(jnp.float32)
+    row_sign = jnp.concatenate([row_sign, row_sign])[:, None]
+    forward = jnp.concatenate([left, left * row_sign], axis=1)
     out_index = row_count + frequency
     back_angles = (out_index[:, None] * frequency[None, :] % length).astype(jnp.float32) * (
         2.0 * math.pi / length

time: 113 us -> 118 us (1.044)
  local copies, waits for them, and re-layouts: 26.6 us -> 33.9 us
  waiting for transfers between devices: 24.6 us -> 22.4 us
  other arithmetic: 21.1 us -> 19.2 us
  matrix products: 9.79 us -> 11.6 us
    select_n x1 -> x0, other arithmetic: 2.14 us -> none  [dft_tables(): jnp.where(frequency[:, None] == 0, parity[None, :], -jnp.sin(angles))]
    reshape x1, local copies, waits for them, and re-layouts: 0.33 us -> 1.53 us  [on_device(): tap_blocks = own_taps.reshape(seq_count, row_count, group)]
    unnamed x112 -> x120, local copies, waits for them, and re-layouts: 7.1 us -> 7.82 us
  transfers between devices with their start and end apart: 6 -> 6, of which waited for: 5 -> 4; matrix products, arithmetic and copies ran while one was open for 23% -> 26% of each run, Pallas kernels for 0% -> 0%
where the time goes in v12:
time: 118 us; the launch traced here: 117 us
  local copies, waits for them, and re-layouts  33.9 us (29%)
  starting transfers between devices  27.9 us (24%)
  waiting for transfers between devices  22.4 us (19%)
  other arithmetic  19.2 us (16%)
  matrix products  11.6 us (10%)
  between operations  1.86 us (2%)
    all_to_all x2, waiting for transfers between devices, swap_layout(): return lax.all_to_all(values, 'seq', 1, 1, tiled=True)  17.5 us
    all_to_all x2, starting transfers between devices, swap_layout(): return lax.all_to_all(values, 'seq', 1, 1, tiled=True)  16.6 us
    mul x15, local copies, waits for them, and re-layouts, spectral_product(): real_out = left_re * right_re - jnp.where(first_row, 0.0, cross_term)  9.2 us
    unnamed x120, local copies, waits for them, and re-layouts  7.82 us
    all_to_all x1, starting transfers between devices, on_device(): lax.all_to_all(copies, 'chan', 0, 0, tiled=True, axis_index_groups=groups)  7.46 us
    another operation x4, other arithmetic  5.82 us
    ppermute x2, waiting for transfers between devices, passed_along(): return lax.ppermute(block, axis, route)  4.91 us
    ppermute x2, starting transfers between devices, passed_along(): return lax.ppermute(block, axis, route)  3.86 us
  transfers between devices with their start and end apart: 6, of which 4 were waited for; matrix products, arithmetic and copies ran while one was open for 26% of the time, Pallas kernels for 0%

profile of v12, /device:TPU:2, one launch (start us, length us, event | category | flops | bytes accessed | tf_op | source)
XLA Modules:
  0.0 117.0 jit_solution(7284887286115000950)
XLA Ops:
  0.6 2.1 %broadcast_in_dim.738 = bf16[8,256,256]{2,1,0:T(8,128)(2,1)} broadcast(bf16[256,256]{1,0:T(8,128)(2,1)} %param.5), dimensions={1,2} | broadcast | bytes 1179648 | tf_op jit(solution)/shard_map/broadcast_in_dim | solution.py:91
  2.8 7.5 %all-to-all-start = ((bf16[8,256,256]{2,1,0:T(8,128)(2,1)}), bf16[8,256,256]{2,1,0:T(8,128)(2,1)}, u32[]{:S(2)}, u32[]{:S(2)}) async-start(bf16[8,256,256]{2,1,0:T(8,128)(2,1)} %broadcast_in_dim.738), calls=%async_computation | async-start | bytes 2097152 | tf_op jit(solution)/shard_map/all_to_all | solution.py:92
  10.3 1.3 %constant_dynamic-slice_fusion = bf16[3840,16]{1,0:T(8,128)(2,1)} fusion(bf16[4096,256]{1,0:T(8,128)(2,1)S(1)} %copy-done, s32[]{:T(128)S(6)} %select_n.394), kind=kLoop, calls=%fused_computation.482 | loop fusion | bytes 245764 | tf_op jit(solution)/shard_map/slice | solution.py:144
  11.6 1.3 %constant_dynamic-slice_fusion.1 = bf16[4096,16]{1,0:T(8,128)(2,1)} fusion(bf16[4096,256]{1,0:T(8,128)(2,1)S(1)} %copy-done, s32[]{:T(128)S(6)} %select_n.394), kind=kLoop, calls=%fused_computation.483 | loop fusion | bytes 262148 | tf_op jit(solution)/shard_map/dynamic_slice | solution.py:141
  12.9 1.1 fusion.104
  14.1 0.9 fusion.38
  15.6 2.2 %copy.19 = bf16[15,256,16]{1,2,0:T(8,128)(2,1)} copy(bf16[15,256,16]{2,1,0:T(8,128)(2,1)} %bitcast.188) | data formatting | bytes 245760 | tf_op jit(solution)/shard_map/slice | solution.py:144
  17.8 1.5 %copy.21 = bf16[16,256,16]{1,2,0:T(8,128)(2,1)S(1)} copy(bf16[16,256,16]{2,1,0:T(8,128)(2,1)} %bitcast.187) | data formatting | bytes 262144 | tf_op jit(solution)/shard_map/reshape | solution.py:142
  19.3 1.2 %convolution_convert_fusion.2 = bf16[16,16,512]{2,1,0:T(8,128)(2,1)S(1)} fusion(bf16[512,512]{1,0:T(8,128)(2,1)S(1)} %copy-done.5, bf16[15,256,16]{1,2,0:T(8,128)(2,1)} %copy.19, bf16[16,256,16]{1,2,0:T(8,128)(2,1)S(1)} %copy.21), kind=kOutput, calls=%fused_computation.15 | convolution fusion | flops 135135232 | bytes 1040384 | tf_op jit(solution)/shard_map/fn,bnc->bcf/dot_general | solution.py:147
  31.0 3.2 %fusion.6 = f32[3,256,256]{1,2,0:T(8,128)S(1)} fusion(bf16[8,2,256,3,256]{4,2,1,0,3:T(8,128)(2,1)} %bitcast.196, s32[]{:T(128)S(6)} %select_n.388, bf16[8,256,256]{2,1,0:T(8,128)(2,1)} %all-to-all-done), kind=kOutput, calls=%fused_computation.8 | convolution fusion | flops 805306368 | bytes 4980740 | tf_op jit(solution)/shard_map/stf,sfqc->qtc/dot_general | solution.py:98
  34.2 2.9 %fusion.18 = bf16[3,256,256]{2,1,0:T(8,128)(2,1)S(1)} fusion(f32[3,256,256]{1,2,0:T(8,128)S(1)} %fusion.6, bf16[8,2,256,3,256]{4,2,1,0,3:T(8,128)(2,1)} %bitcast.197, s32[]{:T(128)S(6)} %select_n.389, bf16[8,256,256]{2,1,0:T(8,128)(2,1)S(1)} %collective-permute-done), kind=kOutput, calls=%fused_computation.12 | convolution fusion | flops 805699584 | bytes 5373956 | tf_op jit(solution)/shard_map/stf,sfqc->qtc/dot_general | solution.py:99
  37.7 2.6 %collective-permute-start.1 = (bf16[3,2,256]{2,1,0:T(2,128)(2,1)S(1)}, bf16[3,2,256]{2,1,0:T(2,128)(2,1)S(1)}, u32[]{:S(2)}, u32[]{:S(2)}) collective-permute-start(bf16[3,2,256]{2,1,0:T(2,128)(2,1)S(1)} %get-tuple-element.85), channel_id=1, source_target_pairs={{0,16},{16,32},{32,48},{48,64},{64,80},{80,96},{96,112},{112,128},... | collective-permute-start | bytes 9224 | tf_op jit(solution)/shard_map/ppermute | solution.py:12
  43.6 1.7 %copy.23 = bf16[256,256]{0,1:T(8,128)(2,1)} copy(bf16[256,256]{1,0:T(8,128)(2,1)} %multiply_convert_fusion.2) | data formatting | bytes 262144 | tf_op jit(solution)/shard_map/convert_element_type | solution.py:113
  45.2 1.7 %copy.22 = bf16[1,256,256]{1,2,0:T(8,128)(2,1)} copy(bf16[1,256,256]{2,1,0:T(8,128)(2,1)} %get-tuple-element.22) | data formatting | bytes 262144 | tf_op jit(solution)/shard_map/convert_element_type | solution.py:112
  46.9 1.7 %pad_maximum_fusion.2 = bf16[256,16,32]{0,2,1:T(8,128)(2,1)} fusion(bf16[256,16,16]{0,2,1:T(8,128)(2,1)} %bitcast.190, bf16[256,16,16]{0,2,1:T(8,128)(2,1)} %bitcast.191), kind=kLoop, calls=%fused_computation.183 | loop fusion | flops 524288 | bytes 524288 | tf_op jit(solution)/shard_map/concatenate | solution.py:116
  48.6 12.3 %all-to-all-start.1 = ((bf16[256,16,32]{0,2,1:T(8,128)(2,1)}), bf16[256,16,32]{0,2,1:T(8,128)(2,1)}, u32[]{:S(2)}, u32[]{:S(2)}) async-start(bf16[256,16,32]{0,2,1:T(8,128)(2,1)} %pad_maximum_fusion.2), calls=%async_computation.1 | async-start | bytes 524288 | tf_op jit(solution)/shard_map/all_to_all | solution.py:74
  61.0 2.4 %select_convert_fusion = bf16[256,256]{1,0:T(8,128)(2,1)} fusion(bf16[256]{0:T(256)(128)(2,1)S(1)} %fusion.140, s32[256]{0:T(256)} %iota_add_fusion, pred[256]{0:T(512)(128)(4,1)S(1)} %iota_compare_fusion.36), kind=kLoop, calls=%fused_computation.197 | loop fusion | flops 1048576 | bytes 132864 | tf_op jit(solution)/shard_map/convert.9
  63.3 2.4 %multiply_convert_fusion.4 = bf16[256,256]{1,0:T(8,128)(2,1)} fusion(f32[256]{0:T(256)} %select_multiply_fusion, s32[256]{0:T(256)} %iota_add_fusion), kind=kLoop, calls=%fused_computation.198 | loop fusion | flops 1048576 | bytes 133120 | tf_op jit(solution)/shard_map/convert.8
  65.7 6.9 %all-to-all-done.1 = bf16[256,16,32]{0,2,1:T(8,128)(2,1)} async-done(((bf16[256,16,32]{0,2,1:T(8,128)(2,1)}), bf16[256,16,32]{0,2,1:T(8,128)(2,1)}, u32[]{:S(2)}, u32[]{:S(2)}) %all-to-all-start.1) | async-done | bytes 262176 | tf_op jit(solution)/shard_map/all_to_all | solution.py:74
  72.7 1.3 %fusion.167 = (f32[16,16,512]{2,1,0:T(8,128)S(1)}, bf16[16,16,512]{2,1,0:T(8,128)(2,1)S(1)}) fusion(bf16[512,512]{1,0:T(8,128)(2,1)} %fusion.38, bf16[256,16,32]{0,2,1:T(8,128)(2,1)} %all-to-all-done.1), kind=kOutput, calls=%fused_computation.502 | convolution fusion | flops 67371008 | bytes 1179648 | tf_op jit(solution)/shard_map/tbc,kt->bck/dot_general | solution.py:138
  74.1 1.1 fusion.168
  84.0 1.0 fusion.29
  85.1 0.9 copy-done.6
  86.9 0.9 fusion.39
  87.8 4.2 %all-to-all-start.2 = ((bf16[258,16,48]{0,2,1:T(8,128)(2,1)}), bf16[258,16,48]{0,2,1:T(8,128)(2,1)}, u32[]{:S(2)}, u32[]{:S(2)}) async-start(bf16[258,16,48]{0,2,1:T(8,128)(2,1)} %fusion.39), calls=%async_computation.2 | async-start | bytes 1179648 | tf_op jit(solution)/shard_map/all_to_all | solution.py:74
  92.1 1.3 %collective-permute-start.2 = (bf16[4,2,256]{2,1,0:T(2,128)(2,1)S(1)}, bf16[4,2,256]{2,1,0:T(2,128)(2,1)S(1)}, u32[]{:S(2)}, u32[]{:S(2)}) collective-permute-start(bf16[4,2,256]{2,1,0:T(2,128)(2,1)S(1)} %pad_maximum_fusion.3), channel_id=1, source_target_pairs={{16,0},{32,16},{48,32},{64,48},{80,64},{96,80},{112,96},{128,112},... | collective-permute-start | bytes 12296 | tf_op jit(solution)/shard_map/ppermute | solution.py:12
  93.4 4.2 %collective-permute-done.2 = bf16[4,2,256]{2,1,0:T(2,128)(2,1)S(1)} collective-permute-done((bf16[4,2,256]{2,1,0:T(2,128)(2,1)S(1)}, bf16[4,2,256]{2,1,0:T(2,128)(2,1)S(1)}, u32[]{:S(2)}, u32[]{:S(2)}) %collective-permute-start.2) | collective-permute-done | bytes 4128 | tf_op jit(solution)/shard_map/ppermute | solution.py:12
  98.8 10.6 %all-to-all-done.2 = bf16[258,16,48]{0,2,1:T(8,128)(2,1)} async-done(((bf16[258,16,48]{0,2,1:T(8,128)(2,1)}), bf16[258,16,48]{0,2,1:T(8,128)(2,1)}, u32[]{:S(2)}, u32[]{:S(2)}) %all-to-all-start.2) | async-done | bytes 396320 | tf_op jit(solution)/shard_map/all_to_all | solution.py:74
  109.4 1.6 %fusion.162 = (bf16[256,16,16]{0,2,1:T(8,128)(2,1)}, bf16[256,16,16]{0,2,1:T(8,128)(2,1)S(1)}) fusion(bf16[258,16,48]{0,2,1:T(8,128)(2,1)} %all-to-all-done.2), kind=kLoop, calls=%fused_computation.497 | loop fusion | bytes 524288 | tf_op jit(solution)/shard_map/slice | solution.py:203
  111.9 1.1 fusion.163
  114.0 1.0 fusion.78
  115.1 1.0 fusion.77
  (241 shorter events, 28.0 us)
Async XLA Ops:
  0.6 9.6 %copy-start = (bf16[4096,256]{1,0:T(8,128)(2,1)S(1)}, bf16[4096,256]{1,0:T(8,128)(2,1)}, u32[]{:S(2)}) copy-start(bf16[4096,256]{1,0:T(8,128)(2,1)} %param.8) | copy-start | bytes 6291460
  2.8 25.8 %all-to-all-start = ((bf16[8,256,256]{2,1,0:T(8,128)(2,1)}), bf16[8,256,256]{2,1,0:T(8,128)(2,1)}, u32[]{:S(2)}, u32[]{:S(2)}) async-start(bf16[8,256,256]{2,1,0:T(8,128)(2,1)} %broadcast_in_dim.738), calls=%async_computation | async-start | bytes 2097152 | tf_op jit(solution)/shard_map/all_to_all | solution.py:92
  14.0 1.0 copy-start.1
  14.0 1.0 copy-start.3
  14.0 1.0 copy-start.49
  15.0 4.3 %copy-start.5 = (bf16[512,512]{1,0:T(8,128)(2,1)S(1)}, bf16[512,512]{1,0:T(8,128)(2,1)}, u32[]{:S(2)}) copy-start(bf16[512,512]{1,0:T(8,128)(2,1)} %fusion.38) | copy-start | bytes 1572868
  19.3 6.8 %copy-start.44 = (f32[3,1,1,256]{3,1,0,2:T(1,128)S(1)}, f32[3,1,1,256]{3,1,0,2:T(1,128)}, u32[]{:S(2)}) copy-start(f32[3,1,1,256]{3,1,0,2:T(1,128)} %get-tuple-element.228) | copy-start | bytes 9220
  28.6 5.6 %collective-permute-start = (bf16[8,256,256]{2,1,0:T(8,128)(2,1)}, bf16[8,256,256]{2,1,0:T(8,128)(2,1)S(1)}, u32[]{:S(2)}, u32[]{:S(2)}) collective-permute-start(bf16[8,256,256]{2,1,0:T(8,128)(2,1)} %all-to-all-done), channel_id=1, source_target_pairs={{0,1},{1,0},{2,3},{3,2},{4,5},{5,4},{6,7},{7,6},{8,9},{9,8},{10,11... | collective-permute-start | bytes 3145736 | tf_op jit(solution)/shard_map/ppermute | solution.py:93
  34.2 6.7 %copy-start.43 = (f32[3,1,1,256]{3,1,0,2:T(1,128)S(1)}, f32[3,1,1,256]{3,1,0,2:T(1,128)}, u32[]{:S(2)}) copy-start(f32[3,1,1,256]{3,1,0,2:T(1,128)} %get-tuple-element.226) | copy-start | bytes 9220
  37.7 4.0 %copy-start.45 = (bf16[3,2,256]{2,1,0:T(2,128)(2,1)}, bf16[3,2,256]{2,1,0:T(2,128)(2,1)S(1)}, u32[]{:S(2)}) copy-start(bf16[3,2,256]{2,1,0:T(2,128)(2,1)S(1)} %get-tuple-element.85) | copy-start | bytes 9220
  37.7 3.9 %collective-permute-start.1 = (bf16[3,2,256]{2,1,0:T(2,128)(2,1)S(1)}, bf16[3,2,256]{2,1,0:T(2,128)(2,1)S(1)}, u32[]{:S(2)}, u32[]{:S(2)}) collective-permute-start(bf16[3,2,256]{2,1,0:T(2,128)(2,1)S(1)} %get-tuple-element.85), channel_id=1, source_target_pairs={{0,16},{16,32},{32,48},{48,64},{64,80},{80,96},{96,112},{112,128},... | collective-permute-start | bytes 9224 | tf_op jit(solution)/shard_map/ppermute | solution.py:12
  42.0 0.9 copy-start.8
  48.6 24.1 %all-to-all-start.1 = ((bf16[256,16,32]{0,2,1:T(8,128)(2,1)}), bf16[256,16,32]{0,2,1:T(8,128)(2,1)}, u32[]{:S(2)}, u32[]{:S(2)}) async-start(bf16[256,16,32]{0,2,1:T(8,128)(2,1)} %pad_maximum_fusion.2), calls=%async_computation.1 | async-start | bytes 524288 | tf_op jit(solution)/shard_map/all_to_all | solution.py:74
  72.7 1.4 %copy-start.9 = (bf16[256,256]{1,0:T(8,128)(2,1)S(1)}, bf16[256,256]{1,0:T(8,128)(2,1)}, u32[]{:S(2)}) copy-start(bf16[256,256]{1,0:T(8,128)(2,1)} %select_convert_fusion) | copy-start | bytes 393220
  72.7 1.4 %copy-start.10 = (bf16[256,256]{1,0:T(8,128)(2,1)S(1)}, bf16[256,256]{1,0:T(8,128)(2,1)}, u32[]{:S(2)}) copy-start(bf16[256,256]{1,0:T(8,128)(2,1)} %multiply_convert_fusion.4) | copy-start | bytes 393220
  76.6 0.7 copy-start.32
  79.7 0.8 copy-start.17
  79.7 0.8 copy-start.18
  82.1 0.7 copy-start.42
  82.3 0.7 copy-start.40
  82.8 0.7 copy-start.36
  82.9 1.0 copy-start.2
  82.9 1.0 copy-start.4
  84.0 1.1 copy-start.12
  85.0 1.0 copy-start.6
  86.9 5.2 %copy-start.47 = (bf16[3,2,256]{2,1,0:T(2,128)(2,1)S(1)}, bf16[3,2,256]{2,1,0:T(2,128)(2,1)}, u32[]{:S(2)}) copy-start(bf16[3,2,256]{2,1,0:T(2,128)(2,1)} %get-tuple-element.84) | copy-start | bytes 9220
  86.9 11.3 %copy-start.46 = (bf16[3,2,256]{2,1,0:T(2,128)(2,1)S(1)}, bf16[3,2,256]{2,1,0:T(2,128)(2,1)}, u32[]{:S(2)}) copy-start(bf16[3,2,256]{2,1,0:T(2,128)(2,1)} %copy-done.45) | copy-start | bytes 9220
  87.8 21.6 %all-to-all-start.2 = ((bf16[258,16,48]{0,2,1:T(8,128)(2,1)}), bf16[258,16,48]{0,2,1:T(8,128)(2,1)}, u32[]{:S(2)}, u32[]{:S(2)}) async-start(bf16[258,16,48]{0,2,1:T(8,128)(2,1)} %fusion.39), calls=%async_computation.2 | async-start | bytes 1179648 | tf_op jit(solution)/shard_map/all_to_all | solution.py:74
  92.1 5.5 %collective-permute-start.2 = (bf16[4,2,256]{2,1,0:T(2,128)(2,1)S(1)}, bf16[4,2,256]{2,1,0:T(2,128)(2,1)S(1)}, u32[]{:S(2)}, u32[]{:S(2)}) collective-permute-start(bf16[4,2,256]{2,1,0:T(2,128)(2,1)S(1)} %pad_maximum_fusion.3), channel_id=1, source_target_pairs={{16,0},{32,16},{48,32},{64,48},{80,64},{96,80},{112,96},{128,112},... | collective-permute-start | bytes 12296 | tf_op jit(solution)/shard_map/ppermute | solution.py:12
  113.0 1.0 copy-start.7
  113.0 0.9 copy-start.48
  115.1 1.0 copy-start.11
  (26 other events, 18.6 us)

commit v13 on v9

--- a/solution.py
+++ b/solution.py
@@ -96,7 +96,17 @@
             "stf,sfqc->qtc", other_core, other_weights, preferred_element_type=jnp.float32
         )
     ).astype(jnp.bfloat16)
-    before = neighbour_rows(streams[:, row_count - 2 :], 1)
+    tail_rows = (
+        jnp.einsum(
+            "stf,sfqc->qtc", same_core[:, row_count - 2 :], own_weights,
+            preferred_element_type=jnp.float32,
+        )
+        + jnp.einsum(
+            "stf,sfqc->qtc", other_core[:, row_count - 2 :], other_weights,
+            preferred_element_type=jnp.float32,
+        )
+    ).astype(jnp.bfloat16)
+    before = neighbour_rows(tail_rows, 1)
     extended = jnp.concatenate([before, streams], axis=1).astype(jnp.float32)
     conv_weight = short_weight[:, :, None, :]
     conv_out = (

time: 113 us -> 110 us (0.973)
  matrix products: 9.79 us -> 14.1 us
  local copies, waits for them, and re-layouts: 26.6 us -> 23 us
  waiting for transfers between devices: 24.6 us -> 22.1 us
  starting transfers between devices: 27.2 us -> 25.8 us
    dot_general x0 -> x2, matrix products: none -> 4.98 us  [the longest x1 2.56 us: on_device(): jnp.einsum('stf,sfqc->qtc', same_core[:, row_count - 2:], own_weights, pr...]
    mul x15 -> x8, local copies, waits for them, and re-layouts: 9.1 us -> 4.99 us  [spectral_product(): real_out = left_re * right_re - jnp.where(first_row, 0.0, cross_term)]
    cos x0 -> x1, other arithmetic: none -> 1.9 us  [dft_tables(): forward = jnp.concatenate([jnp.cos(angles), lower_rows], axis=0)]
    all_to_all x2, starting transfers between devices: 15.9 us -> 14.5 us  [swap_layout(): return lax.all_to_all(values, 'seq', 1, 1, tiled=True)]
    reshape x1, local copies, waits for them, and re-layouts: 0.33 us -> 1.55 us  [on_device(): tap_blocks = own_taps.reshape(seq_count, row_count, group)]
    all_to_all x1, waiting for transfers between devices: 1.16 us -> 0.01 us  [on_device(): lax.all_to_all(copies, 'chan', 0, 0, tiled=True, axis_index_groups=groups)]
    unnamed x112 -> x108, local copies, waits for them, and re-layouts: 7.1 us -> 6.28 us
  transfers between devices with their start and end apart: 6 -> 6, of which waited for: 5 -> 3; matrix products, arithmetic and copies ran while one was open for 23% -> 30% of each run, Pallas kernels for 0% -> 0%
where the time goes in v13:
time: 110 us; the launch traced here: 109 us
  starting transfers between devices  25.8 us (23%)
  local copies, waits for them, and re-layouts  23 us (21%)
  other arithmetic  22.1 us (20%)
  waiting for transfers between devices  22.1 us (20%)
  matrix products  14.1 us (13%)
  between operations  1.95 us (2%)
    all_to_all x2, waiting for transfers between devices, swap_layout(): return lax.all_to_all(values, 'seq', 1, 1, tiled=True)  17.8 us
    all_to_all x2, starting transfers between devices, swap_layout(): return lax.all_to_all(values, 'seq', 1, 1, tiled=True)  14.5 us
    all_to_all x1, starting transfers between devices, on_device(): lax.all_to_all(copies, 'chan', 0, 0, tiled=True, axis_index_groups=groups)  7.46 us
    unnamed x108, local copies, waits for them, and re-layouts  6.28 us
    another operation x4, other arithmetic  5.79 us
    mul x8, local copies, waits for them, and re-layouts, spectral_product(): real_out = left_re * right_re - jnp.where(first_row, 0.0, cross_term)  4.99 us
    ppermute x2, waiting for transfers between devices, passed_along(): return lax.ppermute(block, axis, route)  4.2 us
    ppermute x2, starting transfers between devices, passed_along(): return lax.ppermute(block, axis, route)  3.87 us
  transfers between devices with their start and end apart: 6, of which 3 were waited for; matrix products, arithmetic and copies ran while one was open for 30% of the time, Pallas kernels for 0%

profile of v13, /device:TPU:2, one launch (start us, length us, event | category | flops | bytes accessed | tf_op | source)
XLA Modules:
  0.0 109.0 jit_solution(3456283403594915100)
XLA Ops:
  0.6 2.1 %broadcast_in_dim.737 = bf16[8,256,256]{2,1,0:T(8,128)(2,1)} broadcast(bf16[256,256]{1,0:T(8,128)(2,1)} %param.5), dimensions={1,2} | broadcast | bytes 1179648 | tf_op jit(solution)/shard_map/broadcast_in_dim | solution.py:87
  2.8 7.5 %all-to-all-start = ((bf16[8,256,256]{2,1,0:T(8,128)(2,1)}), bf16[8,256,256]{2,1,0:T(8,128)(2,1)}, u32[]{:S(2)}, u32[]{:S(2)}) async-start(bf16[8,256,256]{2,1,0:T(8,128)(2,1)} %broadcast_in_dim.737), calls=%async_computation | async-start | bytes 2097152 | tf_op jit(solution)/shard_map/all_to_all | solution.py:88
  10.2 1.9 %fusion.116 = f32[256,512]{1,0:T(8,128)S(1)} fusion(), kind=kLoop, calls=%fused_computation.208 | loop fusion | flops 1835008 | bytes 524288 | tf_op jit(solution)/shard_map/cos | solution.py:24
  12.2 1.3 %constant_dynamic-slice_fusion = bf16[3840,16]{1,0:T(8,128)(2,1)} fusion(bf16[4096,256]{1,0:T(8,128)(2,1)S(1)} %copy-done, s32[]{:T(128)S(6)} %select_n.396), kind=kLoop, calls=%fused_computation.492 | loop fusion | bytes 245764 | tf_op jit(solution)/shard_map/slice | solution.py:150
  13.5 1.3 %constant_dynamic-slice_fusion.1 = bf16[4096,16]{1,0:T(8,128)(2,1)} fusion(bf16[4096,256]{1,0:T(8,128)(2,1)S(1)} %copy-done, s32[]{:T(128)S(6)} %select_n.396), kind=kLoop, calls=%fused_computation.493 | loop fusion | bytes 262148 | tf_op jit(solution)/shard_map/dynamic_slice | solution.py:147
  15.4 1.5 %copy.19 = bf16[15,256,16]{1,2,0:T(8,128)(2,1)S(1)} copy(bf16[15,256,16]{2,1,0:T(8,128)(2,1)} %bitcast.228) | data formatting | bytes 245760 | tf_op jit(solution)/shard_map/slice | solution.py:150
  16.9 1.5 %copy.21 = bf16[16,256,16]{1,2,0:T(8,128)(2,1)S(1)} copy(bf16[16,256,16]{2,1,0:T(8,128)(2,1)} %bitcast.227) | data formatting | bytes 262144 | tf_op jit(solution)/shard_map/reshape | solution.py:148
  18.4 2.0 %negate_select_fusion.2 = f32[256,512]{1,0:T(8,128)S(1)} fusion(f32[512]{0:T(512)S(1)} %fusion.130, pred[256]{0:T(512)(128)(4,1)S(1)} %iota_compare_fusion.36), kind=kLoop, calls=%fused_computation.162 | loop fusion | flops 2097152 | bytes 526592 | tf_op jit(solution)/shard_map/jit(_where)/select_n | solution.py:23
  29.7 2.6 %fusion.35 = f32[3,256,2]{1,2,0:T(2,128)S(1)} fusion(bf16[8,2,256,3,256]{4,2,1,0,3:T(8,128)(2,1)} %bitcast.221, s32[]{:T(128)S(6)} %select_n.390, bf16[8,256,256]{2,1,0:T(8,128)(2,1)} %all-to-all-done), kind=kOutput, calls=%fused_computation.35 | convolution fusion | flops 6291456 | bytes 3160068 | tf_op jit(solution)/shard_map/stf,sfqc->qtc/dot_general | solution.py:100
  32.3 3.3 %fusion.12 = f32[3,256,256]{1,2,0:T(8,128)S(1)} fusion(bf16[8,2,256,3,256]{4,2,1,0,3:T(8,128)(2,1)} %bitcast.222, s32[]{:T(128)S(6)} %select_n.390, bf16[8,256,256]{2,1,0:T(8,128)(2,1)} %all-to-all-done), kind=kOutput, calls=%fused_computation.14 | convolution fusion | flops 805306368 | bytes 4980740 | tf_op jit(solution)/shard_map/stf,sfqc->qtc/dot_general | solution.py:94
  35.6 2.4 %fusion.47 = bf16[3,2,256]{2,1,0:T(2,128)(2,1)S(1)} fusion(f32[3,256,2]{1,2,0:T(2,128)S(1)} %fusion.35, bf16[8,2,256,3,256]{4,2,1,0,3:T(8,128)(2,1)} %bitcast.223, s32[]{:T(128)S(6)} %select_n.391, bf16[8,256,256]{2,1,0:T(8,128)(2,1)} %collective-permute-done), kind=kOutput, calls=%fused_computation.39 | convolution fusion | flops 6294528 | bytes 3163140 | tf_op jit(solution)/shard_map/stf,sfqc->qtc/dot_general | solution.py:104
  38.0 2.6 %collective-permute-start.1 = (bf16[3,2,256]{2,1,0:T(2,128)(2,1)S(1)}, bf16[3,2,256]{2,1,0:T(2,128)(2,1)S(1)}, u32[]{:S(2)}, u32[]{:S(2)}) collective-permute-start(bf16[3,2,256]{2,1,0:T(2,128)(2,1)S(1)} %fusion.47), channel_id=1, source_target_pairs={{0,16},{16,32},{32,48},{48,64},{64,80},{80,96},{96,112},{112,128},... | collective-permute-start | bytes 9224 | tf_op jit(solution)/shard_map/ppermute | solution.py:12
  40.7 2.2 %fusion.24 = bf16[3,256,256]{2,1,0:T(8,128)(2,1)S(1)} fusion(f32[3,256,256]{1,2,0:T(8,128)S(1)} %fusion.12, bf16[8,2,256,3,256]{4,2,1,0,3:T(8,128)(2,1)S(1)} %bitcast.226, s32[]{:T(128)S(6)} %select_n.391, bf16[8,256,256]{2,1,0:T(8,128)(2,1)} %collective-permute-done), kind=kOutput, calls=%fused_computation.18 | convolution fusion | flops 805699584 | bytes 5373956 | tf_op jit(solution)/shard_map/stf,sfqc->qtc/dot_general | solution.py:95
  43.7 0.9 copy-done.1
  44.6 0.8 fusion.183
  46.3 1.6 %pad_maximum_fusion.2 = bf16[256,16,32]{0,2,1:T(8,128)(2,1)} fusion(bf16[256,16,16]{0,2,1:T(8,128)(2,1)} %bitcast.230, bf16[256,16,16]{0,2,1:T(8,128)(2,1)S(1)} %bitcast.231), kind=kLoop, calls=%fused_computation.197 | loop fusion | flops 524288 | bytes 524288 | tf_op jit(solution)/shard_map/concatenate | solution.py:122
  47.9 10.9 %all-to-all-start.1 = ((bf16[256,16,32]{0,2,1:T(8,128)(2,1)}), bf16[256,16,32]{0,2,1:T(8,128)(2,1)S(1)}, u32[]{:S(2)}, u32[]{:S(2)}) async-start(bf16[256,16,32]{0,2,1:T(8,128)(2,1)} %pad_maximum_fusion.2), calls=%async_computation.1 | async-start | bytes 524288 | tf_op jit(solution)/shard_map/all_to_all | solution.py:70
  58.8 2.4 %multiply_convert_fusion.4 = bf16[256,256]{1,0:T(8,128)(2,1)} fusion(f32[256]{0:T(256)} %select_multiply_fusion, s32[256]{0:T(256)} %iota_add_fusion), kind=kLoop, calls=%fused_computation.210 | loop fusion | flops 1048576 | bytes 133120 | tf_op jit(solution)/shard_map/convert.8
  61.2 2.4 %select_convert_fusion = bf16[256,256]{1,0:T(8,128)(2,1)} fusion(bf16[256]{0:T(256)(128)(2,1)S(1)} %fusion.167, s32[256]{0:T(256)} %iota_add_fusion, pred[256]{0:T(512)(128)(4,1)S(1)} %iota_compare_fusion.36), kind=kLoop, calls=%fused_computation.209 | loop fusion | flops 1048576 | bytes 132864 | tf_op jit(solution)/shard_map/convert.9
  63.5 6.9 %all-to-all-done.1 = bf16[256,16,32]{0,2,1:T(8,128)(2,1)S(1)} async-done(((bf16[256,16,32]{0,2,1:T(8,128)(2,1)}), bf16[256,16,32]{0,2,1:T(8,128)(2,1)S(1)}, u32[]{:S(2)}, u32[]{:S(2)}) %all-to-all-start.1) | async-done | bytes 262176 | tf_op jit(solution)/shard_map/all_to_all | solution.py:70
  70.5 1.2 %fusion.190 = (f32[16,16,512]{2,1,0:T(8,128)S(1)}, bf16[16,16,512]{2,1,0:T(8,128)(2,1)S(1)}) fusion(bf16[256,256]{1,0:T(8,128)(2,1)} %select_convert_fusion, bf16[256,256]{1,0:T(8,128)(2,1)} %multiply_convert_fusion.4, bf16[256,16,32]{0,2,1:T(8,128)(2,1)S(1)} %all-to-all-done.1), kind=kOutput, calls=%fused_computation.513 | convolution fusion | flops 67895296 | bytes 1179648 | tf_op jit(solution)/shard_map/abc,ak->bck/dot_general | solution.py:166
  79.3 1.1 fusion.50
  80.5 0.9 fusion.60
  81.3 3.6 %all-to-all-start.2 = ((bf16[258,16,48]{0,2,1:T(8,128)(2,1)}), bf16[258,16,48]{0,2,1:T(8,128)(2,1)S(1)}, u32[]{:S(2)}, u32[]{:S(2)}) async-start(bf16[258,16,48]{0,2,1:T(8,128)(2,1)} %fusion.60), calls=%async_computation.2 | async-start | bytes 1179648 | tf_op jit(solution)/shard_map/all_to_all | solution.py:70
  85.7 1.3 %collective-permute-start.2 = (bf16[4,2,256]{2,1,0:T(2,128)(2,1)S(1)}, bf16[4,2,256]{2,1,0:T(2,128)(2,1)S(1)}, u32[]{:S(2)}, u32[]{:S(2)}) collective-permute-start(bf16[4,2,256]{2,1,0:T(2,128)(2,1)S(1)} %pad_maximum_fusion.3), channel_id=1, source_target_pairs={{16,0},{32,16},{48,32},{64,48},{80,64},{96,80},{112,96},{128,112},... | collective-permute-start | bytes 12296 | tf_op jit(solution)/shard_map/ppermute | solution.py:12
  87.0 4.2 %collective-permute-done.2 = bf16[4,2,256]{2,1,0:T(2,128)(2,1)S(1)} collective-permute-done((bf16[4,2,256]{2,1,0:T(2,128)(2,1)S(1)}, bf16[4,2,256]{2,1,0:T(2,128)(2,1)S(1)}, u32[]{:S(2)}, u32[]{:S(2)}) %collective-permute-start.2) | collective-permute-done | bytes 4128 | tf_op jit(solution)/shard_map/ppermute | solution.py:12
  91.2 10.9 %all-to-all-done.2 = bf16[258,16,48]{0,2,1:T(8,128)(2,1)S(1)} async-done(((bf16[258,16,48]{0,2,1:T(8,128)(2,1)}), bf16[258,16,48]{0,2,1:T(8,128)(2,1)S(1)}, u32[]{:S(2)}, u32[]{:S(2)}) %all-to-all-start.2) | async-done | bytes 396320 | tf_op jit(solution)/shard_map/all_to_all | solution.py:70
  102.2 0.8 copy.28
  104.2 1.6 %multiply_convert_fusion.1 = bf16[256,256]{1,0:T(8,128)(2,1)} fusion(f32[256,256]{1,0:T(8,128)S(1)} %copy.24, f32[3,256,256]{2,1,0:T(8,128)} %copy-done.1), kind=kLoop, calls=%fused_computation.199 | loop fusion | flops 131072 | bytes 655360 | tf_op jit(solution)/shard_map/convert_element_type | solution.py:211
  105.8 1.0 bitcast_convert_fusion.1
  106.9 1.0 fusion.105
  108.0 1.0 fusion.104
  (221 shorter events, 20.4 us)
Async XLA Ops:
  0.6 11.5 %copy-start = (bf16[4096,256]{1,0:T(8,128)(2,1)S(1)}, bf16[4096,256]{1,0:T(8,128)(2,1)}, u32[]{:S(2)}) copy-start(bf16[4096,256]{1,0:T(8,128)(2,1)} %param.8) | copy-start | bytes 6291460
  2.8 23.9 %all-to-all-start = ((bf16[8,256,256]{2,1,0:T(8,128)(2,1)}), bf16[8,256,256]{2,1,0:T(8,128)(2,1)}, u32[]{:S(2)}, u32[]{:S(2)}) async-start(bf16[8,256,256]{2,1,0:T(8,128)(2,1)} %broadcast_in_dim.737), calls=%async_computation | async-start | bytes 2097152 | tf_op jit(solution)/shard_map/all_to_all | solution.py:88
  12.1 2.7 %copy-start.41 = (f32[3,3,256]{2,1,0:T(4,128)S(1)}, f32[3,3,256]{2,1,0:T(4,128)}, u32[]{:S(2)}) copy-start(f32[3,3,256]{2,1,0:T(4,128)} %param.7) | copy-start | bytes 27652
  18.4 4.5 %copy-start.40 = (f32[3,1,1,256]{3,1,0,2:T(1,128)S(1)}, f32[3,1,1,256]{3,1,0,2:T(1,128)}, u32[]{:S(2)}) copy-start(f32[3,1,1,256]{3,1,0,2:T(1,128)} %get-tuple-element.228) | copy-start | bytes 9220
  20.4 3.1 %copy-start.5 = (bf16[256,256]{1,0:T(8,128)(2,1)S(1)}, bf16[256,256]{1,0:T(8,128)(2,1)}, u32[]{:S(2)}) copy-start(bf16[256,256]{1,0:T(8,128)(2,1)} %param.9) | copy-start | bytes 393220
  20.5 0.8 copy-start.2
  26.6 9.0 %collective-permute-start = (bf16[8,256,256]{2,1,0:T(8,128)(2,1)}, bf16[8,256,256]{2,1,0:T(8,128)(2,1)}, u32[]{:S(2)}, u32[]{:S(2)}) collective-permute-start(bf16[8,256,256]{2,1,0:T(8,128)(2,1)} %all-to-all-done), channel_id=1, source_target_pairs={{0,1},{1,0},{2,3},{3,2},{4,5},{5,4},{6,7},{7,6},{8,9},{9,8},{10,11... | collective-permute-start | bytes 3145736 | tf_op jit(solution)/shard_map/ppermute | solution.py:89
  29.7 10.9 %slice-start = ((s8[6291456]{0:T(1024)(128)(4,1)}), s8[4194304]{0:T(1024)(128)(4,1)S(1)}, s32[]{:S(2)}) async-start(s8[6291456]{0:T(1024)(128)(4,1)} %bitcast.224), calls=%async_computation.3 | async-start | bytes 8388608
  32.3 8.4 %slice-start.1 = ((s8[6291456]{0:T(1024)(128)(4,1)}), s8[2097152]{0:T(1024)(128)(4,1)S(1)}, s32[]{:S(2)}) async-start(s8[6291456]{0:T(1024)(128)(4,1)} %bitcast.224), calls=%async_computation.4 | async-start | bytes 4194304
  38.0 4.9 %collective-permute-start.1 = (bf16[3,2,256]{2,1,0:T(2,128)(2,1)S(1)}, bf16[3,2,256]{2,1,0:T(2,128)(2,1)S(1)}, u32[]{:S(2)}, u32[]{:S(2)}) collective-permute-start(bf16[3,2,256]{2,1,0:T(2,128)(2,1)S(1)} %fusion.47), channel_id=1, source_target_pairs={{0,16},{16,32},{32,48},{48,64},{64,80},{80,96},{96,112},{112,128},... | collective-permute-start | bytes 9224 | tf_op jit(solution)/shard_map/ppermute | solution.py:12
  43.6 0.9 copy-start.1
  47.9 22.6 %all-to-all-start.1 = ((bf16[256,16,32]{0,2,1:T(8,128)(2,1)}), bf16[256,16,32]{0,2,1:T(8,128)(2,1)S(1)}, u32[]{:S(2)}, u32[]{:S(2)}) async-start(bf16[256,16,32]{0,2,1:T(8,128)(2,1)} %pad_maximum_fusion.2), calls=%async_computation.1 | async-start | bytes 524288 | tf_op jit(solution)/shard_map/all_to_all | solution.py:70
  71.8 1.0 copy-start.3
  73.3 0.8 copy-start.9
  73.3 0.8 copy-start.38
  73.3 0.8 copy-start.39
  73.4 0.8 copy-start.36
  73.4 0.8 copy-start.37
  73.4 0.8 copy-start.34
  73.4 0.8 copy-start.35
  73.5 0.8 copy-start.32
  73.5 0.8 copy-start.33
  73.6 0.9 copy-start.26
  73.6 0.9 copy-start.27
  73.7 0.9 copy-start.22
  73.7 0.9 copy-start.23
  77.0 0.9 copy-start.6
  77.0 1.0 copy-start.7
  80.4 5.3 %copy-start.42 = (bf16[1,2,256]{2,1,0:T(2,128)(2,1)S(1)}, bf16[1,2,256]{2,1,0:T(2,128)(2,1)}, u32[]{:S(2)}) copy-start(bf16[1,2,256]{2,1,0:T(2,128)(2,1)} %slice_bitcast_fusion.38) | copy-start | bytes 3076
  81.3 20.8 %all-to-all-start.2 = ((bf16[258,16,48]{0,2,1:T(8,128)(2,1)}), bf16[258,16,48]{0,2,1:T(8,128)(2,1)S(1)}, u32[]{:S(2)}, u32[]{:S(2)}) async-start(bf16[258,16,48]{0,2,1:T(8,128)(2,1)} %fusion.60), calls=%async_computation.2 | async-start | bytes 1179648 | tf_op jit(solution)/shard_map/all_to_all | solution.py:70
  85.7 5.5 %collective-permute-start.2 = (bf16[4,2,256]{2,1,0:T(2,128)(2,1)S(1)}, bf16[4,2,256]{2,1,0:T(2,128)(2,1)S(1)}, u32[]{:S(2)}, u32[]{:S(2)}) collective-permute-start(bf16[4,2,256]{2,1,0:T(2,128)(2,1)S(1)} %pad_maximum_fusion.3), channel_id=1, source_target_pairs={{16,0},{32,16},{48,32},{64,48},{80,64},{96,80},{112,96},{128,112},... | collective-permute-start | bytes 12296 | tf_op jit(solution)/shard_map/ppermute | solution.py:12
  103.8 3.1 %copy-start.4 = (f32[1,256,256]{2,1,0:T(8,128)S(1)}, f32[1,256,256]{2,1,0:T(8,128)}, u32[]{:S(2)}) copy-start(f32[1,256,256]{2,1,0:T(8,128)} %get-tuple-element.21) | copy-start | bytes 786436
  (19 other events, 13.8 us)

commit v14 on v13

--- a/solution.py
+++ b/solution.py
@@ -119,12 +119,9 @@
     grad_long = (cotangent.astype(jnp.float32) * query_conv).astype(jnp.bfloat16)
 
     both_cols = swap_layout(
-        jnp.concatenate(
-            [gated.reshape(row_count, seq_count, group), grad_long.reshape(row_count, seq_count, group)],
-            axis=2,
-        )
-    )
-    gated_cols, grad_long_cols = (both_cols[..., :group], both_cols[..., group:])
+        jnp.concatenate([gated, grad_long], axis=0).reshape(2 * row_count, seq_count, group)
+    )
+    gated_cols, grad_long_cols = (both_cols[:row_count], both_cols[row_count:])
 
     after_rows, _ = lax.optimization_barrier(
         (jnp.concatenate([streams[:, :2], cotangent[None, :2]], axis=0), both_cols)

time: 110 us -> 108 us (0.982)
  other arithmetic: 22.1 us -> 20.5 us
    concatenate x1, other arithmetic: 1.63 us -> 0.02 us  [on_device(): jnp.concatenate([gated, grad_long], axis=0)]
where the time goes in v14:
time: 108 us; the launch traced here: 107 us
  starting transfers between devices  25.8 us (24%)
  local copies, waits for them, and re-layouts  23 us (21%)
  waiting for transfers between devices  22 us (20%)
  other arithmetic  20.5 us (19%)
  matrix products  14.1 us (13%)
  between operations  1.94 us (2%)
    all_to_all x2, waiting for transfers between devices, swap_layout(): return lax.all_to_all(values, 'seq', 1, 1, tiled=True)  17.8 us
    all_to_all x2, starting transfers between devices, swap_layout(): return lax.all_to_all(values, 'seq', 1, 1, tiled=True)  14.5 us
    all_to_all x1, starting transfers between devices, on_device(): lax.all_to_all(copies, 'chan', 0, 0, tiled=True, axis_index_groups=groups)  7.46 us
    unnamed x108, local copies, waits for them, and re-layouts  6.28 us
    another operation x4, other arithmetic  5.81 us
    mul x8, local copies, waits for them, and re-layouts, spectral_product(): real_out = left_re * right_re - jnp.where(first_row, 0.0, cross_term)  4.99 us
    ppermute x2, waiting for transfers between devices, passed_along(): return lax.ppermute(block, axis, route)  4.2 us
    ppermute x2, starting transfers between devices, passed_along(): return lax.ppermute(block, axis, route)  3.87 us
  transfers between devices with their start and end apart: 6, of which 3 were waited for; matrix products, arithmetic and copies ran while one was open for 30% of the time, Pallas kernels for 0%

profile of v14, /device:TPU:2, one launch (start us, length us, event | category | flops | bytes accessed | tf_op | source)
XLA Modules:
  0.0 107.4 jit_solution(7150614261296167579)
XLA Ops:
  0.6 2.1 %broadcast_in_dim.737 = bf16[8,256,256]{2,1,0:T(8,128)(2,1)} broadcast(bf16[256,256]{1,0:T(8,128)(2,1)} %param.5), dimensions={1,2} | broadcast | bytes 1179648 | tf_op jit(solution)/shard_map/broadcast_in_dim | solution.py:87
  2.8 7.5 %all-to-all-start = ((bf16[8,256,256]{2,1,0:T(8,128)(2,1)}), bf16[8,256,256]{2,1,0:T(8,128)(2,1)}, u32[]{:S(2)}, u32[]{:S(2)}) async-start(bf16[8,256,256]{2,1,0:T(8,128)(2,1)} %broadcast_in_dim.737), calls=%async_computation | async-start | bytes 2097152 | tf_op jit(solution)/shard_map/all_to_all | solution.py:88
  10.2 1.9 %fusion.116 = f32[256,512]{1,0:T(8,128)S(1)} fusion(), kind=kLoop, calls=%fused_computation.208 | loop fusion | flops 1835008 | bytes 524288 | tf_op jit(solution)/shard_map/cos | solution.py:24
  12.2 1.3 %constant_dynamic-slice_fusion = bf16[3840,16]{1,0:T(8,128)(2,1)} fusion(bf16[4096,256]{1,0:T(8,128)(2,1)S(1)} %copy-done, s32[]{:T(128)S(6)} %select_n.396), kind=kLoop, calls=%fused_computation.493 | loop fusion | bytes 245764 | tf_op jit(solution)/shard_map/slice | solution.py:147
  13.5 1.3 %constant_dynamic-slice_fusion.1 = bf16[4096,16]{1,0:T(8,128)(2,1)} fusion(bf16[4096,256]{1,0:T(8,128)(2,1)S(1)} %copy-done, s32[]{:T(128)S(6)} %select_n.396), kind=kLoop, calls=%fused_computation.494 | loop fusion | bytes 262148 | tf_op jit(solution)/shard_map/dynamic_slice | solution.py:144
  15.4 1.5 %copy.18 = bf16[15,256,16]{1,2,0:T(8,128)(2,1)S(1)} copy(bf16[15,256,16]{2,1,0:T(8,128)(2,1)} %bitcast.229) | data formatting | bytes 245760 | tf_op jit(solution)/shard_map/slice | solution.py:147
  16.9 1.5 %copy.20 = bf16[16,256,16]{1,2,0:T(8,128)(2,1)S(1)} copy(bf16[16,256,16]{2,1,0:T(8,128)(2,1)} %bitcast.228) | data formatting | bytes 262144 | tf_op jit(solution)/shard_map/reshape | solution.py:145
  18.4 2.0 %negate_select_fusion.2 = f32[256,512]{1,0:T(8,128)S(1)} fusion(f32[512]{0:T(512)S(1)} %fusion.131, pred[256]{0:T(512)(128)(4,1)S(1)} %iota_compare_fusion.36), kind=kLoop, calls=%fused_computation.162 | loop fusion | flops 2097152 | bytes 526592 | tf_op jit(solution)/shard_map/jit(_where)/select_n | solution.py:23
  29.7 2.6 %fusion.35 = f32[3,256,2]{1,2,0:T(2,128)S(1)} fusion(bf16[8,2,256,3,256]{4,2,1,0,3:T(8,128)(2,1)} %bitcast.222, s32[]{:T(128)S(6)} %select_n.390, bf16[8,256,256]{2,1,0:T(8,128)(2,1)} %all-to-all-done), kind=kOutput, calls=%fused_computation.35 | convolution fusion | flops 6291456 | bytes 3160068 | tf_op jit(solution)/shard_map/stf,sfqc->qtc/dot_general | solution.py:100
  32.3 3.3 %fusion.12 = f32[3,256,256]{1,2,0:T(8,128)S(1)} fusion(bf16[8,2,256,3,256]{4,2,1,0,3:T(8,128)(2,1)} %bitcast.223, s32[]{:T(128)S(6)} %select_n.390, bf16[8,256,256]{2,1,0:T(8,128)(2,1)} %all-to-all-done), kind=kOutput, calls=%fused_computation.14 | convolution fusion | flops 805306368 | bytes 4980740 | tf_op jit(solution)/shard_map/stf,sfqc->qtc/dot_general | solution.py:94
  35.6 2.4 %fusion.47 = bf16[3,2,256]{2,1,0:T(2,128)(2,1)S(1)} fusion(f32[3,256,2]{1,2,0:T(2,128)S(1)} %fusion.35, bf16[8,2,256,3,256]{4,2,1,0,3:T(8,128)(2,1)} %bitcast.224, s32[]{:T(128)S(6)} %select_n.391, bf16[8,256,256]{2,1,0:T(8,128)(2,1)} %collective-permute-done), kind=kOutput, calls=%fused_computation.39 | convolution fusion | flops 6294528 | bytes 3163140 | tf_op jit(solution)/shard_map/stf,sfqc->qtc/dot_general | solution.py:104
  38.0 2.6 %collective-permute-start.1 = (bf16[3,2,256]{2,1,0:T(2,128)(2,1)S(1)}, bf16[3,2,256]{2,1,0:T(2,128)(2,1)S(1)}, u32[]{:S(2)}, u32[]{:S(2)}) collective-permute-start(bf16[3,2,256]{2,1,0:T(2,128)(2,1)S(1)} %fusion.47), channel_id=1, source_target_pairs={{0,16},{16,32},{32,48},{48,64},{64,80},{80,96},{96,112},{112,128},... | collective-permute-start | bytes 9224 | tf_op jit(solution)/shard_map/ppermute | solution.py:12
  40.7 2.2 %fusion.24 = bf16[3,256,256]{2,1,0:T(8,128)(2,1)S(1)} fusion(f32[3,256,256]{1,2,0:T(8,128)S(1)} %fusion.12, bf16[8,2,256,3,256]{4,2,1,0,3:T(8,128)(2,1)S(1)} %bitcast.227, s32[]{:T(128)S(6)} %select_n.391, bf16[8,256,256]{2,1,0:T(8,128)(2,1)} %collective-permute-done), kind=kOutput, calls=%fused_computation.18 | convolution fusion | flops 805699584 | bytes 5373956 | tf_op jit(solution)/shard_map/stf,sfqc->qtc/dot_general | solution.py:95
  43.7 0.9 copy-done.1
  44.6 0.8 fusion.184
  45.4 0.8 copy.21
  46.3 10.9 %all-to-all-start.1 = ((bf16[512,16,16]{0,2,1:T(8,128)(2,1)}), bf16[512,16,16]{0,2,1:T(8,128)(2,1)S(1)}, u32[]{:S(2)}, u32[]{:S(2)}) async-start(bf16[512,16,16]{0,2,1:T(8,128)(2,1)} %bitcast.230), calls=%async_computation.1 | async-start | bytes 524288 | tf_op jit(solution)/shard_map/all_to_all | solution.py:70
  57.2 2.4 %multiply_convert_fusion.4 = bf16[256,256]{1,0:T(8,128)(2,1)} fusion(f32[256]{0:T(256)} %select_multiply_fusion, s32[256]{0:T(256)} %iota_add_fusion), kind=kLoop, calls=%fused_computation.210 | loop fusion | flops 1048576 | bytes 133120 | tf_op jit(solution)/shard_map/convert.8
  59.6 2.4 %select_convert_fusion = bf16[256,256]{1,0:T(8,128)(2,1)} fusion(bf16[256]{0:T(256)(128)(2,1)S(1)} %fusion.168, s32[256]{0:T(256)} %iota_add_fusion, pred[256]{0:T(512)(128)(4,1)S(1)} %iota_compare_fusion.36), kind=kLoop, calls=%fused_computation.209 | loop fusion | flops 1048576 | bytes 132864 | tf_op jit(solution)/shard_map/convert.9
  61.9 6.9 %all-to-all-done.1 = bf16[512,16,16]{0,2,1:T(8,128)(2,1)S(1)} async-done(((bf16[512,16,16]{0,2,1:T(8,128)(2,1)}), bf16[512,16,16]{0,2,1:T(8,128)(2,1)S(1)}, u32[]{:S(2)}, u32[]{:S(2)}) %all-to-all-start.1) | async-done | bytes 262176 | tf_op jit(solution)/shard_map/all_to_all | solution.py:70
  68.8 1.2 %fusion.191 = (f32[16,16,512]{2,1,0:T(8,128)S(1)}, bf16[16,16,512]{2,1,0:T(8,128)(2,1)S(1)}) fusion(bf16[256,256]{1,0:T(8,128)(2,1)} %select_convert_fusion, bf16[256,256]{1,0:T(8,128)(2,1)} %multiply_convert_fusion.4, bf16[512,16,16]{0,2,1:T(8,128)(2,1)S(1)} %all-to-all-done.1), kind=kOutput, calls=%fused_computation.514 | convolution fusion | flops 67895296 | bytes 1179648 | tf_op jit(solution)/shard_map/abc,ak->bck/dot_general | solution.py:163
  77.7 1.1 fusion.50
  78.8 0.9 fusion.60
  79.7 3.6 %all-to-all-start.2 = ((bf16[258,16,48]{0,2,1:T(8,128)(2,1)}), bf16[258,16,48]{0,2,1:T(8,128)(2,1)S(1)}, u32[]{:S(2)}, u32[]{:S(2)}) async-start(bf16[258,16,48]{0,2,1:T(8,128)(2,1)} %fusion.60), calls=%async_computation.2 | async-start | bytes 1179648 | tf_op jit(solution)/shard_map/all_to_all | solution.py:70
  84.0 1.3 %collective-permute-start.2 = (bf16[4,2,256]{2,1,0:T(2,128)(2,1)S(1)}, bf16[4,2,256]{2,1,0:T(2,128)(2,1)S(1)}, u32[]{:S(2)}, u32[]{:S(2)}) collective-permute-start(bf16[4,2,256]{2,1,0:T(2,128)(2,1)S(1)} %pad_maximum_fusion.3), channel_id=1, source_target_pairs={{16,0},{32,16},{48,32},{64,48},{80,64},{96,80},{112,96},{128,112},... | collective-permute-start | bytes 12296 | tf_op jit(solution)/shard_map/ppermute | solution.py:12
  85.3 4.2 %collective-permute-done.2 = bf16[4,2,256]{2,1,0:T(2,128)(2,1)S(1)} collective-permute-done((bf16[4,2,256]{2,1,0:T(2,128)(2,1)S(1)}, bf16[4,2,256]{2,1,0:T(2,128)(2,1)S(1)}, u32[]{:S(2)}, u32[]{:S(2)}) %collective-permute-start.2) | collective-permute-done | bytes 4128 | tf_op jit(solution)/shard_map/ppermute | solution.py:12
  89.6 10.9 %all-to-all-done.2 = bf16[258,16,48]{0,2,1:T(8,128)(2,1)S(1)} async-done(((bf16[258,16,48]{0,2,1:T(8,128)(2,1)}), bf16[258,16,48]{0,2,1:T(8,128)(2,1)S(1)}, u32[]{:S(2)}, u32[]{:S(2)}) %all-to-all-start.2) | async-done | bytes 396320 | tf_op jit(solution)/shard_map/all_to_all | solution.py:70
  100.6 0.8 copy.26
  102.5 1.6 %multiply_convert_fusion.1 = bf16[256,256]{1,0:T(8,128)(2,1)} fusion(f32[256,256]{1,0:T(8,128)S(1)} %copy.22, f32[3,256,256]{2,1,0:T(8,128)} %copy-done.1), kind=kLoop, calls=%fused_computation.199 | loop fusion | flops 131072 | bytes 655360 | tf_op jit(solution)/shard_map/convert_element_type | solution.py:208
  104.2 1.0 bitcast_convert_fusion.1
  105.3 1.0 fusion.105
  106.4 1.0 fusion.104
  (220 shorter events, 19.5 us)
Async XLA Ops:
  0.6 11.5 %copy-start = (bf16[4096,256]{1,0:T(8,128)(2,1)S(1)}, bf16[4096,256]{1,0:T(8,128)(2,1)}, u32[]{:S(2)}) copy-start(bf16[4096,256]{1,0:T(8,128)(2,1)} %param.8) | copy-start | bytes 6291460
  2.8 23.9 %all-to-all-start = ((bf16[8,256,256]{2,1,0:T(8,128)(2,1)}), bf16[8,256,256]{2,1,0:T(8,128)(2,1)}, u32[]{:S(2)}, u32[]{:S(2)}) async-start(bf16[8,256,256]{2,1,0:T(8,128)(2,1)} %broadcast_in_dim.737), calls=%async_computation | async-start | bytes 2097152 | tf_op jit(solution)/shard_map/all_to_all | solution.py:88
  12.1 2.7 %copy-start.41 = (f32[3,3,256]{2,1,0:T(4,128)S(1)}, f32[3,3,256]{2,1,0:T(4,128)}, u32[]{:S(2)}) copy-start(f32[3,3,256]{2,1,0:T(4,128)} %param.7) | copy-start | bytes 27652
  18.4 4.5 %copy-start.40 = (f32[3,1,1,256]{3,1,0,2:T(1,128)S(1)}, f32[3,1,1,256]{3,1,0,2:T(1,128)}, u32[]{:S(2)}) copy-start(f32[3,1,1,256]{3,1,0,2:T(1,128)} %get-tuple-element.228) | copy-start | bytes 9220
  20.4 3.1 %copy-start.5 = (bf16[256,256]{1,0:T(8,128)(2,1)S(1)}, bf16[256,256]{1,0:T(8,128)(2,1)}, u32[]{:S(2)}) copy-start(bf16[256,256]{1,0:T(8,128)(2,1)} %param.9) | copy-start | bytes 393220
  20.5 0.8 copy-start.2
  26.6 9.0 %collective-permute-start = (bf16[8,256,256]{2,1,0:T(8,128)(2,1)}, bf16[8,256,256]{2,1,0:T(8,128)(2,1)}, u32[]{:S(2)}, u32[]{:S(2)}) collective-permute-start(bf16[8,256,256]{2,1,0:T(8,128)(2,1)} %all-to-all-done), channel_id=1, source_target_pairs={{0,1},{1,0},{2,3},{3,2},{4,5},{5,4},{6,7},{7,6},{8,9},{9,8},{10,11... | collective-permute-start | bytes 3145736 | tf_op jit(solution)/shard_map/ppermute | solution.py:89
  29.7 10.9 %slice-start = ((s8[6291456]{0:T(1024)(128)(4,1)}), s8[4194304]{0:T(1024)(128)(4,1)S(1)}, s32[]{:S(2)}) async-start(s8[6291456]{0:T(1024)(128)(4,1)} %bitcast.225), calls=%async_computation.3 | async-start | bytes 8388608
  32.3 8.4 %slice-start.1 = ((s8[6291456]{0:T(1024)(128)(4,1)}), s8[2097152]{0:T(1024)(128)(4,1)S(1)}, s32[]{:S(2)}) async-start(s8[6291456]{0:T(1024)(128)(4,1)} %bitcast.225), calls=%async_computation.4 | async-start | bytes 4194304
  38.0 4.9 %collective-permute-start.1 = (bf16[3,2,256]{2,1,0:T(2,128)(2,1)S(1)}, bf16[3,2,256]{2,1,0:T(2,128)(2,1)S(1)}, u32[]{:S(2)}, u32[]{:S(2)}) collective-permute-start(bf16[3,2,256]{2,1,0:T(2,128)(2,1)S(1)} %fusion.47), channel_id=1, source_target_pairs={{0,16},{16,32},{32,48},{48,64},{64,80},{80,96},{96,112},{112,128},... | collective-permute-start | bytes 9224 | tf_op jit(solution)/shard_map/ppermute | solution.py:12
  43.6 0.9 copy-start.1
  46.3 22.6 %all-to-all-start.1 = ((bf16[512,16,16]{0,2,1:T(8,128)(2,1)}), bf16[512,16,16]{0,2,1:T(8,128)(2,1)S(1)}, u32[]{:S(2)}, u32[]{:S(2)}) async-start(bf16[512,16,16]{0,2,1:T(8,128)(2,1)} %bitcast.230), calls=%async_computation.1 | async-start | bytes 524288 | tf_op jit(solution)/shard_map/all_to_all | solution.py:70
  70.2 1.0 copy-start.3
  71.7 0.8 copy-start.9
  71.7 0.8 copy-start.38
  71.7 0.8 copy-start.39
  71.7 0.8 copy-start.36
  71.7 0.8 copy-start.37
  71.8 0.8 copy-start.34
  71.8 0.8 copy-start.35
  71.9 0.8 copy-start.32
  71.9 0.8 copy-start.33
  72.0 0.9 copy-start.26
  72.0 0.9 copy-start.27
  72.0 0.9 copy-start.22
  72.0 0.9 copy-start.23
  75.3 0.9 copy-start.6
  75.3 1.0 copy-start.7
  78.7 5.3 %copy-start.42 = (bf16[1,2,256]{2,1,0:T(2,128)(2,1)S(1)}, bf16[1,2,256]{2,1,0:T(2,128)(2,1)}, u32[]{:S(2)}) copy-start(bf16[1,2,256]{2,1,0:T(2,128)(2,1)} %slice_bitcast_fusion.38) | copy-start | bytes 3076
  79.7 20.9 %all-to-all-start.2 = ((bf16[258,16,48]{0,2,1:T(8,128)(2,1)}), bf16[258,16,48]{0,2,1:T(8,128)(2,1)S(1)}, u32[]{:S(2)}, u32[]{:S(2)}) async-start(bf16[258,16,48]{0,2,1:T(8,128)(2,1)} %fusion.60), calls=%async_computation.2 | async-start | bytes 1179648 | tf_op jit(solution)/shard_map/all_to_all | solution.py:70
  84.0 5.5 %collective-permute-start.2 = (bf16[4,2,256]{2,1,0:T(2,128)(2,1)S(1)}, bf16[4,2,256]{2,1,0:T(2,128)(2,1)S(1)}, u32[]{:S(2)}, u32[]{:S(2)}) collective-permute-start(bf16[4,2,256]{2,1,0:T(2,128)(2,1)S(1)} %pad_maximum_fusion.3), channel_id=1, source_target_pairs={{16,0},{32,16},{48,32},{64,48},{80,64},{96,80},{112,96},{128,112},... | collective-permute-start | bytes 12296 | tf_op jit(solution)/shard_map/ppermute | solution.py:12
  102.2 3.1 %copy-start.4 = (f32[1,256,256]{2,1,0:T(8,128)S(1)}, f32[1,256,256]{2,1,0:T(8,128)}, u32[]{:S(2)}) copy-start(f32[1,256,256]{2,1,0:T(8,128)} %get-tuple-element.21) | copy-start | bytes 786436
  (19 other events, 13.8 us)

commit v15 on v14

--- a/solution.py
+++ b/solution.py
@@ -190,20 +190,13 @@
         )
         return jnp.concatenate([cols, following], axis=0)
 
+    wide_rows = row_count + 2
     returned = swap_layout(
-        jnp.concatenate(
-            [
-                with_next_rows(long_cols),
-                with_next_rows(gated_grad_cols),
-                jnp.concatenate([tap_cols, jnp.zeros((2, seq_count, group), jnp.bfloat16)], axis=0),
-            ],
-            axis=2,
-        )
-    )
-    wide_rows = row_count + 2
-    long_out = returned[..., :group].reshape(wide_rows, local_width).astype(jnp.float32)
-    gated_wide = returned[..., group : 2 * group].reshape(wide_rows, local_width).astype(jnp.float32)
-    tap_grads = returned[:row_count, :, 2 * group :].astype(jnp.float32).reshape(row_count, local_width)
+        jnp.concatenate([with_next_rows(long_cols), with_next_rows(gated_grad_cols), tap_cols], axis=0)
+    )
+    long_out = returned[:wide_rows].reshape(wide_rows, local_width).astype(jnp.float32)
+    gated_wide = returned[wide_rows : 2 * wide_rows].reshape(wide_rows, local_width).astype(jnp.float32)
+    tap_grads = returned[2 * wide_rows :].astype(jnp.float32).reshape(row_count, local_width)
 
     operator_out = (query_conv[:row_count] * long_out[:row_count]).astype(jnp.bfloat16)
     grad_query = cot_wide * long_out

time: 108 us -> 108 us (level)
  waiting for transfers between devices: 22 us -> 18 us
  local copies, waits for them, and re-layouts: 23 us -> 25.5 us
    all_to_all x2, waiting for transfers between devices: 17.8 us -> 13.8 us  [swap_layout(): return lax.all_to_all(values, 'seq', 1, 1, tiled=True)]
    concatenate x0 -> x3, local copies, waits for them, and re-layouts: none -> 3.3 us  [the longest x1 1.99 us: on_device(): jnp.concatenate([with_next_rows(long_cols), with_next_rows(gated_grad_col...]
    add x1 -> x17, other arithmetic: 0.01 us -> 2.06 us  [spectral_adjoint(): real_out = left_re * grad_re + jnp.where(first_row, 0.0, cross_term)]
    sub x16 -> x0, other arithmetic: 2.03 us -> none  [spectral_product(): real_out = left_re * right_re - jnp.where(first_row, 0.0, cross_term)]
    unnamed x108 -> x106, local copies, waits for them, and re-layouts: 6.28 us -> 5.28 us
  transfers between devices with their start and end apart: 6 -> 6, of which waited for: 3 -> 3; matrix products, arithmetic and copies ran while one was open for 30% -> 32% of each run, Pallas kernels for 0% -> 0%
where the time goes in v15:
time: 108 us; the launch traced here: 106 us
  starting transfers between devices  26.3 us (24%)
  local copies, waits for them, and re-layouts  25.5 us (24%)
  other arithmetic  20.4 us (19%)
  waiting for transfers between devices  18 us (17%)
  matrix products  14.1 us (13%)
  between operations  2.12 us (2%)
    all_to_all x2, starting transfers between devices, swap_layout(): return lax.all_to_all(values, 'seq', 1, 1, tiled=True)  14.9 us
    all_to_all x2, waiting for transfers between devices, swap_layout(): return lax.all_to_all(values, 'seq', 1, 1, tiled=True)  13.8 us
    all_to_all x1, starting transfers between devices, on_device(): lax.all_to_all(copies, 'chan', 0, 0, tiled=True, axis_index_groups=groups)  7.59 us
    another operation x4, other arithmetic  5.84 us
    unnamed x106, local copies, waits for them, and re-layouts  5.28 us
    mul x8, local copies, waits for them, and re-layouts, spectral_product(): real_out = left_re * right_re - jnp.where(first_row, 0.0, cross_term)  5.03 us
    ppermute x2, waiting for transfers between devices, passed_along(): return lax.ppermute(block, axis, route)  4.2 us
    ppermute x2, starting transfers between devices, passed_along(): return lax.ppermute(block, axis, route)  3.87 us
  transfers between devices with their start and end apart: 6, of which 3 were waited for; matrix products, arithmetic and copies ran while one was open for 32% of the time, Pallas kernels for 0%

profile of v15, /device:TPU:2, one launch (start us, length us, event | category | flops | bytes accessed | tf_op | source)
XLA Modules:
  0.0 106.5 jit_solution(10288121538083410685)
XLA Ops:
  0.6 2.1 %broadcast_in_dim.736 = bf16[8,256,256]{2,1,0:T(8,128)(2,1)} broadcast(bf16[256,256]{1,0:T(8,128)(2,1)} %param.5), dimensions={1,2} | broadcast | bytes 1179648 | tf_op jit(solution)/shard_map/broadcast_in_dim | solution.py:87
  2.7 7.6 %all-to-all-start = ((bf16[8,256,256]{2,1,0:T(8,128)(2,1)}), bf16[8,256,256]{2,1,0:T(8,128)(2,1)}, u32[]{:S(2)}, u32[]{:S(2)}) async-start(bf16[8,256,256]{2,1,0:T(8,128)(2,1)} %broadcast_in_dim.736), calls=%async_computation | async-start | bytes 2097152 | tf_op jit(solution)/shard_map/all_to_all | solution.py:88
  10.3 1.9 %fusion.104 = f32[256,512]{1,0:T(8,128)S(1)} fusion(), kind=kLoop, calls=%fused_computation.191 | loop fusion | flops 1835008 | bytes 524288 | tf_op jit(solution)/shard_map/cos | solution.py:24
  12.3 1.3 %constant_dynamic-slice_fusion = bf16[3840,16]{1,0:T(8,128)(2,1)} fusion(bf16[4096,256]{1,0:T(8,128)(2,1)S(1)} %copy-done, s32[]{:T(128)S(6)} %select_n.396), kind=kLoop, calls=%fused_computation.476 | loop fusion | bytes 245764 | tf_op jit(solution)/shard_map/slice | solution.py:147
  13.6 1.3 %constant_dynamic-slice_fusion.1 = bf16[4096,16]{1,0:T(8,128)(2,1)} fusion(bf16[4096,256]{1,0:T(8,128)(2,1)S(1)} %copy-done, s32[]{:T(128)S(6)} %select_n.396), kind=kLoop, calls=%fused_computation.477 | loop fusion | bytes 262148 | tf_op jit(solution)/shard_map/dynamic_slice | solution.py:144
  15.5 1.5 %copy.18 = bf16[15,256,16]{1,2,0:T(8,128)(2,1)S(1)} copy(bf16[15,256,16]{2,1,0:T(8,128)(2,1)} %bitcast.229) | data formatting | bytes 245760 | tf_op jit(solution)/shard_map/slice | solution.py:147
  17.0 1.6 %copy.20 = bf16[16,256,16]{1,2,0:T(8,128)(2,1)S(1)} copy(bf16[16,256,16]{2,1,0:T(8,128)(2,1)} %bitcast.228) | data formatting | bytes 262144 | tf_op jit(solution)/shard_map/reshape | solution.py:145
  18.6 2.0 %negate_select_fusion.2 = f32[256,512]{1,0:T(8,128)S(1)} fusion(f32[512]{0:T(512)S(1)} %fusion.119, pred[256]{0:T(512)(128)(4,1)S(1)} %iota_compare_fusion.31), kind=kLoop, calls=%fused_computation.145 | loop fusion | flops 2097152 | bytes 526592 | tf_op jit(solution)/shard_map/jit(_where)/select_n | solution.py:23
  30.6 2.6 %fusion.27 = f32[3,256,2]{1,2,0:T(2,128)S(1)} fusion(bf16[8,2,256,3,256]{4,2,1,0,3:T(8,128)(2,1)} %bitcast.222, s32[]{:T(128)S(6)} %select_n.390, bf16[8,256,256]{2,1,0:T(8,128)(2,1)} %all-to-all-done), kind=kOutput, calls=%fused_computation.22 | convolution fusion | flops 6291456 | bytes 3160068 | tf_op jit(solution)/shard_map/stf,sfqc->qtc/dot_general | solution.py:100
  33.2 3.3 %fusion.12 = f32[3,256,256]{1,2,0:T(8,128)S(1)} fusion(bf16[8,2,256,3,256]{4,2,1,0,3:T(8,128)(2,1)} %bitcast.223, s32[]{:T(128)S(6)} %select_n.390, bf16[8,256,256]{2,1,0:T(8,128)(2,1)} %all-to-all-done), kind=kOutput, calls=%fused_computation.12 | convolution fusion | flops 805306368 | bytes 4980740 | tf_op jit(solution)/shard_map/stf,sfqc->qtc/dot_general | solution.py:94
  36.5 2.4 %fusion.39 = bf16[3,2,256]{2,1,0:T(2,128)(2,1)S(1)} fusion(f32[3,256,2]{1,2,0:T(2,128)S(1)} %fusion.27, bf16[8,2,256,3,256]{4,2,1,0,3:T(8,128)(2,1)} %bitcast.224, s32[]{:T(128)S(6)} %select_n.391, bf16[8,256,256]{2,1,0:T(8,128)(2,1)} %collective-permute-done), kind=kOutput, calls=%fused_computation.26 | convolution fusion | flops 6294528 | bytes 3163140 | tf_op jit(solution)/shard_map/stf,sfqc->qtc/dot_general | solution.py:104
  38.9 2.6 %collective-permute-start.1 = (bf16[3,2,256]{2,1,0:T(2,128)(2,1)S(1)}, bf16[3,2,256]{2,1,0:T(2,128)(2,1)S(1)}, u32[]{:S(2)}, u32[]{:S(2)}) collective-permute-start(bf16[3,2,256]{2,1,0:T(2,128)(2,1)S(1)} %fusion.39), channel_id=1, source_target_pairs={{0,16},{16,32},{32,48},{48,64},{64,80},{80,96},{96,112},{112,128},... | collective-permute-start | bytes 9224 | tf_op jit(solution)/shard_map/ppermute | solution.py:12
  41.6 2.2 %fusion.24 = bf16[3,256,256]{2,1,0:T(8,128)(2,1)S(1)} fusion(f32[3,256,256]{1,2,0:T(8,128)S(1)} %fusion.12, bf16[8,2,256,3,256]{4,2,1,0,3:T(8,128)(2,1)S(1)} %bitcast.227, s32[]{:T(128)S(6)} %select_n.391, bf16[8,256,256]{2,1,0:T(8,128)(2,1)} %collective-permute-done), kind=kOutput, calls=%fused_computation.16 | convolution fusion | flops 805699584 | bytes 5373956 | tf_op jit(solution)/shard_map/stf,sfqc->qtc/dot_general | solution.py:95
  44.2 0.8 copy-done.1
  45.0 0.8 fusion.172
  45.9 0.8 copy.21
  46.7 11.3 %all-to-all-start.1 = ((bf16[512,16,16]{0,2,1:T(8,128)(2,1)}), bf16[512,16,16]{0,2,1:T(8,128)(2,1)S(1)}, u32[]{:S(2)}, u32[]{:S(2)}) async-start(bf16[512,16,16]{0,2,1:T(8,128)(2,1)} %bitcast.230), calls=%async_computation.1 | async-start | bytes 524288 | tf_op jit(solution)/shard_map/all_to_all | solution.py:70
  58.1 2.4 %multiply_convert_fusion.4 = bf16[256,256]{1,0:T(8,128)(2,1)} fusion(f32[256]{0:T(256)} %select_multiply_fusion, s32[256]{0:T(256)} %iota_add_fusion), kind=kLoop, calls=%fused_computation.193 | loop fusion | flops 1048576 | bytes 133120 | tf_op jit(solution)/shard_map/convert.8
  60.5 2.4 %select_convert_fusion = bf16[256,256]{1,0:T(8,128)(2,1)} fusion(bf16[256]{0:T(256)(128)(2,1)S(1)} %fusion.156, s32[256]{0:T(256)} %iota_add_fusion, pred[256]{0:T(512)(128)(4,1)S(1)} %iota_compare_fusion.31), kind=kLoop, calls=%fused_computation.192 | loop fusion | flops 1048576 | bytes 132864 | tf_op jit(solution)/shard_map/convert.9
  62.8 6.9 %all-to-all-done.1 = bf16[512,16,16]{0,2,1:T(8,128)(2,1)S(1)} async-done(((bf16[512,16,16]{0,2,1:T(8,128)(2,1)}), bf16[512,16,16]{0,2,1:T(8,128)(2,1)S(1)}, u32[]{:S(2)}, u32[]{:S(2)}) %all-to-all-start.1) | async-done | bytes 262176 | tf_op jit(solution)/shard_map/all_to_all | solution.py:70
  69.7 1.2 %fusion.178 = (f32[16,16,512]{2,1,0:T(8,128)S(1)}, bf16[16,16,512]{2,1,0:T(8,128)(2,1)S(1)}) fusion(bf16[256,256]{1,0:T(8,128)(2,1)} %select_convert_fusion, bf16[256,256]{1,0:T(8,128)(2,1)} %multiply_convert_fusion.4, bf16[512,16,16]{0,2,1:T(8,128)(2,1)S(1)} %all-to-all-done.1), kind=kOutput, calls=%fused_computation.496 | convolution fusion | flops 67895296 | bytes 1179648 | tf_op jit(solution)/shard_map/abc,ak->bck/dot_general | solution.py:163
  78.8 1.1 fusion.42
  80.0 2.0 %concatenate.270 = bf16[772,16,16]{0,2,1:T(8,128)(2,1)} concatenate(bf16[256,16,16]{0,2,1:T(8,128)(2,1)S(1)} %convolution_convert_fusion.4, bf16[2,16,16]{0,2,1:T(8,128)(2,1)} %concatenate.235, bf16[256,16,16]{0,2,1:T(8,128)(2,1)} %copy-done.10, bf16[2,16,16]{0,2,1:T(8,128)(2,1)} %concatenate.252, bf16[256,16,16]{0,2,1:T(8,128)(2,1)S(1)} %fusion.111), dimensions={0} | concatenate | bytes 790528 | tf_op jit(solution)/shard_map/concatenate | solution.py:195
  81.9 3.6 %all-to-all-start.2 = ((bf16[772,16,16]{0,2,1:T(8,128)(2,1)}), bf16[772,16,16]{0,2,1:T(8,128)(2,1)S(1)}, u32[]{:S(2)}, u32[]{:S(2)}) async-start(bf16[772,16,16]{0,2,1:T(8,128)(2,1)} %concatenate.270), calls=%async_computation.2 | async-start | bytes 917504 | tf_op jit(solution)/shard_map/all_to_all | solution.py:70
  86.9 1.3 %collective-permute-start.2 = (bf16[4,2,256]{2,1,0:T(2,128)(2,1)S(1)}, bf16[4,2,256]{2,1,0:T(2,128)(2,1)S(1)}, u32[]{:S(2)}, u32[]{:S(2)}) collective-permute-start(bf16[4,2,256]{2,1,0:T(2,128)(2,1)S(1)} %pad_maximum_fusion.3), channel_id=1, source_target_pairs={{16,0},{32,16},{48,32},{64,48},{80,64},{96,80},{112,96},{128,112},... | collective-permute-start | bytes 12296 | tf_op jit(solution)/shard_map/ppermute | solution.py:12
  88.2 4.2 %collective-permute-done.2 = bf16[4,2,256]{2,1,0:T(2,128)(2,1)S(1)} collective-permute-done((bf16[4,2,256]{2,1,0:T(2,128)(2,1)S(1)}, bf16[4,2,256]{2,1,0:T(2,128)(2,1)S(1)}, u32[]{:S(2)}, u32[]{:S(2)}) %collective-permute-start.2) | collective-permute-done | bytes 4128 | tf_op jit(solution)/shard_map/ppermute | solution.py:12
  92.5 6.9 %all-to-all-done.2 = bf16[772,16,16]{0,2,1:T(8,128)(2,1)S(1)} async-done(((bf16[772,16,16]{0,2,1:T(8,128)(2,1)}), bf16[772,16,16]{0,2,1:T(8,128)(2,1)S(1)}, u32[]{:S(2)}, u32[]{:S(2)}) %all-to-all-start.2) | async-done | bytes 395296 | tf_op jit(solution)/shard_map/all_to_all | solution.py:70
  99.6 0.8 copy.26
  101.6 1.6 %multiply_convert_fusion.1 = bf16[256,256]{1,0:T(8,128)(2,1)} fusion(f32[256,256]{1,0:T(8,128)S(1)} %copy.22, f32[3,256,256]{2,1,0:T(8,128)} %copy-done.1), kind=kLoop, calls=%fused_computation.182 | loop fusion | flops 131072 | bytes 655360 | tf_op jit(solution)/shard_map/convert_element_type | solution.py:201
  103.2 1.0 bitcast_convert_fusion.1
  104.4 1.0 fusion.93
  105.5 1.0 fusion.92
  (220 shorter events, 20.8 us)
Async XLA Ops:
  0.6 11.6 %copy-start = (bf16[4096,256]{1,0:T(8,128)(2,1)S(1)}, bf16[4096,256]{1,0:T(8,128)(2,1)}, u32[]{:S(2)}) copy-start(bf16[4096,256]{1,0:T(8,128)(2,1)} %param.8) | copy-start | bytes 6291460
  2.7 12.2 %copy-start.41 = (f32[3,3,256]{2,1,0:T(4,128)S(1)}, f32[3,3,256]{2,1,0:T(4,128)}, u32[]{:S(2)}) copy-start(f32[3,3,256]{2,1,0:T(4,128)} %param.7) | copy-start | bytes 27652
  2.7 24.8 %all-to-all-start = ((bf16[8,256,256]{2,1,0:T(8,128)(2,1)}), bf16[8,256,256]{2,1,0:T(8,128)(2,1)}, u32[]{:S(2)}, u32[]{:S(2)}) async-start(bf16[8,256,256]{2,1,0:T(8,128)(2,1)} %broadcast_in_dim.736), calls=%async_computation | async-start | bytes 2097152 | tf_op jit(solution)/shard_map/all_to_all | solution.py:88
  17.0 7.4 %copy-start.5 = (bf16[256,256]{1,0:T(8,128)(2,1)S(1)}, bf16[256,256]{1,0:T(8,128)(2,1)}, u32[]{:S(2)}) copy-start(bf16[256,256]{1,0:T(8,128)(2,1)} %param.9) | copy-start | bytes 393220
  27.5 9.0 %collective-permute-start = (bf16[8,256,256]{2,1,0:T(8,128)(2,1)}, bf16[8,256,256]{2,1,0:T(8,128)(2,1)}, u32[]{:S(2)}, u32[]{:S(2)}) collective-permute-start(bf16[8,256,256]{2,1,0:T(8,128)(2,1)} %all-to-all-done), channel_id=1, source_target_pairs={{0,1},{1,0},{2,3},{3,2},{4,5},{5,4},{6,7},{7,6},{8,9},{9,8},{10,11... | collective-permute-start | bytes 3145736 | tf_op jit(solution)/shard_map/ppermute | solution.py:89
  30.6 10.9 %slice-start = ((s8[6291456]{0:T(1024)(128)(4,1)}), s8[4194304]{0:T(1024)(128)(4,1)S(1)}, s32[]{:S(2)}) async-start(s8[6291456]{0:T(1024)(128)(4,1)} %bitcast.225), calls=%async_computation.3 | async-start | bytes 8388608
  33.2 8.4 %slice-start.1 = ((s8[6291456]{0:T(1024)(128)(4,1)}), s8[2097152]{0:T(1024)(128)(4,1)S(1)}, s32[]{:S(2)}) async-start(s8[6291456]{0:T(1024)(128)(4,1)} %bitcast.225), calls=%async_computation.4 | async-start | bytes 4194304
  38.9 4.9 %collective-permute-start.1 = (bf16[3,2,256]{2,1,0:T(2,128)(2,1)S(1)}, bf16[3,2,256]{2,1,0:T(2,128)(2,1)S(1)}, u32[]{:S(2)}, u32[]{:S(2)}) collective-permute-start(bf16[3,2,256]{2,1,0:T(2,128)(2,1)S(1)} %fusion.39), channel_id=1, source_target_pairs={{0,16},{16,32},{32,48},{48,64},{64,80},{80,96},{96,112},{112,128},... | collective-permute-start | bytes 9224 | tf_op jit(solution)/shard_map/ppermute | solution.py:12
  43.8 2.1 %copy-start.8 = (bf16[3,256,256]{2,1,0:T(8,128)(2,1)}, bf16[3,256,256]{2,1,0:T(8,128)(2,1)S(1)}, u32[]{:S(2)}) copy-start(bf16[3,256,256]{2,1,0:T(8,128)(2,1)S(1)} %fusion.24) | copy-start | bytes 1179652
  44.1 0.9 copy-start.1
  46.7 23.0 %all-to-all-start.1 = ((bf16[512,16,16]{0,2,1:T(8,128)(2,1)}), bf16[512,16,16]{0,2,1:T(8,128)(2,1)S(1)}, u32[]{:S(2)}, u32[]{:S(2)}) async-start(bf16[512,16,16]{0,2,1:T(8,128)(2,1)} %bitcast.230), calls=%async_computation.1 | async-start | bytes 524288 | tf_op jit(solution)/shard_map/all_to_all | solution.py:70
  70.9 1.0 copy-start.3
  72.4 0.8 copy-start.33
  72.4 0.8 copy-start.34
  72.5 0.9 copy-start.27
  72.5 0.9 copy-start.28
  72.6 0.9 copy-start.23
  72.6 0.9 copy-start.24
  72.7 0.9 copy-start.19
  72.7 0.9 copy-start.20
  72.8 1.0 copy-start.17
  72.8 1.0 copy-start.18
  73.2 0.8 copy-start.15
  73.2 0.8 copy-start.16
  73.4 0.8 copy-start.13
  73.4 0.8 copy-start.14
  75.1 0.9 copy-start.6
  75.1 1.0 copy-start.7
  76.9 2.0 %copy-start.10 = (bf16[256,16,16]{0,2,1:T(8,128)(2,1)}, bf16[256,16,16]{0,2,1:T(8,128)(2,1)S(1)}, u32[]{:S(2)}) copy-start(bf16[256,16,16]{0,2,1:T(8,128)(2,1)S(1)} %convolution_convert_fusion.3) | copy-start | bytes 393220
  81.9 17.5 %all-to-all-start.2 = ((bf16[772,16,16]{0,2,1:T(8,128)(2,1)}), bf16[772,16,16]{0,2,1:T(8,128)(2,1)S(1)}, u32[]{:S(2)}, u32[]{:S(2)}) async-start(bf16[772,16,16]{0,2,1:T(8,128)(2,1)} %concatenate.270), calls=%async_computation.2 | async-start | bytes 917504 | tf_op jit(solution)/shard_map/all_to_all | solution.py:70
  86.9 5.5 %collective-permute-start.2 = (bf16[4,2,256]{2,1,0:T(2,128)(2,1)S(1)}, bf16[4,2,256]{2,1,0:T(2,128)(2,1)S(1)}, u32[]{:S(2)}, u32[]{:S(2)}) collective-permute-start(bf16[4,2,256]{2,1,0:T(2,128)(2,1)S(1)} %pad_maximum_fusion.3), channel_id=1, source_target_pairs={{16,0},{32,16},{48,32},{64,48},{80,64},{96,80},{112,96},{128,112},... | collective-permute-start | bytes 12296 | tf_op jit(solution)/shard_map/ppermute | solution.py:12
  99.5 4.8 %copy-start.4 = (f32[1,256,256]{2,1,0:T(8,128)S(1)}, f32[1,256,256]{2,1,0:T(8,128)}, u32[]{:S(2)}) copy-start(f32[1,256,256]{2,1,0:T(8,128)} %get-tuple-element.21) | copy-start | bytes 786436
  (18 other events, 13.8 us)
